TPU v7x, 512 devices: a whole 4x8x8 slice. The times are simulated.
512 devices in a mesh: seq: 128 (over y, z, core), head: 4 (over x).
Axes of the slice: x: 4, y: 8, z: 8, core: 2. Of those that a mesh axis runs over, the one named last changes fastest.
Arguments:
- x_raw: bfloat16 [32768, 4096], P('seq', 'head'), may hold values from -6 to 6
- bc_raw: bfloat16 [32768, 256], P('seq'), may hold values from -6 to 6
- gate_z: bfloat16 [32768, 4096], P('seq', 'head'), may hold values from -6 to 6
- step_size: float32 [32768, 64], P('seq', 'head'), may hold values from 0.002 to 0.05
- log_decay: float32 [32768, 64], P('seq', 'head'), may hold values from -1 to 0, as said below
- doc_ids: int32 [32768], P('seq'), may hold values from 0 to 63, as said below
- conv_x: float32 [4, 4096], P(None, 'head'), may hold values from -3 to 3
- conv_bc: float32 [4, 256], replicated, may hold values from -3 to 3
- skip: float32 [64], P('head'), may hold values from 0.5 to 2
- norm_gain: float32 [4096], P('head'), may hold values from 0.25 to 1.75
Outputs:
- mixed: bfloat16 [32768, 4096], P('seq', 'head')
Inputs may be any that keep to these rules, and one draw needn't show every extreme that they name: `doc_ids`: document ids never fall along the sequence; each document has 1 to 4096 tokens, one exactly 4096. `log_decay`: every entry is negative.
All inputs are finite; a program needn't handle non-finite values.
Results may differ from a plain program's by a relative error of at most 0.005.
Values may be sent and summed in bfloat16 or wider, within the bound.
No kernel may reach another device: no remote copies, remote signals or barrier semaphores. Data moves between devices by JAX's collectives and lax.ppermute only.
A program may use at most 192 MiB of HBM per device.

v0:
```python
import jax
import jax.numpy as jnp
from jax import lax
from jax.sharding import PartitionSpec as P

GROUP = 256


EPS = 1e-05


def shifted(block, axis, distance):
    devices = range(lax.axis_size(axis))
    route = [(i - distance, i) for i in devices if i - distance in devices]
    return lax.ppermute(block, axis, route)


def body(x_raw, bc_raw, gate_z, step_size, log_decay, doc_ids, conv_x, conv_bc, skip, norm_gain):
    rows_dev, head_cols = x_raw.shape
    heads_dev = step_size.shape[1]
    head_size = head_cols // heads_dev
    states = bc_raw.shape[1] // 2
    taps = conv_x.shape[0]
    raw_all = jnp.concatenate([x_raw, bc_raw], axis=1)
    labels = doc_ids + 1
    edge_rows = shifted(raw_all[rows_dev - (taps - 1) :], "seq", 1)
    edge_docs = shifted(labels[rows_dev - (taps - 1) :], "seq", 1)
    extended = jnp.concatenate([edge_rows, raw_all], axis=0)
    ext_docs = jnp.concatenate([edge_docs, labels], axis=0)
    kernel = jnp.concatenate([conv_x, conv_bc], axis=1)
    total = jnp.zeros(raw_all.shape, jnp.float32)
    for k in range(taps):
        moved = extended[taps - 1 - k : taps - 1 - k + rows_dev].astype(jnp.float32)
        keep = (ext_docs[taps - 1 - k : taps - 1 - k + rows_dev] == labels).astype(jnp.float32)
        total = total + kernel[k][None, :] * moved * keep[:, None]
    activated = jax.nn.silu(total).astype(jnp.bfloat16)
    xconv = activated[:, :head_cols].reshape(rows_dev, heads_dev, head_size)
    bconv = activated[:, head_cols : head_cols + states]
    cconv = activated[:, head_cols + states :]
    xdt = (xconv.astype(jnp.float32) * step_size[:, :, None]).astype(jnp.bfloat16)
    lower = jnp.arange(GROUP)[:, None] >= jnp.arange(GROUP)[None, :]
    previous = edge_docs[taps - 2] - 1
    local_in = []
    running = jnp.zeros((heads_dev, head_size, states), jnp.float32)
    through_all = jnp.ones((heads_dev,), jnp.float32)
    cum = jnp.cumsum(log_decay, axis=0)
    gram = jnp.dot(cconv, bconv.T, preferred_element_type=jnp.float32)
    mask = ((doc_ids[:, None] == doc_ids[None, :]) & lower)[None]
    diff = cum.T[:, :, None] - cum.T[:, None, :]
    weights = (jnp.where(mask, jnp.exp(jnp.where(mask, diff, 0.0)), 0.0) * gram[None]).astype(
        jnp.bfloat16
    )
    inners = jnp.einsum("hts,shp->thp", weights, xdt, preferred_element_type=jnp.float32)
    cont = (doc_ids == previous).astype(jnp.float32)
    entries = jnp.exp(cum) * cont[:, None]
    ends = jnp.where((doc_ids == doc_ids[-1])[:, None], jnp.exp(cum[-1][None, :] - cum), 0.0)
    written = (xdt.astype(jnp.float32) * ends[:, :, None]).astype(jnp.bfloat16)
    local = jnp.einsum("shp,sn->hpn", written, bconv, preferred_element_type=jnp.float32)
    local_in.append(running)
    before = through_all
    through = jnp.exp(cum[-1]) * cont[-1]
    running = through[:, None, None] * running + local
    through_all = through_all * through
    length = lax.axis_size("seq")
    hops = min(length - 1, min(16 * rows_dev, rows_dev * length // 2) // rows_dev)

    def relay_step(step, incoming):
        leaving = through_all[:, None, None] * incoming + running
        return shifted(leaving, "seq", 1)

    incoming = lax.fori_loop(0, hops, relay_step, jnp.zeros_like(running))
    entered = (before[:, None, None] * incoming).astype(jnp.bfloat16)
    carried = (
        jnp.einsum("tn,hpn->thp", cconv, entered, preferred_element_type=jnp.float32)
        * entries[:, :, None]
    )
    scanned = inners + carried + skip[None, :, None] * xconv.astype(jnp.float32)
    gated_rows = scanned.reshape(GROUP, head_cols) * jax.nn.silu(gate_z.astype(jnp.float32))
    squares = lax.psum(jnp.sum(gated_rows * gated_rows, axis=1), "head")
    scale = lax.rsqrt(squares / (head_cols * lax.axis_size("head")) + EPS)
    return (gated_rows * scale[:, None] * norm_gain[None, :]).astype(jnp.bfloat16)


def solution(mesh):
    return jax.shard_map(
        body,
        mesh=mesh,
        in_specs=(
            P("seq", "head"),
            P("seq", None),
            P("seq", "head"),
            P("seq", "head"),
            P("seq", "head"),
            P("seq"),
            P(None, "head"),
            P(),
            P("head"),
            P("head"),
        ),
        out_specs=P("seq", "head"),
        check_vma=False,
    )
```

profile of v0, /device:TPU:32, one launch (start us, length us, event | category | flops | bytes accessed | tf_op | source)
XLA Modules:
  0.0 258.5 jit_solution(3667123741944502180)
XLA Ops:
  0.0 0.7 broadcast_add_fusion
  0.8 1.9 collective-permute-start.2
  2.8 1.1 constant_dynamic-update-slice_fusion.3
  3.9 4.4 %collective-permute-start.1 = (bf16[3,1280]{1,0:T(4,128)(2,1)S(1)}, bf16[3,1280]{1,0:T(4,128)(2,1)S(1)}, u32[]{:S(2)}, u32[]{:S(2)}) collective-permute-start(bf16[3,1280]{1,0:T(4,128)(2,1)S(1)} %slice.87), channel_id=1, source_target_pairs={{0,4},{4,8},{8,12},{12,16},{16,20},{20,24},{24,28},{28,32},{32,36}... | collective-permute-start | bytes 23048 | tf_op jit(solution)/shard_map/ppermute | solution.py:15
  8.3 0.6 slice.84
  9.1 0.6 reduce-window.6
  9.7 0.2 slice_reduce_fusion
  10.0 0.2 slice_reduce_fusion.1
  10.2 2.2 collective-permute-done.2
  12.4 0.7 slice.82
  13.8 0.7 compare_convert_fusion.3
  14.5 0.6 slice.83
  15.2 0.7 broadcast_multiply_fusion
  15.8 1.2 multiply_convert_fusion.4
  17.2 0.2 fusion.21
  17.4 0.3 copy.22
  17.7 0.4 copy-done.3
  18.1 0.3 convolution_add_fusion
  18.4 2.3 fusion.6
  20.8 223.1 %while.10 = (s32[]{:T(128)}, f32[16,64,128]{2,1,0:T(8,128)S(1)}, f32[16]{0:T(128)S(1)}, f32[16,64,128]{2,1,0:T(8,128)S(1)}, s32[]{:T(128)}) while((s32[]{:T(128)}, f32[16,64,128]{2,1,0:T(8,128)S(1)}, f32[16]{0:T(128)S(1)}, f32[16,64,128]{2,1,0:T(8,128)S(1)}, s32[]{:T(128)}) %tuple.28), condition=%wide.region_3.4_spmd, body=%wide.region_2.3_spmd.sunk | while | flops 262146 | bytes 3670181 | solution.py:71
  20.8 0.1 multiply_add_fusion.2
  20.9 1.9 collective-permute-start
  22.9 11.9 %collective-permute-done = f32[16,64,128]{2,1,0:T(8,128)S(1)} collective-permute-done((f32[16,64,128]{2,1,0:T(8,128)S(1)}, f32[16,64,128]{2,1,0:T(8,128)S(1)}, u32[]{:S(2)}, u32[]{:S(2)}) %collective-permute-start) | collective-permute-done | bytes 524320 | tf_op jit(solution)/shard_map/while/body/eval_jaxpr/ppermute | solution.py:15
  34.8 0.1 multiply_add_fusion.2
  34.9 1.9 collective-permute-start
  36.8 11.9 %collective-permute-done = f32[16,64,128]{2,1,0:T(8,128)S(1)} collective-permute-done((f32[16,64,128]{2,1,0:T(8,128)S(1)}, f32[16,64,128]{2,1,0:T(8,128)S(1)}, u32[]{:S(2)}, u32[]{:S(2)}) %collective-permute-start) | collective-permute-done | bytes 524320 | tf_op jit(solution)/shard_map/while/body/eval_jaxpr/ppermute | solution.py:15
  48.7 0.1 multiply_add_fusion.2
  48.8 1.9 collective-permute-start
  50.7 11.9 %collective-permute-done = f32[16,64,128]{2,1,0:T(8,128)S(1)} collective-permute-done((f32[16,64,128]{2,1,0:T(8,128)S(1)}, f32[16,64,128]{2,1,0:T(8,128)S(1)}, u32[]{:S(2)}, u32[]{:S(2)}) %collective-permute-start) | collective-permute-done | bytes 524320 | tf_op jit(solution)/shard_map/while/body/eval_jaxpr/ppermute | solution.py:15
  62.8 1.9 collective-permute-start
  64.7 11.9 %collective-permute-done = f32[16,64,128]{2,1,0:T(8,128)S(1)} collective-permute-done((f32[16,64,128]{2,1,0:T(8,128)S(1)}, f32[16,64,128]{2,1,0:T(8,128)S(1)}, u32[]{:S(2)}, u32[]{:S(2)}) %collective-permute-start) | collective-permute-done | bytes 524320 | tf_op jit(solution)/shard_map/while/body/eval_jaxpr/ppermute | solution.py:15
  76.7 1.9 collective-permute-start
  78.6 11.9 %collective-permute-done = f32[16,64,128]{2,1,0:T(8,128)S(1)} collective-permute-done((f32[16,64,128]{2,1,0:T(8,128)S(1)}, f32[16,64,128]{2,1,0:T(8,128)S(1)}, u32[]{:S(2)}, u32[]{:S(2)}) %collective-permute-start) | collective-permute-done | bytes 524320 | tf_op jit(solution)/shard_map/while/body/eval_jaxpr/ppermute | solution.py:15
  90.5 0.1 multiply_add_fusion.2
  90.6 1.9 collective-permute-start
  92.6 11.9 %collective-permute-done = f32[16,64,128]{2,1,0:T(8,128)S(1)} collective-permute-done((f32[16,64,128]{2,1,0:T(8,128)S(1)}, f32[16,64,128]{2,1,0:T(8,128)S(1)}, u32[]{:S(2)}, u32[]{:S(2)}) %collective-permute-start) | collective-permute-done | bytes 524320 | tf_op jit(solution)/shard_map/while/body/eval_jaxpr/ppermute | solution.py:15
  104.6 1.9 collective-permute-start
  106.5 11.9 %collective-permute-done = f32[16,64,128]{2,1,0:T(8,128)S(1)} collective-permute-done((f32[16,64,128]{2,1,0:T(8,128)S(1)}, f32[16,64,128]{2,1,0:T(8,128)S(1)}, u32[]{:S(2)}, u32[]{:S(2)}) %collective-permute-start) | collective-permute-done | bytes 524320 | tf_op jit(solution)/shard_map/while/body/eval_jaxpr/ppermute | solution.py:15
  118.5 1.9 collective-permute-start
  120.5 11.9 %collective-permute-done = f32[16,64,128]{2,1,0:T(8,128)S(1)} collective-permute-done((f32[16,64,128]{2,1,0:T(8,128)S(1)}, f32[16,64,128]{2,1,0:T(8,128)S(1)}, u32[]{:S(2)}, u32[]{:S(2)}) %collective-permute-start) | collective-permute-done | bytes 524320 | tf_op jit(solution)/shard_map/while/body/eval_jaxpr/ppermute | solution.py:15
  132.3 0.1 multiply_add_fusion.2
  132.5 1.9 collective-permute-start
  134.4 11.9 %collective-permute-done = f32[16,64,128]{2,1,0:T(8,128)S(1)} collective-permute-done((f32[16,64,128]{2,1,0:T(8,128)S(1)}, f32[16,64,128]{2,1,0:T(8,128)S(1)}, u32[]{:S(2)}, u32[]{:S(2)}) %collective-permute-start) | collective-permute-done | bytes 524320 | tf_op jit(solution)/shard_map/while/body/eval_jaxpr/ppermute | solution.py:15
  146.4 1.9 collective-permute-start
  148.3 11.9 %collective-permute-done = f32[16,64,128]{2,1,0:T(8,128)S(1)} collective-permute-done((f32[16,64,128]{2,1,0:T(8,128)S(1)}, f32[16,64,128]{2,1,0:T(8,128)S(1)}, u32[]{:S(2)}, u32[]{:S(2)}) %collective-permute-start) | collective-permute-done | bytes 524320 | tf_op jit(solution)/shard_map/while/body/eval_jaxpr/ppermute | solution.py:15
  160.3 1.9 collective-permute-start
  162.3 11.9 %collective-permute-done = f32[16,64,128]{2,1,0:T(8,128)S(1)} collective-permute-done((f32[16,64,128]{2,1,0:T(8,128)S(1)}, f32[16,64,128]{2,1,0:T(8,128)S(1)}, u32[]{:S(2)}, u32[]{:S(2)}) %collective-permute-start) | collective-permute-done | bytes 524320 | tf_op jit(solution)/shard_map/while/body/eval_jaxpr/ppermute | solution.py:15
  174.2 0.1 multiply_add_fusion.2
  174.3 1.9 collective-permute-start
  176.2 11.9 %collective-permute-done = f32[16,64,128]{2,1,0:T(8,128)S(1)} collective-permute-done((f32[16,64,128]{2,1,0:T(8,128)S(1)}, f32[16,64,128]{2,1,0:T(8,128)S(1)}, u32[]{:S(2)}, u32[]{:S(2)}) %collective-permute-start) | collective-permute-done | bytes 524320 | tf_op jit(solution)/shard_map/while/body/eval_jaxpr/ppermute | solution.py:15
  188.2 1.9 collective-permute-start
  190.2 11.9 %collective-permute-done = f32[16,64,128]{2,1,0:T(8,128)S(1)} collective-permute-done((f32[16,64,128]{2,1,0:T(8,128)S(1)}, f32[16,64,128]{2,1,0:T(8,128)S(1)}, u32[]{:S(2)}, u32[]{:S(2)}) %collective-permute-start) | collective-permute-done | bytes 524320 | tf_op jit(solution)/shard_map/while/body/eval_jaxpr/ppermute | solution.py:15
  202.2 1.9 collective-permute-start
  204.1 11.9 %collective-permute-done = f32[16,64,128]{2,1,0:T(8,128)S(1)} collective-permute-done((f32[16,64,128]{2,1,0:T(8,128)S(1)}, f32[16,64,128]{2,1,0:T(8,128)S(1)}, u32[]{:S(2)}, u32[]{:S(2)}) %collective-permute-start) | collective-permute-done | bytes 524320 | tf_op jit(solution)/shard_map/while/body/eval_jaxpr/ppermute | solution.py:15
  216.1 1.9 collective-permute-start
  218.0 11.9 %collective-permute-done = f32[16,64,128]{2,1,0:T(8,128)S(1)} collective-permute-done((f32[16,64,128]{2,1,0:T(8,128)S(1)}, f32[16,64,128]{2,1,0:T(8,128)S(1)}, u32[]{:S(2)}, u32[]{:S(2)}) %collective-permute-start) | collective-permute-done | bytes 524320 | tf_op jit(solution)/shard_map/while/body/eval_jaxpr/ppermute | solution.py:15
  230.0 1.9 collective-permute-start
  232.0 11.9 %collective-permute-done = f32[16,64,128]{2,1,0:T(8,128)S(1)} collective-permute-done((f32[16,64,128]{2,1,0:T(8,128)S(1)}, f32[16,64,128]{2,1,0:T(8,128)S(1)}, u32[]{:S(2)}, u32[]{:S(2)}) %collective-permute-start) | collective-permute-done | bytes 524320 | tf_op jit(solution)/shard_map/while/body/eval_jaxpr/ppermute | solution.py:15
  243.9 1.5 fusion.8
  245.4 0.3 copy.25
  245.8 0.7 copy-done.1
  246.5 0.4 multiply_reduce_fusion
  246.9 10.5 %psum.7 = f32[256]{0:T(256)S(1)} all-reduce(f32[256]{0:T(256)S(1)} %multiply_reduce_fusion), channel_id=1, replica_groups=mesh['seq'=128,'head'=4] {'head'}, use_global_device_ids=true, to_apply=%region_5.6 | all-reduce | flops 256 | bytes 2048 | tf_op jit(solution)/shard_map/psum | solution.py:79
  257.4 1.2 multiply_convert_fusion.5
  (43 shorter events, 1.9 us)
Async XLA Ops:
  0.0 9.1 %copy-start = (f32[256,16]{0,1:T(8,128)S(1)}, f32[256,16]{0,1:T(8,128)}, u32[]{:S(2)}) copy-start(f32[256,16]{0,1:T(8,128)} %param.16) | copy-start | bytes 49156
  0.0 8.3 %copy-start.4 = (s32[256]{0:T(256)S(1)}, s32[256]{0:T(256)}, u32[]{:S(2)}) copy-start(s32[256]{0:T(256)} %param.17) | copy-start | bytes 3076
  0.0 3.8 %copy-start.2 = (bf16[256,256]{1,0:T(8,128)(2,1)S(1)}, bf16[256,256]{1,0:T(8,128)(2,1)}, u32[]{:S(2)}) copy-start(bf16[256,256]{1,0:T(8,128)(2,1)} %param.13) | copy-start | bytes 393220
  0.0 9.0 %copy-start.5 = (f32[4,1024]{1,0:T(4,128)S(1)}, f32[4,1024]{1,0:T(4,128)}, u32[]{:S(2)}) copy-start(f32[4,1024]{1,0:T(4,128)} %param.18) | copy-start | bytes 49156
  0.0 9.0 %copy-start.7 = (f32[4,256]{1,0:T(4,128)S(1)}, f32[4,256]{1,0:T(4,128)}, u32[]{:S(2)}) copy-start(f32[4,256]{1,0:T(4,128)} %param.19) | copy-start | bytes 12292
  0.8 11.5 %collective-permute-start.2 = (s32[3]{0:T(128)S(1)}, s32[3]{0:T(128)S(1)}, u32[]{:S(2)}, u32[]{:S(2)}) collective-permute-start(s32[3]{0:T(128)S(1)} %slice.68), channel_id=1, source_target_pairs={{0,4},{4,8},{8,12},{12,16},{16,20},{20,24},{24,28},{28,32},{32,36}... | collective-permute-start | bytes 44 | tf_op jit(solution)/shard_map/ppermute | solution.py:15
  3.9 11.9 %collective-permute-start.1 = (bf16[3,1280]{1,0:T(4,128)(2,1)S(1)}, bf16[3,1280]{1,0:T(4,128)(2,1)S(1)}, u32[]{:S(2)}, u32[]{:S(2)}) collective-permute-start(bf16[3,1280]{1,0:T(4,128)(2,1)S(1)} %slice.87), channel_id=1, source_target_pairs={{0,4},{4,8},{8,12},{12,16},{16,20},{20,24},{24,28},{28,32},{32,36}... | collective-permute-start | bytes 23048 | tf_op jit(solution)/shard_map/ppermute | solution.py:15
  17.4 0.7 copy-start.3
  20.8 223.1 %copy-start.8 = (f32[16]{0:T(128)S(1)}, f32[16]{0:T(128)}, u32[]{:S(2)}) copy-start(f32[16]{0:T(128)} %param.20) | copy-start | bytes 196
  20.9 13.8 %collective-permute-start = (f32[16,64,128]{2,1,0:T(8,128)S(1)}, f32[16,64,128]{2,1,0:T(8,128)S(1)}, u32[]{:S(2)}, u32[]{:S(2)}) collective-permute-start(f32[16,64,128]{2,1,0:T(8,128)S(1)} %multiply_add_fusion.2), channel_id=1, source_target_pairs={{0,4},{4,8},{8,12},{12,16},{16,20},{20,24},{24,28},{28,32},{32,36}... | collective-permute-start | bytes 1572872 | tf_op jit(solution)/shard_map/while/body/eval_jaxpr/ppermute | solution.py:15
  34.9 13.8 %collective-permute-start = (f32[16,64,128]{2,1,0:T(8,128)S(1)}, f32[16,64,128]{2,1,0:T(8,128)S(1)}, u32[]{:S(2)}, u32[]{:S(2)}) collective-permute-start(f32[16,64,128]{2,1,0:T(8,128)S(1)} %multiply_add_fusion.2), channel_id=1, source_target_pairs={{0,4},{4,8},{8,12},{12,16},{16,20},{20,24},{24,28},{28,32},{32,36}... | collective-permute-start | bytes 1572872 | tf_op jit(solution)/shard_map/while/body/eval_jaxpr/ppermute | solution.py:15
  48.8 13.8 %collective-permute-start = (f32[16,64,128]{2,1,0:T(8,128)S(1)}, f32[16,64,128]{2,1,0:T(8,128)S(1)}, u32[]{:S(2)}, u32[]{:S(2)}) collective-permute-start(f32[16,64,128]{2,1,0:T(8,128)S(1)} %multiply_add_fusion.2), channel_id=1, source_target_pairs={{0,4},{4,8},{8,12},{12,16},{16,20},{20,24},{24,28},{28,32},{32,36}... | collective-permute-start | bytes 1572872 | tf_op jit(solution)/shard_map/while/body/eval_jaxpr/ppermute | solution.py:15
  62.8 13.8 %collective-permute-start = (f32[16,64,128]{2,1,0:T(8,128)S(1)}, f32[16,64,128]{2,1,0:T(8,128)S(1)}, u32[]{:S(2)}, u32[]{:S(2)}) collective-permute-start(f32[16,64,128]{2,1,0:T(8,128)S(1)} %multiply_add_fusion.2), channel_id=1, source_target_pairs={{0,4},{4,8},{8,12},{12,16},{16,20},{20,24},{24,28},{28,32},{32,36}... | collective-permute-start | bytes 1572872 | tf_op jit(solution)/shard_map/while/body/eval_jaxpr/ppermute | solution.py:15
  76.7 13.8 %collective-permute-start = (f32[16,64,128]{2,1,0:T(8,128)S(1)}, f32[16,64,128]{2,1,0:T(8,128)S(1)}, u32[]{:S(2)}, u32[]{:S(2)}) collective-permute-start(f32[16,64,128]{2,1,0:T(8,128)S(1)} %multiply_add_fusion.2), channel_id=1, source_target_pairs={{0,4},{4,8},{8,12},{12,16},{16,20},{20,24},{24,28},{28,32},{32,36}... | collective-permute-start | bytes 1572872 | tf_op jit(solution)/shard_map/while/body/eval_jaxpr/ppermute | solution.py:15
  90.6 13.8 %collective-permute-start = (f32[16,64,128]{2,1,0:T(8,128)S(1)}, f32[16,64,128]{2,1,0:T(8,128)S(1)}, u32[]{:S(2)}, u32[]{:S(2)}) collective-permute-start(f32[16,64,128]{2,1,0:T(8,128)S(1)} %multiply_add_fusion.2), channel_id=1, source_target_pairs={{0,4},{4,8},{8,12},{12,16},{16,20},{20,24},{24,28},{28,32},{32,36}... | collective-permute-start | bytes 1572872 | tf_op jit(solution)/shard_map/while/body/eval_jaxpr/ppermute | solution.py:15
  104.6 13.8 %collective-permute-start = (f32[16,64,128]{2,1,0:T(8,128)S(1)}, f32[16,64,128]{2,1,0:T(8,128)S(1)}, u32[]{:S(2)}, u32[]{:S(2)}) collective-permute-start(f32[16,64,128]{2,1,0:T(8,128)S(1)} %multiply_add_fusion.2), channel_id=1, source_target_pairs={{0,4},{4,8},{8,12},{12,16},{16,20},{20,24},{24,28},{28,32},{32,36}... | collective-permute-start | bytes 1572872 | tf_op jit(solution)/shard_map/while/body/eval_jaxpr/ppermute | solution.py:15
  118.5 13.8 %collective-permute-start = (f32[16,64,128]{2,1,0:T(8,128)S(1)}, f32[16,64,128]{2,1,0:T(8,128)S(1)}, u32[]{:S(2)}, u32[]{:S(2)}) collective-permute-start(f32[16,64,128]{2,1,0:T(8,128)S(1)} %multiply_add_fusion.2), channel_id=1, source_target_pairs={{0,4},{4,8},{8,12},{12,16},{16,20},{20,24},{24,28},{28,32},{32,36}... | collective-permute-start | bytes 1572872 | tf_op jit(solution)/shard_map/while/body/eval_jaxpr/ppermute | solution.py:15
  132.5 13.8 %collective-permute-start = (f32[16,64,128]{2,1,0:T(8,128)S(1)}, f32[16,64,128]{2,1,0:T(8,128)S(1)}, u32[]{:S(2)}, u32[]{:S(2)}) collective-permute-start(f32[16,64,128]{2,1,0:T(8,128)S(1)} %multiply_add_fusion.2), channel_id=1, source_target_pairs={{0,4},{4,8},{8,12},{12,16},{16,20},{20,24},{24,28},{28,32},{32,36}... | collective-permute-start | bytes 1572872 | tf_op jit(solution)/shard_map/while/body/eval_jaxpr/ppermute | solution.py:15
  146.4 13.8 %collective-permute-start = (f32[16,64,128]{2,1,0:T(8,128)S(1)}, f32[16,64,128]{2,1,0:T(8,128)S(1)}, u32[]{:S(2)}, u32[]{:S(2)}) collective-permute-start(f32[16,64,128]{2,1,0:T(8,128)S(1)} %multiply_add_fusion.2), channel_id=1, source_target_pairs={{0,4},{4,8},{8,12},{12,16},{16,20},{20,24},{24,28},{28,32},{32,36}... | collective-permute-start | bytes 1572872 | tf_op jit(solution)/shard_map/while/body/eval_jaxpr/ppermute | solution.py:15
  160.3 13.8 %collective-permute-start = (f32[16,64,128]{2,1,0:T(8,128)S(1)}, f32[16,64,128]{2,1,0:T(8,128)S(1)}, u32[]{:S(2)}, u32[]{:S(2)}) collective-permute-start(f32[16,64,128]{2,1,0:T(8,128)S(1)} %multiply_add_fusion.2), channel_id=1, source_target_pairs={{0,4},{4,8},{8,12},{12,16},{16,20},{20,24},{24,28},{28,32},{32,36}... | collective-permute-start | bytes 1572872 | tf_op jit(solution)/shard_map/while/body/eval_jaxpr/ppermute | solution.py:15
  174.3 13.8 %collective-permute-start = (f32[16,64,128]{2,1,0:T(8,128)S(1)}, f32[16,64,128]{2,1,0:T(8,128)S(1)}, u32[]{:S(2)}, u32[]{:S(2)}) collective-permute-start(f32[16,64,128]{2,1,0:T(8,128)S(1)} %multiply_add_fusion.2), channel_id=1, source_target_pairs={{0,4},{4,8},{8,12},{12,16},{16,20},{20,24},{24,28},{28,32},{32,36}... | collective-permute-start | bytes 1572872 | tf_op jit(solution)/shard_map/while/body/eval_jaxpr/ppermute | solution.py:15
  188.2 13.8 %collective-permute-start = (f32[16,64,128]{2,1,0:T(8,128)S(1)}, f32[16,64,128]{2,1,0:T(8,128)S(1)}, u32[]{:S(2)}, u32[]{:S(2)}) collective-permute-start(f32[16,64,128]{2,1,0:T(8,128)S(1)} %multiply_add_fusion.2), channel_id=1, source_target_pairs={{0,4},{4,8},{8,12},{12,16},{16,20},{20,24},{24,28},{28,32},{32,36}... | collective-permute-start | bytes 1572872 | tf_op jit(solution)/shard_map/while/body/eval_jaxpr/ppermute | solution.py:15
  202.2 13.8 %collective-permute-start = (f32[16,64,128]{2,1,0:T(8,128)S(1)}, f32[16,64,128]{2,1,0:T(8,128)S(1)}, u32[]{:S(2)}, u32[]{:S(2)}) collective-permute-start(f32[16,64,128]{2,1,0:T(8,128)S(1)} %multiply_add_fusion.2), channel_id=1, source_target_pairs={{0,4},{4,8},{8,12},{12,16},{16,20},{20,24},{24,28},{28,32},{32,36}... | collective-permute-start | bytes 1572872 | tf_op jit(solution)/shard_map/while/body/eval_jaxpr/ppermute | solution.py:15
  216.1 13.8 %collective-permute-start = (f32[16,64,128]{2,1,0:T(8,128)S(1)}, f32[16,64,128]{2,1,0:T(8,128)S(1)}, u32[]{:S(2)}, u32[]{:S(2)}) collective-permute-start(f32[16,64,128]{2,1,0:T(8,128)S(1)} %multiply_add_fusion.2), channel_id=1, source_target_pairs={{0,4},{4,8},{8,12},{12,16},{16,20},{20,24},{24,28},{28,32},{32,36}... | collective-permute-start | bytes 1572872 | tf_op jit(solution)/shard_map/while/body/eval_jaxpr/ppermute | solution.py:15
  230.0 13.8 %collective-permute-start = (f32[16,64,128]{2,1,0:T(8,128)S(1)}, f32[16,64,128]{2,1,0:T(8,128)S(1)}, u32[]{:S(2)}, u32[]{:S(2)}) collective-permute-start(f32[16,64,128]{2,1,0:T(8,128)S(1)} %multiply_add_fusion.2), channel_id=1, source_target_pairs={{0,4},{4,8},{8,12},{12,16},{16,20},{20,24},{24,28},{28,32},{32,36}... | collective-permute-start | bytes 1572872 | tf_op jit(solution)/shard_map/while/body/eval_jaxpr/ppermute | solution.py:15
  245.4 1.0 copy-start.1
  246.4 10.9 %copy-start.6 = (f32[1024]{0:T(1024)S(1)}, f32[1024]{0:T(1024)}, u32[]{:S(2)}) copy-start(f32[1024]{0:T(1024)} %param.21) | copy-start | bytes 12292
where the time goes:
time: 259 us
  waiting for transfers between devices  192 us (74%)
  starting transfers between devices  37 us (14%)
  blocking collectives  10.5 us (4%)
  other arithmetic  7.79 us (3%)
  local copies, waits for them, and re-layouts  5.22 us (2%)
  matrix products  4.33 us (2%)
    ppermute x18, waiting for transfers between devices, shifted(): return lax.ppermute(block, axis, route)  192 us
    ppermute x18, starting transfers between devices, shifted(): return lax.ppermute(block, axis, route)  37 us
    psum x1, blocking collectives, body(): squares = lax.psum(jnp.sum(gated_rows * gated_rows, axis=1), 'head')  10.5 us
  transfers between devices with their start and end apart: 18, of which 17 were waited for; matrix products, arithmetic and copies ran while one was open for 2% of the time, Pallas kernels for 0%

commit v1 on v0

--- a/solution.py
+++ b/solution.py
@@ -1,12 +1,15 @@
 import jax
 import jax.numpy as jnp
 from jax import lax
+from jax.sharding import Mesh
 from jax.sharding import PartitionSpec as P
 
 GROUP = 256
+SEGMENT = 16
 
 
 EPS = 1e-05
+SEQ = ("row", "seg")
 
 
 def shifted(block, axis, distance):
@@ -21,10 +24,16 @@
     head_size = head_cols // heads_dev
     states = bc_raw.shape[1] // 2
     taps = conv_x.shape[0]
+    seg = lax.axis_size("seg")
+    per_owner = heads_dev // seg
     raw_all = jnp.concatenate([x_raw, bc_raw], axis=1)
     labels = doc_ids + 1
-    edge_rows = shifted(raw_all[rows_dev - (taps - 1) :], "seq", 1)
-    edge_docs = shifted(labels[rows_dev - (taps - 1) :], "seq", 1)
+    edge = jnp.concatenate(
+        [raw_all[rows_dev - (taps - 1) :], labels[rows_dev - (taps - 1) :, None].astype(jnp.bfloat16)], axis=1
+    )
+    edge = shifted(edge, SEQ, 1)
+    edge_rows = edge[:, : raw_all.shape[1]]
+    edge_docs = edge[:, raw_all.shape[1]].astype(jnp.int32)
     extended = jnp.concatenate([edge_rows, raw_all], axis=0)
     ext_docs = jnp.concatenate([edge_docs, labels], axis=0)
     kernel = jnp.concatenate([conv_x, conv_bc], axis=1)
@@ -40,9 +49,6 @@
     xdt = (xconv.astype(jnp.float32) * step_size[:, :, None]).astype(jnp.bfloat16)
     lower = jnp.arange(GROUP)[:, None] >= jnp.arange(GROUP)[None, :]
     previous = edge_docs[taps - 2] - 1
-    local_in = []
-    running = jnp.zeros((heads_dev, head_size, states), jnp.float32)
-    through_all = jnp.ones((heads_dev,), jnp.float32)
     cum = jnp.cumsum(log_decay, axis=0)
     gram = jnp.dot(cconv, bconv.T, preferred_element_type=jnp.float32)
     mask = ((doc_ids[:, None] == doc_ids[None, :]) & lower)[None]
@@ -56,20 +62,30 @@
     ends = jnp.where((doc_ids == doc_ids[-1])[:, None], jnp.exp(cum[-1][None, :] - cum), 0.0)
     written = (xdt.astype(jnp.float32) * ends[:, :, None]).astype(jnp.bfloat16)
     local = jnp.einsum("shp,sn->hpn", written, bconv, preferred_element_type=jnp.float32)
-    local_in.append(running)
-    before = through_all
     through = jnp.exp(cum[-1]) * cont[-1]
-    running = through[:, None, None] * running + local
-    through_all = through_all * through
-    length = lax.axis_size("seq")
-    hops = min(length - 1, min(16 * rows_dev, rows_dev * length // 2) // rows_dev)
 
-    def relay_step(step, incoming):
-        leaving = through_all[:, None, None] * incoming + running
-        return shifted(leaving, "seq", 1)
+    flat = head_size * states
+    payload = jnp.concatenate(
+        [local.reshape(heads_dev, flat), jnp.broadcast_to(through[:, None], (heads_dev, 128))], axis=1
+    )
+    got = lax.all_to_all(payload, "seg", 0, 0, tiled=True).reshape(seg, per_owner, flat + 128)
+    pieces = got[:, :, :flat].reshape(seg, per_owner, head_size, states)
+    decays = got[:, :, flat]
+    folds = []
+    decay_before = []
+    running = jnp.zeros((per_owner, head_size, states), jnp.float32)
+    product = jnp.ones((per_owner,), jnp.float32)
+    for i in range(seg):
+        folds.append(running)
+        decay_before.append(product)
+        running = decays[i][:, None, None] * running + pieces[i]
+        product = product * decays[i]
+    carry = shifted(running, "row", 1)
+    entering = jnp.stack(decay_before)[:, :, None, None] * carry[None] + jnp.stack(folds)
+    entered = lax.all_to_all(entering.astype(jnp.bfloat16), "seg", 0, 0, tiled=True).reshape(
+        heads_dev, head_size, states
+    )
 
-    incoming = lax.fori_loop(0, hops, relay_step, jnp.zeros_like(running))
-    entered = (before[:, None, None] * incoming).astype(jnp.bfloat16)
     carried = (
         jnp.einsum("tn,hpn->thp", cconv, entered, preferred_element_type=jnp.float32)
         * entries[:, :, None]
@@ -82,21 +98,25 @@
 
 
 def solution(mesh):
+    seq_size = mesh.shape["seq"]
+    grid = Mesh(
+        mesh.devices.reshape(seq_size // SEGMENT, SEGMENT, mesh.shape["head"]), ("row", "seg", "head")
+    )
     return jax.shard_map(
         body,
-        mesh=mesh,
+        mesh=grid,
         in_specs=(
-            P("seq", "head"),
-            P("seq", None),
-            P("seq", "head"),
-            P("seq", "head"),
-            P("seq", "head"),
-            P("seq"),
+            P(SEQ, "head"),
+            P(SEQ, None),
+            P(SEQ, "head"),
+            P(SEQ, "head"),
+            P(SEQ, "head"),
+            P(SEQ),
             P(None, "head"),
             P(),
             P("head"),
             P("head"),
         ),
-        out_specs=P("seq", "head"),
+        out_specs=P(SEQ, "head"),
         check_vma=False,
     )

time: 259 us -> 101 us (0.39)
  the two profiles are of different devices: /device:TPU:32 before, /device:TPU:24 now
where the time goes in v1:
time: 101 us; the launch traced here: 99.9 us
  waiting for transfers between devices  32.6 us (32%)
  other arithmetic  17.8 us (18%)
  starting transfers between devices  15.8 us (16%)
  between operations  11 us (11%)
  blocking collectives  10.5 us (10%)
  local copies, waits for them, and re-layouts  7.87 us (8%)
  matrix products  4.35 us (4%)
    all_to_all x1, waiting for transfers between devices, body(): lax.all_to_all(payload, 'seg', 0, 0, tiled=True)  16 us
    psum x1, blocking collectives, body(): squares = lax.psum(jnp.sum(gated_rows * gated_rows, axis=1), 'head')  10.5 us
    all_to_all x1, waiting for transfers between devices, body(): lax.all_to_all(entering.astype(jnp.bfloat16), 'seg', 0, 0, tiled=True)  8.67 us
    ppermute x2, waiting for transfers between devices, shifted(): return lax.ppermute(block, axis, route)  7.94 us
    ppermute x2, starting transfers between devices, shifted(): return lax.ppermute(block, axis, route)  6.62 us
    slice x1, other arithmetic, body(): running = decays[i][:, None, None] * running + pieces[i]  5.2 us
    all_to_all x1, starting transfers between devices, body(): lax.all_to_all(payload, 'seg', 0, 0, tiled=True)  4.97 us
    add x1, other arithmetic, body(): running = decays[i][:, None, None] * running + pieces[i]  4.41 us
  transfers between devices with their start and end apart: 4, of which 3 were waited for; matrix products, arithmetic and copies ran while one was open for 6% of the time, Pallas kernels for 0%

profile of v1, /device:TPU:24, one launch (start us, length us, event | category | flops | bytes accessed | tf_op | source)
XLA Modules:
  0.0 99.9 jit_solution(6631790488698472753)
XLA Ops:
  0.0 0.0 copy-start
  0.0 0.0 copy-start.2
  0.0 0.0 copy-start.4
  0.0 0.0 copy-start.5
  0.0 0.0 copy-start.7
  0.0 1.1 %constant_dynamic-update-slice_fusion.3 = bf16[256,1280]{1,0:T(8,128)(2,1)S(1)} fusion(bf16[256,1024]{1,0:T(8,128)(2,1)} %param.10), kind=kLoop, calls=%fused_computation.46 | loop fusion | bytes 1048576
  1.2 0.0 copy-done.2
  1.2 0.0 copy-done.4
  1.2 0.1 slice_bitcast_fusion
  1.3 0.1 copy.89
  1.4 1.9 %collective-permute-start = (bf16[3,1281]{1,0:T(4,128)(2,1)S(1)}, bf16[3,1281]{1,0:T(4,128)(2,1)S(1)}, u32[]{:S(2)}, u32[]{:S(2)}) collective-permute-start(bf16[3,1281]{1,0:T(4,128)(2,1)S(1)} %pad_maximum_fusion.2), channel_id=1, source_target_pairs={{0,4},{4,8},{8,12},{12,16},{16,20},{20,24},{24,28},{28,32},{32,36}... | collective-permute-start | bytes 23066 | tf_op jit(solution)/shard_map/ppermute | solution.py:18
  3.4 0.0 copy-done.5
  3.4 0.0 copy-done.7
  3.4 0.1 slice_reduce_fusion.5
  3.5 0.0 copy-done
  3.5 0.6 reduce-window.6
  4.1 0.2 slice_reduce_fusion
  4.3 0.1 fusion.29
  4.4 0.2 slice_reduce_fusion.1
  4.6 0.6 slice.270
  5.1 7.9 %collective-permute-done = bf16[3,1281]{1,0:T(4,128)(2,1)S(1)} collective-permute-done((bf16[3,1281]{1,0:T(4,128)(2,1)S(1)}, bf16[3,1281]{1,0:T(4,128)(2,1)S(1)}, u32[]{:S(2)}, u32[]{:S(2)}) %collective-permute-start) | collective-permute-done | bytes 7718 | tf_op jit(solution)/shard_map/ppermute | solution.py:18
  13.1 0.6 slice.272
  13.7 0.1 fusion.26
  13.8 0.1 pad_add_fusion
  14.6 0.7 compare_convert_fusion.3
  15.3 1.2 %multiply_convert_fusion.4 = bf16[256,1280]{1,0:T(8,128)(2,1)S(1)} fusion(bf16[256,1280]{1,0:T(8,128)(2,1)S(1)} %constant_dynamic-update-slice_fusion.2, bf16[3,1280]{1,0:T(4,128)(2,1)S(1)} %slice.310, f32[256]{0:T(256)S(1)} %get-tuple-element.60, f32[1280]{0:T(1024)S(1)} %get-tuple-element.6, f32[256]{0:T(256)S(1)} %get-tuple-element.61, ...), kind=kLoop, calls=%fused_computation.13 | loop fusion | flops 9175040 | bytes 1341952 | tf_op jit(solution)/shard_map/convert_element_type | solution.py:45
  16.5 0.1 slice_convert_fusion
  16.7 0.0 copy-start.3
  16.7 0.3 copy.90
  17.0 0.6 slice.273
  17.6 0.1 exponential_select_fusion
  17.7 0.0 copy-done.3
  17.7 0.3 fusion.15
  18.0 0.3 copy.120
  18.3 0.7 exponential_multiply_fusion.1
  19.0 0.1 broadcast_in_dim.34
  19.1 1.2 %all_to_all.9 = f32[16,1,8320]{2,1,0:T(1,128)} reshape(f32[16,8320]{1,0:T(8,128)S(1)} %pad_maximum_fusion.1) | data formatting | bytes 1064960 | tf_op jit(solution)/shard_map/all_to_all | solution.py:71
  20.2 5.0 %all-to-all-start = ((f32[16,1,8320]{2,1,0:T(1,128)}), f32[16,1,8320]{2,1,0:T(1,128)S(1)}, u32[]{:S(2)}, u32[]{:S(2)}) async-start(f32[16,1,8320]{2,1,0:T(1,128)} %all_to_all.9), calls=%async_computation | async-start | bytes 1064960 | tf_op jit(solution)/shard_map/all_to_all | solution.py:71
  25.2 0.1 fusion.18
  25.3 16.0 %all-to-all-done = f32[16,1,8320]{2,1,0:T(1,128)S(1)} async-done(((f32[16,1,8320]{2,1,0:T(1,128)}), f32[16,1,8320]{2,1,0:T(1,128)S(1)}, u32[]{:S(2)}, u32[]{:S(2)}) %all-to-all-start) | async-done | bytes 532512 | tf_op jit(solution)/shard_map/all_to_all | solution.py:71
  41.3 0.7 fusion.30
  42.5 5.2 %fusion.31 = (f32[1,1,8192]{2,1,0:T(1,128)S(1)}, f32[1,1,8192]{2,1,0:T(1,128)S(1)}, f32[1,1,8192]{2,1,0:T(1,128)S(1)}, f32[1,1,8192]{2,1,0:T(1,128)S(1)}, f32[1,...) fusion(f32[16,1,8320]{2,1,0:T(1,128)S(1)} %all-to-all-done, ...), kind=kLoop, calls=%fused_computation.107 | loop fusion | flops 131072 | bytes 688164 | tf_op jit(solution)/shard_map/slice | solution.py:81
  47.9 4.4 %multiply_add_fusion = (f32[1,64,128]{2,1,0:T(8,128)S(1)}, f32[1,64,128]{2,1,0:T(8,128)S(1)}, f32[1,64,128]{2,1,0:T(8,128)S(1)}, f32[1,64,128]{2,1,0:T(8,128)S(1)}) fusion(f32[1,64,128]{2,1,0:T(8,128)S(1)} %bitcast.161, f32[]{:T(128)} %bitcast.40, f32[1,64,128]{2,1,0:T(8,128)S(1)} %bitcast.146, f32[]{:T(128)} %bitcast.41, f32[1,64,128]{2,1,0:T(8,128)S(1)} %bitcast.162, ...), kind=kLoop, calls=%fused_computation.71 | loop fusion | flops 122880 | bytes 426012 | tf_op jit(solution)/shard_map/add | solution.py:81
  52.3 0.6 constant_dynamic-update-slice_fusion.8
  52.9 0.6 constant_dynamic-update-slice_fusion.6
  53.5 4.7 %collective-permute-start.1 = (f32[1,64,128]{2,1,0:T(8,128)S(1)}, f32[1,64,128]{2,1,0:T(8,128)S(1)}, u32[]{:S(2)}, u32[]{:S(2)}) collective-permute-start(f32[1,64,128]{2,1,0:T(8,128)S(1)} %get-tuple-element.9), channel_id=1, source_target_pairs={{0,64},{64,128},{128,192},{192,256},{256,320},{320,384},{384,448},... | collective-permute-start | bytes 98312 | tf_op jit(solution)/shard_map/ppermute | solution.py:18
  58.3 0.7 constant_dynamic-update-slice_fusion.4
  68.3 0.7 stack.107
  69.0 0.0 collective-permute-done.1
  69.0 0.8 add_convert_fusion
  69.8 4.3 %all-to-all-start.1 = ((bf16[16,1,64,128]{3,2,1,0:T(8,128)(2,1)}), bf16[16,1,64,128]{3,2,1,0:T(8,128)(2,1)S(1)}, u32[]{:S(2)}, u32[]{:S(2)}) async-start(bf16[16,1,64,128]{3,2,1,0:T(8,128)(2,1)} %add_convert_fusion), calls=%async_computation.1 | async-start | bytes 524288 | tf_op jit(solution)/shard_map/all_to_all | solution.py:85
  74.1 0.2 fusion.22
  74.3 0.0 copy-start.8
  74.3 2.3 %fusion.6 = f32[256,16,64]{0,2,1:T(8,128)} fusion(f32[256,256]{1,0:T(8,128)S(1)} %fusion.22, f32[16,256]{1,0:T(8,128)S(1)} %get-tuple-element.58, pred[256,256]{1,0:T(8,128)(4,1)S(1)} %fusion.18, f32[256,16,64]{0,2,1:T(8,128)S(1)} %bitcast.137, f32[256,16]{0,1:T(8,128)S(1)} %copy-done.3), kind=kOutput, calls=%fused_computation.7 | convolution fusion | flops 139984896 | bytes 2457600 | tf_op jit(solution)/shard_map/hts,shp->thp/dot_general | solution.py:59
  76.6 8.7 %all-to-all-done.1 = bf16[16,1,64,128]{3,2,1,0:T(8,128)(2,1)S(1)} async-done(((bf16[16,1,64,128]{3,2,1,0:T(8,128)(2,1)}), bf16[16,1,64,128]{3,2,1,0:T(8,128)(2,1)S(1)}, u32[]{:S(2)}, u32[]{:S(2)}) %all-to-all-start.1) | async-done | bytes 262176 | tf_op jit(solution)/shard_map/all_to_all | solution.py:85
  85.3 0.0 copy-done.8
  85.3 1.5 %fusion.8 = f32[256,16,64]{0,2,1:T(8,128)S(1)} fusion(f32[256,16,64]{0,2,1:T(8,128)} %fusion.6, f32[256,16,64]{0,2,1:T(8,128)S(1)} %bitcast.138, f32[16]{0:T(128)S(1)} %copy-done.8, f32[256,16]{0,1:T(8,128)S(1)} %get-tuple-element.56, bf16[16,1,64,128]{3,2,1,0:T(8,128)(2,1)S(1)} %all-to-all-done.1, bf16[256,1280]{1,0:T(8,128)(2,1)S(1)} %multiply_convert_fusion.4), kind=kOutput, calls=%fused_computation.10 | convolution fusion | flops 68157440 | bytes 3490304 | tf_op jit(solution)/shard_map/tn,hpn->thp/dot_general | solution.py:90
  86.8 0.0 copy-start.1
  86.8 0.3 copy.107
  87.2 0.7 copy-done.1
  87.9 0.4 multiply_reduce_fusion
  88.3 10.5 %psum.7 = f32[256]{0:T(256)S(1)} all-reduce(f32[256]{0:T(256)S(1)} %multiply_reduce_fusion), channel_id=1, replica_groups=mesh['row'=8,'seg'=16,'head'=4] {'head'}, use_global_device_ids=true, to_apply=%region_3.4 | all-reduce | flops 256 | bytes 2048 | tf_op jit(solution)/shard_map/psum | solution.py:95
  98.8 0.0 copy-done.6
  98.8 1.2 %multiply_convert_fusion.5 = bf16[256,1024]{1,0:T(8,128)(2,1)} fusion(f32[1024]{0:T(1024)S(1)} %copy-done.6, f32[256]{0:T(256)S(1)} %add_rsqrt_fusion, f32[256,1024]{1,0:T(8,128)S(1)} %copy.107, bf16[256,1024]{1,0:T(8,128)(2,1)S(1)} %copy-done.1), kind=kLoop, calls=%fused_computation.18 | loop fusion | flops 2359296 | bytes 2102272 | tf_op jit(solution)/shard_map/convert_element_type | solution.py:97
  (28 shorter events, 0.2 us)
Async XLA Ops:
  0.0 3.5 %copy-start = (f32[256,16]{0,1:T(8,128)S(1)}, f32[256,16]{0,1:T(8,128)}, u32[]{:S(2)}) copy-start(f32[256,16]{0,1:T(8,128)} %param.14) | copy-start | bytes 49156
  0.0 1.2 %copy-start.2 = (bf16[256,256]{1,0:T(8,128)(2,1)S(1)}, bf16[256,256]{1,0:T(8,128)(2,1)}, u32[]{:S(2)}) copy-start(bf16[256,256]{1,0:T(8,128)(2,1)} %param.11) | copy-start | bytes 393220
  0.0 1.2 %copy-start.4 = (s32[256]{0:T(256)S(1)}, s32[256]{0:T(256)}, u32[]{:S(2)}) copy-start(s32[256]{0:T(256)} %param.15) | copy-start | bytes 3076
  0.0 3.4 %copy-start.5 = (f32[4,1024]{1,0:T(4,128)S(1)}, f32[4,1024]{1,0:T(4,128)}, u32[]{:S(2)}) copy-start(f32[4,1024]{1,0:T(4,128)} %param.16) | copy-start | bytes 49156
  0.0 3.4 %copy-start.7 = (f32[4,256]{1,0:T(4,128)S(1)}, f32[4,256]{1,0:T(4,128)}, u32[]{:S(2)}) copy-start(f32[4,256]{1,0:T(4,128)} %param.17) | copy-start | bytes 12292
  1.4 11.6 %collective-permute-start = (bf16[3,1281]{1,0:T(4,128)(2,1)S(1)}, bf16[3,1281]{1,0:T(4,128)(2,1)S(1)}, u32[]{:S(2)}, u32[]{:S(2)}) collective-permute-start(bf16[3,1281]{1,0:T(4,128)(2,1)S(1)} %pad_maximum_fusion.2), channel_id=1, source_target_pairs={{0,4},{4,8},{8,12},{12,16},{16,20},{20,24},{24,28},{28,32},{32,36}... | collective-permute-start | bytes 23066 | tf_op jit(solution)/shard_map/ppermute | solution.py:18
  16.7 1.0 %copy-start.3 = (f32[256,16]{0,1:T(8,128)S(1)}, f32[256,16]{0,1:T(8,128)}, u32[]{:S(2)}) copy-start(f32[256,16]{0,1:T(8,128)} %param.13) | copy-start | bytes 49156
  20.2 21.1 %all-to-all-start = ((f32[16,1,8320]{2,1,0:T(1,128)}), f32[16,1,8320]{2,1,0:T(1,128)S(1)}, u32[]{:S(2)}, u32[]{:S(2)}) async-start(f32[16,1,8320]{2,1,0:T(1,128)} %all_to_all.9), calls=%async_computation | async-start | bytes 1064960 | tf_op jit(solution)/shard_map/all_to_all | solution.py:71
  53.5 15.4 %collective-permute-start.1 = (f32[1,64,128]{2,1,0:T(8,128)S(1)}, f32[1,64,128]{2,1,0:T(8,128)S(1)}, u32[]{:S(2)}, u32[]{:S(2)}) collective-permute-start(f32[1,64,128]{2,1,0:T(8,128)S(1)} %get-tuple-element.9), channel_id=1, source_target_pairs={{0,64},{64,128},{128,192},{192,256},{256,320},{320,384},{384,448},... | collective-permute-start | bytes 98312 | tf_op jit(solution)/shard_map/ppermute | solution.py:18
  69.8 15.5 %all-to-all-start.1 = ((bf16[16,1,64,128]{3,2,1,0:T(8,128)(2,1)}), bf16[16,1,64,128]{3,2,1,0:T(8,128)(2,1)S(1)}, u32[]{:S(2)}, u32[]{:S(2)}) async-start(bf16[16,1,64,128]{3,2,1,0:T(8,128)(2,1)} %add_convert_fusion), calls=%async_computation.1 | async-start | bytes 524288 | tf_op jit(solution)/shard_map/all_to_all | solution.py:85
  74.3 11.0 %copy-start.8 = (f32[16]{0:T(128)S(1)}, f32[16]{0:T(128)}, u32[]{:S(2)}) copy-start(f32[16]{0:T(128)} %param.18) | copy-start | bytes 196
  86.8 1.0 %copy-start.1 = (bf16[256,1024]{1,0:T(8,128)(2,1)S(1)}, bf16[256,1024]{1,0:T(8,128)(2,1)}, u32[]{:S(2)}) copy-start(bf16[256,1024]{1,0:T(8,128)(2,1)} %param.12) | copy-start | bytes 1572868
  87.9 10.9 %copy-start.6 = (f32[1024]{0:T(1024)S(1)}, f32[1024]{0:T(1024)}, u32[]{:S(2)}) copy-start(f32[1024]{0:T(1024)} %param.19) | copy-start | bytes 12292

commit v2 on v1

--- a/solution.py
+++ b/solution.py
@@ -69,19 +69,22 @@
         [local.reshape(heads_dev, flat), jnp.broadcast_to(through[:, None], (heads_dev, 128))], axis=1
     )
     got = lax.all_to_all(payload, "seg", 0, 0, tiled=True).reshape(seg, per_owner, flat + 128)
-    pieces = got[:, :, :flat].reshape(seg, per_owner, head_size, states)
-    decays = got[:, :, flat]
-    folds = []
-    decay_before = []
-    running = jnp.zeros((per_owner, head_size, states), jnp.float32)
-    product = jnp.ones((per_owner,), jnp.float32)
-    for i in range(seg):
-        folds.append(running)
-        decay_before.append(product)
-        running = decays[i][:, None, None] * running + pieces[i]
-        product = product * decays[i]
-    carry = shifted(running, "row", 1)
-    entering = jnp.stack(decay_before)[:, :, None, None] * carry[None] + jnp.stack(folds)
+    pieces = jnp.transpose(got[:, :, :flat], (1, 0, 2))
+    decays = got[:, :, flat].T
+    after = jnp.arange(seg + 1)[:, None, None]
+    source = jnp.arange(seg)[None, :, None]
+    between = (source < jnp.arange(seg)[None, None, :]) & (jnp.arange(seg)[None, None, :] < after)
+    spans = jnp.prod(jnp.where(between[None], decays[:, None, None, :], 1.0), axis=3)
+    weights_to = jnp.where((source[..., 0] < after[..., 0])[None], spans, 0.0)
+    head_first = jnp.prod(
+        jnp.where(jnp.arange(seg)[None, :] < jnp.arange(seg)[:, None], decays[:, None, :], 1.0), axis=2
+    )
+    exact = lax.Precision.HIGHEST
+    total_row = jnp.einsum("gj,gjf->gf", weights_to[:, seg], pieces, precision=exact)
+    carry = shifted(total_row, "row", 1)
+    folds = jnp.einsum("gij,gjf->gif", weights_to[:, :seg], pieces, precision=exact)
+    entering = head_first[:, :, None] * carry[:, None, :] + folds
+    entering = jnp.transpose(entering, (1, 0, 2)).reshape(seg, per_owner, head_size, states)
     entered = lax.all_to_all(entering.astype(jnp.bfloat16), "seg", 0, 0, tiled=True).reshape(
         heads_dev, head_size, states
     )
@@ -92,7 +95,15 @@
     )
     scanned = inners + carried + skip[None, :, None] * xconv.astype(jnp.float32)
     gated_rows = scanned.reshape(GROUP, head_cols) * jax.nn.silu(gate_z.astype(jnp.float32))
-    squares = lax.psum(jnp.sum(gated_rows * gated_rows, axis=1), "head")
+    own = jnp.sum(gated_rows * gated_rows, axis=1)
+    width = lax.axis_size("head")
+    me = lax.axis_index("head")
+    parts = [own] + [
+        lax.ppermute(own, "head", [(i, (i + d) % width) for i in range(width)]) for d in range(1, width)
+    ]
+    squares = sum(
+        sum(jnp.where((me - d) % width == src, parts[d], 0.0) for d in range(width)) for src in range(width)
+    )
     scale = lax.rsqrt(squares / (head_cols * lax.axis_size("head")) + EPS)
     return (gated_rows * scale[:, None] * norm_gain[None, :]).astype(jnp.bfloat16)
 

time: 101 us -> 84.9 us (0.84)
  the two profiles are of different devices: /device:TPU:24 before, /device:TPU:32 now
where the time goes in v2:
time: 84.9 us; the launch traced here: 84.4 us
  waiting for transfers between devices  38.8 us (46%)
  starting transfers between devices  25.1 us (30%)
  local copies, waits for them, and re-layouts  7.66 us (9%)
  matrix products  5.85 us (7%)
  other arithmetic  5.73 us (7%)
  between operations  1.18 us (1%)
    all_to_all x1, waiting for transfers between devices, body(): lax.all_to_all(payload, 'seg', 0, 0, tiled=True)  15.9 us
    ppermute x2, waiting for transfers between devices, shifted(): return lax.ppermute(block, axis, route)  12.2 us
    ppermute x3, starting transfers between devices, body(): lax.ppermute(own, 'head', [(i, (i + d) % width) for i in range(width)])  11.4 us
    all_to_all x1, waiting for transfers between devices, body(): lax.all_to_all(entering.astype(jnp.bfloat16), 'seg', 0, 0, tiled=True)  8.61 us
    all_to_all x1, starting transfers between devices, body(): lax.all_to_all(payload, 'seg', 0, 0, tiled=True)  4.97 us
    ppermute x2, starting transfers between devices, shifted(): return lax.ppermute(block, axis, route)  4.51 us
    all_to_all x1, starting transfers between devices, body(): lax.all_to_all(entering.astype(jnp.bfloat16), 'seg', 0, 0, tiled=True)  4.26 us
    unnamed x22, local copies, waits for them, and re-layouts  2.95 us
  transfers between devices with their start and end apart: 7, of which 5 were waited for; matrix products, arithmetic and copies ran while one was open for 5% of the time, Pallas kernels for 0%

profile of v2, /device:TPU:32, one launch (start us, length us, event | category | flops | bytes accessed | tf_op | source)
XLA Modules:
  0.0 84.4 jit_solution(5276348017592965434)
XLA Ops:
  0.0 0.0 copy-start
  0.0 0.0 copy-start.5
  0.0 0.0 copy-start.7
  0.0 1.1 %constant_dynamic-update-slice_fusion.3 = bf16[256,1280]{1,0:T(8,128)(2,1)S(1)} fusion(bf16[256,1024]{1,0:T(8,128)(2,1)} %param.10), kind=kLoop, calls=%fused_computation.61 | loop fusion | bytes 1048576
  1.2 0.0 copy-done.2
  1.2 0.0 copy-done.4
  1.2 0.1 slice_bitcast_fusion.4
  1.3 0.1 copy.50
  1.4 1.9 %collective-permute-start = (bf16[3,1281]{1,0:T(4,128)(2,1)S(1)}, bf16[3,1281]{1,0:T(4,128)(2,1)S(1)}, u32[]{:S(2)}, u32[]{:S(2)}) collective-permute-start(bf16[3,1281]{1,0:T(4,128)(2,1)S(1)} %pad_maximum_fusion.2), channel_id=1, source_target_pairs={{0,4},{4,8},{8,12},{12,16},{16,20},{20,24},{24,28},{28,32},{32,36}... | collective-permute-start | bytes 23066 | tf_op jit(solution)/shard_map/ppermute | solution.py:18
  3.4 0.0 copy-done.5
  3.4 0.0 copy-done.7
  3.4 0.1 slice_reduce_fusion.7
  3.5 0.0 copy-done
  3.5 0.6 reduce-window.6
  4.1 0.2 slice_reduce_fusion
  4.3 0.1 fusion.39
  4.4 0.2 slice_reduce_fusion.3
  4.6 0.6 slice.103
  5.1 7.9 %collective-permute-done = bf16[3,1281]{1,0:T(4,128)(2,1)S(1)} collective-permute-done((bf16[3,1281]{1,0:T(4,128)(2,1)S(1)}, bf16[3,1281]{1,0:T(4,128)(2,1)S(1)}, u32[]{:S(2)}, u32[]{:S(2)}) %collective-permute-start) | collective-permute-done | bytes 7718 | tf_op jit(solution)/shard_map/ppermute | solution.py:18
  13.1 0.6 slice.105
  13.7 0.1 fusion.36
  13.8 0.1 pad_add_fusion
  14.6 0.7 compare_convert_fusion.3
  15.3 1.2 %multiply_convert_fusion.4 = bf16[256,1280]{1,0:T(8,128)(2,1)S(1)} fusion(bf16[256,1280]{1,0:T(8,128)(2,1)S(1)} %constant_dynamic-update-slice_fusion.2, bf16[3,1280]{1,0:T(4,128)(2,1)S(1)} %slice.114, f32[256]{0:T(256)S(1)} %get-tuple-element.14, f32[1280]{0:T(1024)S(1)} %get-tuple-element.6, f32[256]{0:T(256)S(1)} %get-tuple-element.15, ...), kind=kLoop, calls=%fused_computation.13 | loop fusion | flops 9175040 | bytes 1341952 | tf_op jit(solution)/shard_map/convert_element_type | solution.py:45
  16.6 0.1 slice_convert_fusion
  16.7 0.0 copy-start.3
  16.7 0.3 copy.51
  17.0 0.6 slice.106
  17.6 0.1 exponential_select_fusion
  17.7 0.3 fusion.15
  18.0 0.3 copy.80
  18.3 0.7 exponential_multiply_fusion.1
  19.0 0.1 broadcast_in_dim.119
  19.1 1.2 %all_to_all.9 = f32[16,1,8320]{2,1,0:T(1,128)} reshape(f32[16,8320]{1,0:T(8,128)S(1)} %pad_maximum_fusion.1) | data formatting | bytes 1064960 | tf_op jit(solution)/shard_map/all_to_all | solution.py:71
  20.3 5.0 %all-to-all-start = ((f32[16,1,8320]{2,1,0:T(1,128)}), f32[16,1,8320]{2,1,0:T(1,128)S(1)}, u32[]{:S(2)}, u32[]{:S(2)}) async-start(f32[16,1,8320]{2,1,0:T(1,128)} %all_to_all.9), calls=%async_computation | async-start | bytes 1064960 | tf_op jit(solution)/shard_map/all_to_all | solution.py:71
  25.3 0.1 fusion.25
  25.4 15.9 %all-to-all-done = f32[16,1,8320]{2,1,0:T(1,128)S(1)} async-done(((f32[16,1,8320]{2,1,0:T(1,128)}), f32[16,1,8320]{2,1,0:T(1,128)S(1)}, u32[]{:S(2)}, u32[]{:S(2)}) %all-to-all-start) | async-done | bytes 532512 | tf_op jit(solution)/shard_map/all_to_all | solution.py:71
  41.3 0.2 slice_reduce_fusion.2
  41.5 0.1 select_reduce_fusion
  41.7 0.2 slice_reduce_fusion.1
  41.9 0.1 slice.129
  41.9 0.7 fusion.18
  42.6 2.6 %collective-permute-start.1 = (f32[1,8192]{1,0:T(1,128)S(1)}, f32[1,8192]{1,0:T(1,128)S(1)}, u32[]{:S(2)}, u32[]{:S(2)}) collective-permute-start(f32[1,8192]{1,0:T(1,128)S(1)} %fusion.18), channel_id=1, source_target_pairs={{0,64},{64,128},{128,192},{192,256},{256,320},{320,384},{384,448},... | collective-permute-start | bytes 98312 | tf_op jit(solution)/shard_map/ppermute | solution.py:18
  45.2 0.1 select_reduce_fusion.1
  45.3 4.3 %collective-permute-done.1 = f32[1,8192]{1,0:T(1,128)S(1)} collective-permute-done((f32[1,8192]{1,0:T(1,128)S(1)}, f32[1,8192]{1,0:T(1,128)S(1)}, u32[]{:S(2)}, u32[]{:S(2)}) %collective-permute-start.1) | collective-permute-done | bytes 32800 | tf_op jit(solution)/shard_map/ppermute | solution.py:18
  49.6 0.9 %fusion.23 = bf16[2,8,64,128]{3,1,2,0:T(8,128)(2,1)S(1)} fusion(f32[8192]{0:T(1024)S(1)} %bitcast.76, f32[16]{0:T(128)S(1)} %select_reduce_fusion.1, f32[16,1,8192]{2,1,0:T(1,128)S(1)} %slice.129, f32[1,17,16]{1,2,0:T(8,128)S(1)} %bitcast_select_fusion), kind=kOutput, calls=%fused_computation.39 | convolution fusion | flops 25559040 | bytes 820352 | tf_op jit(solution)/shard_map/gij,gjf->gif/dot_general | solution.py:85
  50.5 0.8 copy.60
  51.2 4.3 %all-to-all-start.1 = ((bf16[16,1,64,128]{3,2,1,0:T(8,128)(2,1)}), bf16[16,1,64,128]{3,2,1,0:T(8,128)(2,1)S(1)}, u32[]{:S(2)}, u32[]{:S(2)}) async-start(bf16[16,1,64,128]{3,2,1,0:T(8,128)(2,1)} %bitcast.14), calls=%async_computation.1 | async-start | bytes 524288 | tf_op jit(solution)/shard_map/all_to_all | solution.py:88
  55.5 0.2 fusion.29
  55.7 0.0 copy-start.8
  55.7 2.3 %fusion.6 = f32[256,16,64]{0,2,1:T(8,128)} fusion(f32[256,256]{1,0:T(8,128)S(1)} %fusion.29, f32[16,256]{1,0:T(8,128)S(1)} %get-tuple-element.12, pred[256,256]{1,0:T(8,128)(4,1)S(1)} %fusion.25, f32[256,16,64]{0,2,1:T(8,128)S(1)} %bitcast.71, f32[256,16]{0,1:T(8,128)S(1)} %copy-done.3), kind=kOutput, calls=%fused_computation.7 | convolution fusion | flops 139984896 | bytes 2457600 | tf_op jit(solution)/shard_map/hts,shp->thp/dot_general | solution.py:59
  58.0 8.6 %all-to-all-done.1 = bf16[16,1,64,128]{3,2,1,0:T(8,128)(2,1)S(1)} async-done(((bf16[16,1,64,128]{3,2,1,0:T(8,128)(2,1)}), bf16[16,1,64,128]{3,2,1,0:T(8,128)(2,1)S(1)}, u32[]{:S(2)}, u32[]{:S(2)}) %all-to-all-start.1) | async-done | bytes 262176 | tf_op jit(solution)/shard_map/all_to_all | solution.py:88
  66.6 1.5 %fusion.8 = f32[256,16,64]{0,2,1:T(8,128)S(1)} fusion(f32[256,16,64]{0,2,1:T(8,128)} %fusion.6, f32[256,16,64]{0,2,1:T(8,128)S(1)} %bitcast.72, f32[16]{0:T(128)S(1)} %copy-done.8, f32[256,16]{0,1:T(8,128)S(1)} %get-tuple-element.10, bf16[16,1,64,128]{3,2,1,0:T(8,128)(2,1)S(1)} %all-to-all-done.1, bf16[256,1280]{1,0:T(8,128)(2,1)S(1)} %multiply_convert_fusion.4), kind=kOutput, calls=%fused_computation.10 | convolution fusion | flops 68157440 | bytes 3490304 | tf_op jit(solution)/shard_map/tn,hpn->thp/dot_general | solution.py:93
  68.2 0.0 copy-start.1
  68.2 0.3 copy.55
  68.5 0.7 copy-done.1
  69.2 0.4 multiply_reduce_fusion
  69.6 3.4 %collective-permute-start.2 = (f32[256]{0:T(256)S(1)}, f32[256]{0:T(256)S(1)}, u32[]{:S(2)}, u32[]{:S(2)}) collective-permute-start(f32[256]{0:T(256)S(1)} %multiply_reduce_fusion), channel_id=1, source_target_pairs={{0,1},{1,2},{2,3},{3,0},{4,5},{5,6},{6,7},{7,4},{8,9},{9,10},{10,1... | collective-permute-start | bytes 3080 | tf_op jit(solution)/shard_map/ppermute | solution.py:102
  73.0 4.6 %collective-permute-start.3 = (f32[256]{0:T(256)S(1)}, f32[256]{0:T(256)S(1)}, u32[]{:S(2)}, u32[]{:S(2)}) collective-permute-start(f32[256]{0:T(256)S(1)} %multiply_reduce_fusion), channel_id=1, source_target_pairs={{0,2},{1,3},{2,0},{3,1},{4,6},{5,7},{6,4},{7,5},{8,10},{9,11},{10,... | collective-permute-start | bytes 3080 | tf_op jit(solution)/shard_map/ppermute | solution.py:102
  77.7 3.3 %collective-permute-start.4 = (f32[256]{0:T(256)S(1)}, f32[256]{0:T(256)S(1)}, u32[]{:S(2)}, u32[]{:S(2)}) collective-permute-start(f32[256]{0:T(256)S(1)} %multiply_reduce_fusion), channel_id=1, source_target_pairs={{0,3},{1,0},{2,1},{3,2},{4,7},{5,4},{6,5},{7,6},{8,11},{9,8},{10,9... | collective-permute-start | bytes 3080 | tf_op jit(solution)/shard_map/ppermute | solution.py:102
  81.1 0.0 collective-permute-done.2
  81.1 0.0 collective-permute-done.3
  81.1 2.1 %collective-permute-done.4 = f32[256]{0:T(256)S(1)} collective-permute-done((f32[256]{0:T(256)S(1)}, f32[256]{0:T(256)S(1)}, u32[]{:S(2)}, u32[]{:S(2)}) %collective-permute-start.4) | collective-permute-done | bytes 1056 | tf_op jit(solution)/shard_map/ppermute | solution.py:102
  83.2 1.2 %multiply_convert_fusion.5 = bf16[256,1024]{1,0:T(8,128)(2,1)} fusion(f32[1024]{0:T(1024)S(1)} %copy-done.6, f32[256]{0:T(256)S(1)} %add_rsqrt_fusion, f32[256,1024]{1,0:T(8,128)S(1)} %copy.55, bf16[256,1024]{1,0:T(8,128)(2,1)S(1)} %copy-done.1), kind=kLoop, calls=%fused_computation.18 | loop fusion | flops 2359296 | bytes 2102272 | tf_op jit(solution)/shard_map/convert_element_type | solution.py:108
  (22 shorter events, 0.2 us)
Async XLA Ops:
  0.0 3.5 %copy-start = (f32[256,16]{0,1:T(8,128)S(1)}, f32[256,16]{0,1:T(8,128)}, u32[]{:S(2)}) copy-start(f32[256,16]{0,1:T(8,128)} %param.14) | copy-start | bytes 49156
  0.0 1.2 %copy-start.2 = (bf16[256,256]{1,0:T(8,128)(2,1)S(1)}, bf16[256,256]{1,0:T(8,128)(2,1)}, u32[]{:S(2)}) copy-start(bf16[256,256]{1,0:T(8,128)(2,1)} %param.11) | copy-start | bytes 393220
  0.0 1.2 %copy-start.4 = (s32[256]{0:T(256)S(1)}, s32[256]{0:T(256)}, u32[]{:S(2)}) copy-start(s32[256]{0:T(256)} %param.15) | copy-start | bytes 3076
  0.0 3.4 %copy-start.5 = (f32[4,1024]{1,0:T(4,128)S(1)}, f32[4,1024]{1,0:T(4,128)}, u32[]{:S(2)}) copy-start(f32[4,1024]{1,0:T(4,128)} %param.16) | copy-start | bytes 49156
  0.0 3.4 %copy-start.7 = (f32[4,256]{1,0:T(4,128)S(1)}, f32[4,256]{1,0:T(4,128)}, u32[]{:S(2)}) copy-start(f32[4,256]{1,0:T(4,128)} %param.17) | copy-start | bytes 12292
  1.4 11.6 %collective-permute-start = (bf16[3,1281]{1,0:T(4,128)(2,1)S(1)}, bf16[3,1281]{1,0:T(4,128)(2,1)S(1)}, u32[]{:S(2)}, u32[]{:S(2)}) collective-permute-start(bf16[3,1281]{1,0:T(4,128)(2,1)S(1)} %pad_maximum_fusion.2), channel_id=1, source_target_pairs={{0,4},{4,8},{8,12},{12,16},{16,20},{20,24},{24,28},{28,32},{32,36}... | collective-permute-start | bytes 23066 | tf_op jit(solution)/shard_map/ppermute | solution.py:18
  16.7 1.0 %copy-start.3 = (f32[256,16]{0,1:T(8,128)S(1)}, f32[256,16]{0,1:T(8,128)}, u32[]{:S(2)}) copy-start(f32[256,16]{0,1:T(8,128)} %param.13) | copy-start | bytes 49156
  20.3 21.1 %all-to-all-start = ((f32[16,1,8320]{2,1,0:T(1,128)}), f32[16,1,8320]{2,1,0:T(1,128)S(1)}, u32[]{:S(2)}, u32[]{:S(2)}) async-start(f32[16,1,8320]{2,1,0:T(1,128)} %all_to_all.9), calls=%async_computation | async-start | bytes 1064960 | tf_op jit(solution)/shard_map/all_to_all | solution.py:71
  42.6 7.0 %collective-permute-start.1 = (f32[1,8192]{1,0:T(1,128)S(1)}, f32[1,8192]{1,0:T(1,128)S(1)}, u32[]{:S(2)}, u32[]{:S(2)}) collective-permute-start(f32[1,8192]{1,0:T(1,128)S(1)} %fusion.18), channel_id=1, source_target_pairs={{0,64},{64,128},{128,192},{192,256},{256,320},{320,384},{384,448},... | collective-permute-start | bytes 98312 | tf_op jit(solution)/shard_map/ppermute | solution.py:18
  51.2 15.4 %all-to-all-start.1 = ((bf16[16,1,64,128]{3,2,1,0:T(8,128)(2,1)}), bf16[16,1,64,128]{3,2,1,0:T(8,128)(2,1)S(1)}, u32[]{:S(2)}, u32[]{:S(2)}) async-start(bf16[16,1,64,128]{3,2,1,0:T(8,128)(2,1)} %bitcast.14), calls=%async_computation.1 | async-start | bytes 524288 | tf_op jit(solution)/shard_map/all_to_all | solution.py:88
  55.7 11.0 %copy-start.8 = (f32[16]{0:T(128)S(1)}, f32[16]{0:T(128)}, u32[]{:S(2)}) copy-start(f32[16]{0:T(128)} %param.18) | copy-start | bytes 196
  68.2 1.0 %copy-start.1 = (bf16[256,1024]{1,0:T(8,128)(2,1)S(1)}, bf16[256,1024]{1,0:T(8,128)(2,1)}, u32[]{:S(2)}) copy-start(bf16[256,1024]{1,0:T(8,128)(2,1)} %param.12) | copy-start | bytes 1572868
  69.2 13.9 %copy-start.6 = (f32[1024]{0:T(1024)S(1)}, f32[1024]{0:T(1024)}, u32[]{:S(2)}) copy-start(f32[1024]{0:T(1024)} %param.19) | copy-start | bytes 12292
  69.6 11.4 %collective-permute-start.2 = (f32[256]{0:T(256)S(1)}, f32[256]{0:T(256)S(1)}, u32[]{:S(2)}, u32[]{:S(2)}) collective-permute-start(f32[256]{0:T(256)S(1)} %multiply_reduce_fusion), channel_id=1, source_target_pairs={{0,1},{1,2},{2,3},{3,0},{4,5},{5,6},{6,7},{7,4},{8,9},{9,10},{10,1... | collective-permute-start | bytes 3080 | tf_op jit(solution)/shard_map/ppermute | solution.py:102
  73.0 8.0 %collective-permute-start.3 = (f32[256]{0:T(256)S(1)}, f32[256]{0:T(256)S(1)}, u32[]{:S(2)}, u32[]{:S(2)}) collective-permute-start(f32[256]{0:T(256)S(1)} %multiply_reduce_fusion), channel_id=1, source_target_pairs={{0,2},{1,3},{2,0},{3,1},{4,6},{5,7},{6,4},{7,5},{8,10},{9,11},{10,... | collective-permute-start | bytes 3080 | tf_op jit(solution)/shard_map/ppermute | solution.py:102
  77.7 5.5 %collective-permute-start.4 = (f32[256]{0:T(256)S(1)}, f32[256]{0:T(256)S(1)}, u32[]{:S(2)}, u32[]{:S(2)}) collective-permute-start(f32[256]{0:T(256)S(1)} %multiply_reduce_fusion), channel_id=1, source_target_pairs={{0,3},{1,0},{2,1},{3,2},{4,7},{5,4},{6,5},{7,6},{8,11},{9,8},{10,9... | collective-permute-start | bytes 3080 | tf_op jit(solution)/shard_map/ppermute | solution.py:102

commit v3 on v1

--- a/solution.py
+++ b/solution.py
@@ -24,8 +24,6 @@
     head_size = head_cols // heads_dev
     states = bc_raw.shape[1] // 2
     taps = conv_x.shape[0]
-    seg = lax.axis_size("seg")
-    per_owner = heads_dev // seg
     raw_all = jnp.concatenate([x_raw, bc_raw], axis=1)
     labels = doc_ids + 1
     edge = jnp.concatenate(
@@ -64,25 +62,27 @@
     local = jnp.einsum("shp,sn->hpn", written, bconv, preferred_element_type=jnp.float32)
     through = jnp.exp(cum[-1]) * cont[-1]
 
-    flat = head_size * states
+    owners = lax.axis_size(SEQ)
+    rows_per = heads_dev * head_size // owners
+    width = rows_per * states
     payload = jnp.concatenate(
-        [local.reshape(heads_dev, flat), jnp.broadcast_to(through[:, None], (heads_dev, 128))], axis=1
+        [
+            local.reshape(owners, width),
+            jnp.broadcast_to(jnp.repeat(through, owners // heads_dev)[:, None], (owners, 128)),
+        ],
+        axis=1,
     )
-    got = lax.all_to_all(payload, "seg", 0, 0, tiled=True).reshape(seg, per_owner, flat + 128)
-    pieces = got[:, :, :flat].reshape(seg, per_owner, head_size, states)
-    decays = got[:, :, flat]
-    folds = []
-    decay_before = []
-    running = jnp.zeros((per_owner, head_size, states), jnp.float32)
-    product = jnp.ones((per_owner,), jnp.float32)
-    for i in range(seg):
-        folds.append(running)
-        decay_before.append(product)
-        running = decays[i][:, None, None] * running + pieces[i]
-        product = product * decays[i]
-    carry = shifted(running, "row", 1)
-    entering = jnp.stack(decay_before)[:, :, None, None] * carry[None] + jnp.stack(folds)
-    entered = lax.all_to_all(entering.astype(jnp.bfloat16), "seg", 0, 0, tiled=True).reshape(
+    got = lax.all_to_all(payload, SEQ, 0, 0, tiled=True)
+    pieces = got[:, :width]
+    decays = got[:, width]
+    after = jnp.arange(owners)[:, None, None]
+    source = jnp.arange(owners)[None, :, None]
+    middle = jnp.arange(owners)[None, None, :]
+    between = (source < middle) & (middle < after)
+    spans = jnp.prod(jnp.where(between, decays[None, None, :], 1.0), axis=2)
+    weights_to = jnp.where(source[..., 0] < after[..., 0], spans, 0.0)
+    entering = jnp.dot(weights_to, pieces, precision=lax.Precision.HIGHEST)
+    entered = lax.all_to_all(entering.astype(jnp.bfloat16), SEQ, 0, 0, tiled=True).reshape(
         heads_dev, head_size, states
     )
 
@@ -92,7 +92,12 @@
     )
     scanned = inners + carried + skip[None, :, None] * xconv.astype(jnp.float32)
     gated_rows = scanned.reshape(GROUP, head_cols) * jax.nn.silu(gate_z.astype(jnp.float32))
-    squares = lax.psum(jnp.sum(gated_rows * gated_rows, axis=1), "head")
+    own = jnp.sum(gated_rows * gated_rows, axis=1)
+    ways = lax.axis_size("head")
+    each = lax.all_to_all(jnp.broadcast_to(own[None], (ways, own.shape[0])), "head", 0, 0, tiled=True)
+    squares = each[0]
+    for src in range(1, ways):
+        squares = squares + each[src]
     scale = lax.rsqrt(squares / (head_cols * lax.axis_size("head")) + EPS)
     return (gated_rows * scale[:, None] * norm_gain[None, :]).astype(jnp.bfloat16)
 

time: 101 us -> 97.3 us (0.963)
  the two profiles are of different devices: /device:TPU:24 before, /device:TPU:8 now
where the time goes in v3:
time: 97.3 us; the launch traced here: 96.8 us
  waiting for transfers between devices  41.7 us (43%)
  starting transfers between devices  20.4 us (21%)
  other arithmetic  10.7 us (11%)
  blocking collectives  9.4 us (10%)
  local copies, waits for them, and re-layouts  8.64 us (9%)
  matrix products  4.9 us (5%)
  between operations  1.01 us (1%)
    all_to_all x1, waiting for transfers between devices, body(): got = lax.all_to_all(payload, SEQ, 0, 0, tiled=True)  21.5 us
    all_to_all x1, waiting for transfers between devices, body(): lax.all_to_all(entering.astype(jnp.bfloat16), SEQ, 0, 0, tiled=True)  12.2 us
    all_to_all x1, starting transfers between devices, body(): got = lax.all_to_all(payload, SEQ, 0, 0, tiled=True)  11.9 us
    all_to_all x1, blocking collectives, body(): lax.all_to_all(jnp.broadcast_to(own[None], (ways, own.shape[0])), 'head',...  9.4 us
    ppermute x1, waiting for transfers between devices, shifted(): return lax.ppermute(block, axis, route)  7.96 us
    all_to_all x1, starting transfers between devices, body(): lax.all_to_all(entering.astype(jnp.bfloat16), SEQ, 0, 0, tiled=True)  6.53 us
    unnamed x23, local copies, waits for them, and re-layouts  3.32 us
    dot_general x1, matrix products, body(): jnp.einsum('hts,shp->thp', weights, xdt, preferred_element_type=jnp.float32)  2.32 us
  transfers between devices with their start and end apart: 3, of which 3 were waited for; matrix products, arithmetic and copies ran while one was open for 4% of the time, Pallas kernels for 0%

profile of v3, /device:TPU:8, one launch (start us, length us, event | category | flops | bytes accessed | tf_op | source)
XLA Modules:
  0.0 96.8 jit_solution(18070087724905115743)
XLA Ops:
  0.0 0.0 copy-start
  0.0 0.0 copy-start.4
  0.0 0.0 copy-start.5
  0.0 0.0 copy-start.7
  0.0 0.7 broadcast_add_fusion
  0.8 0.1 slice_bitcast_fusion
  0.9 0.1 copy.44
  1.0 1.1 %constant_dynamic-update-slice_fusion.3 = bf16[256,1280]{1,0:T(8,128)(2,1)S(1)} fusion(bf16[256,1024]{1,0:T(8,128)(2,1)} %param.10), kind=kLoop, calls=%fused_computation.60 | loop fusion | bytes 1048576
  2.0 0.0 copy-done.2
  2.1 1.9 %collective-permute-start = (bf16[3,1281]{1,0:T(4,128)(2,1)S(1)}, bf16[3,1281]{1,0:T(4,128)(2,1)S(1)}, u32[]{:S(2)}, u32[]{:S(2)}) collective-permute-start(bf16[3,1281]{1,0:T(4,128)(2,1)S(1)} %pad_maximum_fusion.2), channel_id=1, source_target_pairs={{0,4},{4,8},{8,12},{12,16},{16,20},{20,24},{24,28},{28,32},{32,36}... | collective-permute-start | bytes 23066 | tf_op jit(solution)/shard_map/ppermute | solution.py:18
  4.0 0.0 copy-done
  4.1 0.6 reduce-window.6
  4.6 0.2 slice_reduce_fusion.1
  4.9 0.0 copy-done.5
  4.9 0.0 copy-done.7
  4.9 0.1 slice_reduce_fusion.6
  4.9 0.1 fusion.34
  5.0 0.2 slice_reduce_fusion.2
  5.2 0.0 copy-done.4
  5.2 0.6 slice.113
  5.8 8.0 %collective-permute-done = bf16[3,1281]{1,0:T(4,128)(2,1)S(1)} collective-permute-done((bf16[3,1281]{1,0:T(4,128)(2,1)S(1)}, bf16[3,1281]{1,0:T(4,128)(2,1)S(1)}, u32[]{:S(2)}, u32[]{:S(2)}) %collective-permute-start) | collective-permute-done | bytes 7718 | tf_op jit(solution)/shard_map/ppermute | solution.py:18
  13.8 0.6 slice.115
  14.3 0.1 fusion.30
  14.5 0.1 pad_add_fusion
  15.2 0.7 compare_convert_fusion.3
  16.0 0.6 slice.116
  16.5 0.6 exponential_multiply_fusion.1
  17.2 0.1 broadcast_in_dim.89
  17.3 0.1 broadcast_in_dim.90
  17.4 0.1 exponential_multiply_fusion
  17.5 1.2 %multiply_convert_fusion.4 = bf16[256,1280]{1,0:T(8,128)(2,1)S(1)} fusion(bf16[256,1280]{1,0:T(8,128)(2,1)S(1)} %constant_dynamic-update-slice_fusion.2, bf16[3,1280]{1,0:T(4,128)(2,1)S(1)} %slice.126, f32[256]{0:T(256)S(1)} %get-tuple-element.14, f32[1280]{0:T(1024)S(1)} %get-tuple-element.6, f32[256]{0:T(256)S(1)} %get-tuple-element.15, ...), kind=kLoop, calls=%fused_computation.14 | loop fusion | flops 9175040 | bytes 1341952 | tf_op jit(solution)/shard_map/convert_element_type | solution.py:43
  18.7 0.1 slice_convert_fusion
  18.8 0.0 copy-start.3
  18.8 0.3 copy.45
  19.2 0.4 copy-done.3
  19.6 0.3 fusion.16
  19.9 0.1 reshape.181
  19.9 0.1 broadcast_in_dim.91
  20.1 1.2 %all_to_all.18 = f32[128,1,1152]{2,1,0:T(1,128)} reshape(f32[128,1152]{1,0:T(8,128)S(1)} %pad_maximum_fusion.1) | data formatting | bytes 1179648 | tf_op jit(solution)/shard_map/all_to_all | solution.py:75
  21.3 11.9 %all-to-all-start = ((f32[128,1,1152]{2,1,0:T(1,128)}), f32[128,1,1152]{2,1,0:T(1,128)S(1)}, u32[]{:S(2)}, u32[]{:S(2)}) async-start(f32[128,1,1152]{2,1,0:T(1,128)} %all_to_all.18), calls=%async_computation | async-start | bytes 1179648 | tf_op jit(solution)/shard_map/all_to_all | solution.py:75
  33.2 0.1 fusion.19
  33.4 21.5 %all-to-all-done = f32[128,1,1152]{2,1,0:T(1,128)S(1)} async-done(((f32[128,1,1152]{2,1,0:T(1,128)}), f32[128,1,1152]{2,1,0:T(1,128)S(1)}, u32[]{:S(2)}, u32[]{:S(2)}) %all-to-all-start) | async-done | bytes 589856 | tf_op jit(solution)/shard_map/all_to_all | solution.py:75
  54.9 0.1 slice_reduce_fusion
  55.0 2.2 %select_reduce_fusion = f32[128,128]{1,0:T(8,128)S(1)} fusion(f32[128]{0:T(128)S(1)} %slice_reduce_fusion, pred[128,128]{1,0:T(8,128)(4,1)S(1)} %get-tuple-element.21, pred[128,128]{1,0:T(8,128)(4,1)S(1)} %get-tuple-element.20), kind=kLoop, calls=%fused_computation | loop fusion | flops 6275072 | bytes 98816 | tf_op jit(solution)/shard_map/reduce_prod | solution.py:82
  57.3 0.6 fusion.9
  57.9 0.5 broadcast.92
  58.4 0.8 reduce.17
  59.2 0.9 reshape.199
  60.0 6.5 %all-to-all-start.1 = ((bf16[128,2,512]{2,1,0:T(2,128)(2,1)}), bf16[128,2,512]{2,1,0:T(2,128)(2,1)S(1)}, u32[]{:S(2)}, u32[]{:S(2)}) async-start(bf16[128,2,512]{2,1,0:T(2,128)(2,1)} %reshape.199), calls=%async_computation.1 | async-start | bytes 524288 | tf_op jit(solution)/shard_map/all_to_all | solution.py:85
  66.6 0.2 fusion.24
  66.8 2.3 %fusion.6 = f32[256,16,64]{0,2,1:T(8,128)} fusion(f32[256,256]{1,0:T(8,128)S(1)} %fusion.24, f32[16,256]{1,0:T(8,128)S(1)} %get-tuple-element.12, pred[256,256]{1,0:T(8,128)(4,1)S(1)} %fusion.19, f32[256,16,64]{0,2,1:T(8,128)S(1)} %bitcast.45, f32[256,16]{0,1:T(8,128)S(1)} %copy-done.3), kind=kOutput, calls=%fused_computation.8 | convolution fusion | flops 139984896 | bytes 2457600 | tf_op jit(solution)/shard_map/hts,shp->thp/dot_general | solution.py:57
  69.1 12.2 %all-to-all-done.1 = bf16[128,2,512]{2,1,0:T(2,128)(2,1)S(1)} async-done(((bf16[128,2,512]{2,1,0:T(2,128)(2,1)}), bf16[128,2,512]{2,1,0:T(2,128)(2,1)S(1)}, u32[]{:S(2)}, u32[]{:S(2)}) %all-to-all-start.1) | async-done | bytes 262176 | tf_op jit(solution)/shard_map/all_to_all | solution.py:85
  81.3 0.2 reshape.200
  81.5 1.5 %reduce.8 = bf16[128,1024]{1,0:T(8,128)(2,1)S(1)} reduce(bf16[128,1,1024]{2,1,0:T(2,128)(2,1)S(1)} %reshape.200, bf16[]{:T(256)} %constant.31), dimensions={1}, to_apply=%all_to_all.22.reduce_sub_computation | reduce | bytes 524290 | tf_op jit(solution)/shard_map/all_to_all | solution.py:85
  83.1 0.1 reshape.182
  83.2 0.0 copy-done.8
  83.2 1.5 %fusion.8 = f32[256,16,64]{0,2,1:T(8,128)S(1)} fusion(f32[256,16,64]{0,2,1:T(8,128)} %fusion.6, bf16[16,64,128]{2,1,0:T(8,128)(2,1)S(1)} %reshape.182, f32[256,16,64]{0,2,1:T(8,128)S(1)} %bitcast.46, f32[16]{0:T(128)S(1)} %copy-done.8, f32[256,16]{0,1:T(8,128)S(1)} %get-tuple-element.9, bf16[256,1280]{1,0:T(8,128)(2,1)S(1)} %multiply_convert_fusion.4), kind=kOutput, calls=%fused_computation.11 | convolution fusion | flops 68157440 | bytes 3490304 | tf_op jit(solution)/shard_map/tn,hpn->thp/dot_general | solution.py:90
  84.7 0.0 copy-start.1
  84.7 0.3 copy.49
  85.1 0.7 copy-done.1
  85.8 0.4 multiply_reduce_fusion
  86.2 9.4 %all_to_all.27 = f32[4,1,256]{2,1,0:T(1,128)S(1)} all-to-all(f32[4,1,256]{2,1,0:T(1,128)S(1)} %broadcast_in_dim.96), channel_id=1, replica_groups=mesh['row'=8,'seg'=16,'head'=4] {'head'}, dimensions={0} | all-to-all | bytes 8192 | tf_op jit(solution)/shard_map/all_to_all | solution.py:97
  95.6 0.0 copy-done.6
  95.6 1.2 %multiply_convert_fusion.5 = bf16[256,1024]{1,0:T(8,128)(2,1)} fusion(f32[1024]{0:T(1024)S(1)} %copy-done.6, f32[256]{0:T(256)S(1)} %bitcast.50, f32[256,1024]{1,0:T(8,128)S(1)} %copy.49, bf16[256,1024]{1,0:T(8,128)(2,1)S(1)} %copy-done.1), kind=kLoop, calls=%fused_computation.21 | loop fusion | flops 2359296 | bytes 2102272 | tf_op jit(solution)/shard_map/convert_element_type | solution.py:102
  (18 shorter events, 0.2 us)
Async XLA Ops:
  0.0 4.0 %copy-start = (f32[256,16]{0,1:T(8,128)S(1)}, f32[256,16]{0,1:T(8,128)}, u32[]{:S(2)}) copy-start(f32[256,16]{0,1:T(8,128)} %param.14) | copy-start | bytes 49156
  0.0 5.2 %copy-start.4 = (s32[256]{0:T(256)S(1)}, s32[256]{0:T(256)}, u32[]{:S(2)}) copy-start(s32[256]{0:T(256)} %param.15) | copy-start | bytes 3076
  0.0 2.0 %copy-start.2 = (bf16[256,256]{1,0:T(8,128)(2,1)S(1)}, bf16[256,256]{1,0:T(8,128)(2,1)}, u32[]{:S(2)}) copy-start(bf16[256,256]{1,0:T(8,128)(2,1)} %param.11) | copy-start | bytes 393220
  0.0 4.8 %copy-start.5 = (f32[4,1024]{1,0:T(4,128)S(1)}, f32[4,1024]{1,0:T(4,128)}, u32[]{:S(2)}) copy-start(f32[4,1024]{1,0:T(4,128)} %param.16) | copy-start | bytes 49156
  0.0 4.8 %copy-start.7 = (f32[4,256]{1,0:T(4,128)S(1)}, f32[4,256]{1,0:T(4,128)}, u32[]{:S(2)}) copy-start(f32[4,256]{1,0:T(4,128)} %param.17) | copy-start | bytes 12292
  2.1 11.6 %collective-permute-start = (bf16[3,1281]{1,0:T(4,128)(2,1)S(1)}, bf16[3,1281]{1,0:T(4,128)(2,1)S(1)}, u32[]{:S(2)}, u32[]{:S(2)}) collective-permute-start(bf16[3,1281]{1,0:T(4,128)(2,1)S(1)} %pad_maximum_fusion.2), channel_id=1, source_target_pairs={{0,4},{4,8},{8,12},{12,16},{16,20},{20,24},{24,28},{28,32},{32,36}... | collective-permute-start | bytes 23066 | tf_op jit(solution)/shard_map/ppermute | solution.py:18
  18.8 0.7 copy-start.3
  21.3 33.6 %all-to-all-start = ((f32[128,1,1152]{2,1,0:T(1,128)}), f32[128,1,1152]{2,1,0:T(1,128)S(1)}, u32[]{:S(2)}, u32[]{:S(2)}) async-start(f32[128,1,1152]{2,1,0:T(1,128)} %all_to_all.18), calls=%async_computation | async-start | bytes 1179648 | tf_op jit(solution)/shard_map/all_to_all | solution.py:75
  60.0 21.3 %all-to-all-start.1 = ((bf16[128,2,512]{2,1,0:T(2,128)(2,1)}), bf16[128,2,512]{2,1,0:T(2,128)(2,1)S(1)}, u32[]{:S(2)}, u32[]{:S(2)}) async-start(bf16[128,2,512]{2,1,0:T(2,128)(2,1)} %reshape.199), calls=%async_computation.1 | async-start | bytes 524288 | tf_op jit(solution)/shard_map/all_to_all | solution.py:85
  69.1 14.1 %copy-start.8 = (f32[16]{0:T(128)S(1)}, f32[16]{0:T(128)}, u32[]{:S(2)}) copy-start(f32[16]{0:T(128)} %param.18) | copy-start | bytes 196
  84.7 1.0 %copy-start.1 = (bf16[256,1024]{1,0:T(8,128)(2,1)S(1)}, bf16[256,1024]{1,0:T(8,128)(2,1)}, u32[]{:S(2)}) copy-start(bf16[256,1024]{1,0:T(8,128)(2,1)} %param.12) | copy-start | bytes 1572868
  85.8 9.8 %copy-start.6 = (f32[1024]{0:T(1024)S(1)}, f32[1024]{0:T(1024)}, u32[]{:S(2)}) copy-start(f32[1024]{0:T(1024)} %param.19) | copy-start | bytes 12292

commit v4 on v2

--- a/solution.py
+++ b/solution.py
@@ -96,14 +96,11 @@
     scanned = inners + carried + skip[None, :, None] * xconv.astype(jnp.float32)
     gated_rows = scanned.reshape(GROUP, head_cols) * jax.nn.silu(gate_z.astype(jnp.float32))
     own = jnp.sum(gated_rows * gated_rows, axis=1)
-    width = lax.axis_size("head")
-    me = lax.axis_index("head")
-    parts = [own] + [
-        lax.ppermute(own, "head", [(i, (i + d) % width) for i in range(width)]) for d in range(1, width)
-    ]
-    squares = sum(
-        sum(jnp.where((me - d) % width == src, parts[d], 0.0) for d in range(width)) for src in range(width)
-    )
+    ways = lax.axis_size("head")
+    each = lax.all_to_all(jnp.broadcast_to(own[None], (ways, own.shape[0])), "head", 0, 0, tiled=True)
+    squares = each[0]
+    for src in range(1, ways):
+        squares = squares + each[src]
     scale = lax.rsqrt(squares / (head_cols * lax.axis_size("head")) + EPS)
     return (gated_rows * scale[:, None] * norm_gain[None, :]).astype(jnp.bfloat16)
 

time: 84.9 us -> 81.8 us (0.963)
  starting transfers between devices: 25.1 us -> 13.7 us
  blocking collectives: 0 us -> 9.39 us
  waiting for transfers between devices: 38.8 us -> 36.9 us
    ppermute x3 -> x0, starting transfers between devices: 11.4 us -> none  [body(): lax.ppermute(own, 'head', [(i, (i + d) % width) for i in range(width)])]
    all_to_all x0 -> x1, blocking collectives: none -> 9.39 us  [body(): lax.all_to_all(jnp.broadcast_to(own[None], (ways, own.shape[0])), 'head',...]
    ppermute x3 -> x0, waiting for transfers between devices: 2.08 us -> none  [body(): lax.ppermute(own, 'head', [(i, (i + d) % width) for i in range(width)])]
  transfers between devices with their start and end apart: 7 -> 4, of which waited for: 5 -> 4; matrix products, arithmetic and copies ran while one was open for 5% -> 5% of each run, Pallas kernels for 0% -> 0%
where the time goes in v4:
time: 81.8 us; the launch traced here: 81.2 us
  waiting for transfers between devices  36.9 us (45%)
  starting transfers between devices  13.7 us (17%)
  blocking collectives  9.39 us (11%)
  local copies, waits for them, and re-layouts  7.96 us (10%)
  other arithmetic  6.45 us (8%)
  matrix products  5.83 us (7%)
  between operations  1.01 us (1%)
    all_to_all x1, waiting for transfers between devices, body(): lax.all_to_all(payload, 'seg', 0, 0, tiled=True)  16 us
    ppermute x2, waiting for transfers between devices, shifted(): return lax.ppermute(block, axis, route)  12.3 us
    all_to_all x1, blocking collectives, body(): lax.all_to_all(jnp.broadcast_to(own[None], (ways, own.shape[0])), 'head',...  9.39 us
    all_to_all x1, waiting for transfers between devices, body(): lax.all_to_all(entering.astype(jnp.bfloat16), 'seg', 0, 0, tiled=True)  8.62 us
    all_to_all x1, starting transfers between devices, body(): lax.all_to_all(payload, 'seg', 0, 0, tiled=True)  4.97 us
    ppermute x2, starting transfers between devices, shifted(): return lax.ppermute(block, axis, route)  4.51 us
    all_to_all x1, starting transfers between devices, body(): lax.all_to_all(entering.astype(jnp.bfloat16), 'seg', 0, 0, tiled=True)  4.26 us
    unnamed x22, local copies, waits for them, and re-layouts  3.24 us
  transfers between devices with their start and end apart: 4, of which 4 were waited for; matrix products, arithmetic and copies ran while one was open for 5% of the time, Pallas kernels for 0%

profile of v4, /device:TPU:32, one launch (start us, length us, event | category | flops | bytes accessed | tf_op | source)
XLA Modules:
  0.0 81.2 jit_solution(8274071109000793031)
XLA Ops:
  0.0 0.0 copy-start
  0.0 0.0 copy-start.4
  0.0 0.0 copy-start.5
  0.0 0.0 copy-start.7
  0.0 0.7 broadcast_add_fusion
  0.8 0.1 slice_bitcast_fusion.4
  0.9 0.1 copy.50
  1.0 1.1 %constant_dynamic-update-slice_fusion.3 = bf16[256,1280]{1,0:T(8,128)(2,1)S(1)} fusion(bf16[256,1024]{1,0:T(8,128)(2,1)} %param.10), kind=kLoop, calls=%fused_computation.61 | loop fusion | bytes 1048576
  2.0 0.0 copy-done.2
  2.1 1.9 %collective-permute-start = (bf16[3,1281]{1,0:T(4,128)(2,1)S(1)}, bf16[3,1281]{1,0:T(4,128)(2,1)S(1)}, u32[]{:S(2)}, u32[]{:S(2)}) collective-permute-start(bf16[3,1281]{1,0:T(4,128)(2,1)S(1)} %pad_maximum_fusion.2), channel_id=1, source_target_pairs={{0,4},{4,8},{8,12},{12,16},{16,20},{20,24},{24,28},{28,32},{32,36}... | collective-permute-start | bytes 23066 | tf_op jit(solution)/shard_map/ppermute | solution.py:18
  4.0 0.0 copy-done
  4.1 0.6 reduce-window.6
  4.6 0.2 slice_reduce_fusion
  4.9 0.0 copy-done.5
  4.9 0.0 copy-done.7
  4.9 0.1 slice_reduce_fusion.7
  4.9 0.1 fusion.40
  5.0 0.2 slice_reduce_fusion.3
  5.2 0.0 copy-done.4
  5.2 0.6 slice.119
  5.8 8.0 %collective-permute-done = bf16[3,1281]{1,0:T(4,128)(2,1)S(1)} collective-permute-done((bf16[3,1281]{1,0:T(4,128)(2,1)S(1)}, bf16[3,1281]{1,0:T(4,128)(2,1)S(1)}, u32[]{:S(2)}, u32[]{:S(2)}) %collective-permute-start) | collective-permute-done | bytes 7718 | tf_op jit(solution)/shard_map/ppermute | solution.py:18
  13.8 0.6 slice.121
  14.3 0.1 fusion.37
  14.5 0.1 pad_add_fusion
  15.2 0.7 compare_convert_fusion.3
  16.0 0.6 slice.122
  16.5 0.6 exponential_multiply_fusion.1
  17.2 0.1 exponential_select_fusion
  17.3 1.2 %multiply_convert_fusion.4 = bf16[256,1280]{1,0:T(8,128)(2,1)S(1)} fusion(bf16[256,1280]{1,0:T(8,128)(2,1)S(1)} %constant_dynamic-update-slice_fusion.2, bf16[3,1280]{1,0:T(4,128)(2,1)S(1)} %slice.134, f32[256]{0:T(256)S(1)} %get-tuple-element.14, f32[1280]{0:T(1024)S(1)} %get-tuple-element.6, f32[256]{0:T(256)S(1)} %get-tuple-element.15, ...), kind=kLoop, calls=%fused_computation.13 | loop fusion | flops 9175040 | bytes 1341952 | tf_op jit(solution)/shard_map/convert_element_type | solution.py:45
  18.5 0.1 slice_convert_fusion
  18.7 0.0 copy-start.3
  18.7 0.3 copy.51
  19.0 0.4 copy-done.3
  19.4 0.3 fusion.15
  19.7 0.3 copy.80
  20.0 0.1 broadcast_in_dim.68
  20.1 1.2 %all_to_all.13 = f32[16,1,8320]{2,1,0:T(1,128)} reshape(f32[16,8320]{1,0:T(8,128)S(1)} %pad_maximum_fusion.1) | data formatting | bytes 1064960 | tf_op jit(solution)/shard_map/all_to_all | solution.py:71
  21.3 5.0 %all-to-all-start = ((f32[16,1,8320]{2,1,0:T(1,128)}), f32[16,1,8320]{2,1,0:T(1,128)S(1)}, u32[]{:S(2)}, u32[]{:S(2)}) async-start(f32[16,1,8320]{2,1,0:T(1,128)} %all_to_all.13), calls=%async_computation | async-start | bytes 1064960 | tf_op jit(solution)/shard_map/all_to_all | solution.py:71
  26.3 0.1 fusion.25
  26.4 16.0 %all-to-all-done = f32[16,1,8320]{2,1,0:T(1,128)S(1)} async-done(((f32[16,1,8320]{2,1,0:T(1,128)}), f32[16,1,8320]{2,1,0:T(1,128)S(1)}, u32[]{:S(2)}, u32[]{:S(2)}) %all-to-all-start) | async-done | bytes 532512 | tf_op jit(solution)/shard_map/all_to_all | solution.py:71
  42.4 0.2 slice_reduce_fusion.2
  42.6 0.1 select_reduce_fusion
  42.7 0.2 slice_reduce_fusion.1
  42.9 0.1 slice.149
  43.0 0.7 fusion.18
  43.6 2.6 %collective-permute-start.1 = (f32[1,8192]{1,0:T(1,128)S(1)}, f32[1,8192]{1,0:T(1,128)S(1)}, u32[]{:S(2)}, u32[]{:S(2)}) collective-permute-start(f32[1,8192]{1,0:T(1,128)S(1)} %fusion.18), channel_id=1, source_target_pairs={{0,64},{64,128},{128,192},{192,256},{256,320},{320,384},{384,448},... | collective-permute-start | bytes 98312 | tf_op jit(solution)/shard_map/ppermute | solution.py:18
  46.2 0.1 select_reduce_fusion.1
  46.3 4.3 %collective-permute-done.1 = f32[1,8192]{1,0:T(1,128)S(1)} collective-permute-done((f32[1,8192]{1,0:T(1,128)S(1)}, f32[1,8192]{1,0:T(1,128)S(1)}, u32[]{:S(2)}, u32[]{:S(2)}) %collective-permute-start.1) | collective-permute-done | bytes 32800 | tf_op jit(solution)/shard_map/ppermute | solution.py:18
  50.6 0.8 %fusion.23 = bf16[2,8,64,128]{3,1,2,0:T(8,128)(2,1)S(1)} fusion(f32[8192]{0:T(1024)S(1)} %bitcast.77, f32[16]{0:T(128)S(1)} %select_reduce_fusion.1, f32[16,1,8192]{2,1,0:T(1,128)S(1)} %slice.149, f32[1,17,16]{1,2,0:T(8,128)S(1)} %bitcast_select_fusion), kind=kOutput, calls=%fused_computation.39 | convolution fusion | flops 25559040 | bytes 820352 | tf_op jit(solution)/shard_map/gij,gjf->gif/dot_general | solution.py:85
  51.5 0.8 copy.60
  52.2 4.3 %all-to-all-start.1 = ((bf16[16,1,64,128]{3,2,1,0:T(8,128)(2,1)}), bf16[16,1,64,128]{3,2,1,0:T(8,128)(2,1)S(1)}, u32[]{:S(2)}, u32[]{:S(2)}) async-start(bf16[16,1,64,128]{3,2,1,0:T(8,128)(2,1)} %bitcast.14), calls=%async_computation.1 | async-start | bytes 524288 | tf_op jit(solution)/shard_map/all_to_all | solution.py:88
  56.5 0.2 fusion.29
  56.7 0.0 copy-start.8
  56.7 2.3 %fusion.6 = f32[256,16,64]{0,2,1:T(8,128)} fusion(f32[256,256]{1,0:T(8,128)S(1)} %fusion.29, f32[16,256]{1,0:T(8,128)S(1)} %get-tuple-element.12, pred[256,256]{1,0:T(8,128)(4,1)S(1)} %fusion.25, f32[256,16,64]{0,2,1:T(8,128)S(1)} %bitcast.72, f32[256,16]{0,1:T(8,128)S(1)} %copy-done.3), kind=kOutput, calls=%fused_computation.7 | convolution fusion | flops 139984896 | bytes 2457600 | tf_op jit(solution)/shard_map/hts,shp->thp/dot_general | solution.py:59
  59.0 8.6 %all-to-all-done.1 = bf16[16,1,64,128]{3,2,1,0:T(8,128)(2,1)S(1)} async-done(((bf16[16,1,64,128]{3,2,1,0:T(8,128)(2,1)}), bf16[16,1,64,128]{3,2,1,0:T(8,128)(2,1)S(1)}, u32[]{:S(2)}, u32[]{:S(2)}) %all-to-all-start.1) | async-done | bytes 262176 | tf_op jit(solution)/shard_map/all_to_all | solution.py:88
  67.7 0.0 copy-done.8
  67.7 1.5 %fusion.8 = f32[256,16,64]{0,2,1:T(8,128)S(1)} fusion(f32[256,16,64]{0,2,1:T(8,128)} %fusion.6, f32[256,16,64]{0,2,1:T(8,128)S(1)} %bitcast.73, f32[16]{0:T(128)S(1)} %copy-done.8, f32[256,16]{0,1:T(8,128)S(1)} %get-tuple-element.10, bf16[16,1,64,128]{3,2,1,0:T(8,128)(2,1)S(1)} %all-to-all-done.1, bf16[256,1280]{1,0:T(8,128)(2,1)S(1)} %multiply_convert_fusion.4), kind=kOutput, calls=%fused_computation.10 | convolution fusion | flops 68157440 | bytes 3490304 | tf_op jit(solution)/shard_map/tn,hpn->thp/dot_general | solution.py:93
  69.2 0.0 copy-start.1
  69.2 0.3 copy.55
  69.6 0.7 copy-done.1
  70.3 0.4 multiply_reduce_fusion
  70.7 9.4 %all_to_all.20 = f32[4,1,256]{2,1,0:T(1,128)S(1)} all-to-all(f32[4,1,256]{2,1,0:T(1,128)S(1)} %broadcast_in_dim.113), channel_id=1, replica_groups=mesh['row'=8,'seg'=16,'head'=4] {'head'}, dimensions={0} | all-to-all | bytes 8192 | tf_op jit(solution)/shard_map/all_to_all | solution.py:100
  80.1 0.0 copy-done.6
  80.1 1.2 %multiply_convert_fusion.5 = bf16[256,1024]{1,0:T(8,128)(2,1)} fusion(f32[1024]{0:T(1024)S(1)} %copy-done.6, f32[256]{0:T(256)S(1)} %bitcast.78, f32[256,1024]{1,0:T(8,128)S(1)} %copy.55, bf16[256,1024]{1,0:T(8,128)(2,1)S(1)} %copy-done.1), kind=kLoop, calls=%fused_computation.18 | loop fusion | flops 2359296 | bytes 2102272 | tf_op jit(solution)/shard_map/convert_element_type | solution.py:105
  (18 shorter events, 0.2 us)
Async XLA Ops:
  0.0 4.0 %copy-start = (f32[256,16]{0,1:T(8,128)S(1)}, f32[256,16]{0,1:T(8,128)}, u32[]{:S(2)}) copy-start(f32[256,16]{0,1:T(8,128)} %param.14) | copy-start | bytes 49156
  0.0 5.2 %copy-start.4 = (s32[256]{0:T(256)S(1)}, s32[256]{0:T(256)}, u32[]{:S(2)}) copy-start(s32[256]{0:T(256)} %param.15) | copy-start | bytes 3076
  0.0 2.0 %copy-start.2 = (bf16[256,256]{1,0:T(8,128)(2,1)S(1)}, bf16[256,256]{1,0:T(8,128)(2,1)}, u32[]{:S(2)}) copy-start(bf16[256,256]{1,0:T(8,128)(2,1)} %param.11) | copy-start | bytes 393220
  0.0 4.8 %copy-start.5 = (f32[4,1024]{1,0:T(4,128)S(1)}, f32[4,1024]{1,0:T(4,128)}, u32[]{:S(2)}) copy-start(f32[4,1024]{1,0:T(4,128)} %param.16) | copy-start | bytes 49156
  0.0 4.8 %copy-start.7 = (f32[4,256]{1,0:T(4,128)S(1)}, f32[4,256]{1,0:T(4,128)}, u32[]{:S(2)}) copy-start(f32[4,256]{1,0:T(4,128)} %param.17) | copy-start | bytes 12292
  2.1 11.6 %collective-permute-start = (bf16[3,1281]{1,0:T(4,128)(2,1)S(1)}, bf16[3,1281]{1,0:T(4,128)(2,1)S(1)}, u32[]{:S(2)}, u32[]{:S(2)}) collective-permute-start(bf16[3,1281]{1,0:T(4,128)(2,1)S(1)} %pad_maximum_fusion.2), channel_id=1, source_target_pairs={{0,4},{4,8},{8,12},{12,16},{16,20},{20,24},{24,28},{28,32},{32,36}... | collective-permute-start | bytes 23066 | tf_op jit(solution)/shard_map/ppermute | solution.py:18
  18.7 0.7 copy-start.3
  21.3 21.1 %all-to-all-start = ((f32[16,1,8320]{2,1,0:T(1,128)}), f32[16,1,8320]{2,1,0:T(1,128)S(1)}, u32[]{:S(2)}, u32[]{:S(2)}) async-start(f32[16,1,8320]{2,1,0:T(1,128)} %all_to_all.13), calls=%async_computation | async-start | bytes 1064960 | tf_op jit(solution)/shard_map/all_to_all | solution.py:71
  43.6 7.0 %collective-permute-start.1 = (f32[1,8192]{1,0:T(1,128)S(1)}, f32[1,8192]{1,0:T(1,128)S(1)}, u32[]{:S(2)}, u32[]{:S(2)}) collective-permute-start(f32[1,8192]{1,0:T(1,128)S(1)} %fusion.18), channel_id=1, source_target_pairs={{0,64},{64,128},{128,192},{192,256},{256,320},{320,384},{384,448},... | collective-permute-start | bytes 98312 | tf_op jit(solution)/shard_map/ppermute | solution.py:18
  52.2 15.4 %all-to-all-start.1 = ((bf16[16,1,64,128]{3,2,1,0:T(8,128)(2,1)}), bf16[16,1,64,128]{3,2,1,0:T(8,128)(2,1)S(1)}, u32[]{:S(2)}, u32[]{:S(2)}) async-start(bf16[16,1,64,128]{3,2,1,0:T(8,128)(2,1)} %bitcast.14), calls=%async_computation.1 | async-start | bytes 524288 | tf_op jit(solution)/shard_map/all_to_all | solution.py:88
  56.7 11.0 %copy-start.8 = (f32[16]{0:T(128)S(1)}, f32[16]{0:T(128)}, u32[]{:S(2)}) copy-start(f32[16]{0:T(128)} %param.18) | copy-start | bytes 196
  69.2 1.0 %copy-start.1 = (bf16[256,1024]{1,0:T(8,128)(2,1)S(1)}, bf16[256,1024]{1,0:T(8,128)(2,1)}, u32[]{:S(2)}) copy-start(bf16[256,1024]{1,0:T(8,128)(2,1)} %param.12) | copy-start | bytes 1572868
  70.3 9.8 %copy-start.6 = (f32[1024]{0:T(1024)S(1)}, f32[1024]{0:T(1024)}, u32[]{:S(2)}) copy-start(f32[1024]{0:T(1024)} %param.19) | copy-start | bytes 12292

commit v5 on v4

--- a/solution.py
+++ b/solution.py
@@ -25,30 +25,32 @@
     states = bc_raw.shape[1] // 2
     taps = conv_x.shape[0]
     seg = lax.axis_size("seg")
-    per_owner = heads_dev // seg
-    raw_all = jnp.concatenate([x_raw, bc_raw], axis=1)
-    labels = doc_ids + 1
+    halo = taps - 1
     edge = jnp.concatenate(
-        [raw_all[rows_dev - (taps - 1) :], labels[rows_dev - (taps - 1) :, None].astype(jnp.bfloat16)], axis=1
+        [x_raw[rows_dev - halo :], bc_raw[rows_dev - halo :], doc_ids[rows_dev - halo :, None].astype(jnp.bfloat16)],
+        axis=1,
     )
     edge = shifted(edge, SEQ, 1)
-    edge_rows = edge[:, : raw_all.shape[1]]
-    edge_docs = edge[:, raw_all.shape[1]].astype(jnp.int32)
-    extended = jnp.concatenate([edge_rows, raw_all], axis=0)
-    ext_docs = jnp.concatenate([edge_docs, labels], axis=0)
-    kernel = jnp.concatenate([conv_x, conv_bc], axis=1)
-    total = jnp.zeros(raw_all.shape, jnp.float32)
-    for k in range(taps):
-        moved = extended[taps - 1 - k : taps - 1 - k + rows_dev].astype(jnp.float32)
-        keep = (ext_docs[taps - 1 - k : taps - 1 - k + rows_dev] == labels).astype(jnp.float32)
-        total = total + kernel[k][None, :] * moved * keep[:, None]
-    activated = jax.nn.silu(total).astype(jnp.bfloat16)
-    xconv = activated[:, :head_cols].reshape(rows_dev, heads_dev, head_size)
-    bconv = activated[:, head_cols : head_cols + states]
-    cconv = activated[:, head_cols + states :]
+    edge_docs = edge[:, head_cols + 2 * states].astype(jnp.int32)
+    ext_docs = jnp.concatenate([edge_docs, doc_ids], axis=0)
+    keeps = [(ext_docs[halo - k : halo - k + rows_dev] == doc_ids).astype(jnp.float32) for k in range(taps)]
+
+    def conv(raw, edge_rows, taps_w):
+        extended = jnp.concatenate([edge_rows, raw], axis=0)
+        total = jnp.zeros(raw.shape, jnp.float32)
+        for k in range(taps):
+            moved = extended[halo - k : halo - k + rows_dev].astype(jnp.float32)
+            total = total + taps_w[k][None, :] * moved * keeps[k][:, None]
+        return jax.nn.silu(total).astype(jnp.bfloat16)
+
+    xflat = conv(x_raw, edge[:, :head_cols], conv_x)
+    bcconv = conv(bc_raw, edge[:, head_cols : head_cols + 2 * states], conv_bc)
+    xconv = xflat.reshape(rows_dev, heads_dev, head_size)
+    bconv = bcconv[:, :states]
+    cconv = bcconv[:, states:]
     xdt = (xconv.astype(jnp.float32) * step_size[:, :, None]).astype(jnp.bfloat16)
     lower = jnp.arange(GROUP)[:, None] >= jnp.arange(GROUP)[None, :]
-    previous = edge_docs[taps - 2] - 1
+    previous = edge_docs[halo - 1]
     cum = jnp.cumsum(log_decay, axis=0)
     gram = jnp.dot(cconv, bconv.T, preferred_element_type=jnp.float32)
     mask = ((doc_ids[:, None] == doc_ids[None, :]) & lower)[None]
@@ -68,25 +70,20 @@
     payload = jnp.concatenate(
         [local.reshape(heads_dev, flat), jnp.broadcast_to(through[:, None], (heads_dev, 128))], axis=1
     )
-    got = lax.all_to_all(payload, "seg", 0, 0, tiled=True).reshape(seg, per_owner, flat + 128)
-    pieces = jnp.transpose(got[:, :, :flat], (1, 0, 2))
-    decays = got[:, :, flat].T
+    got = lax.all_to_all(payload, "seg", 0, 0, tiled=True)
+    pieces = got[:, :flat]
+    decays = got[:, flat]
     after = jnp.arange(seg + 1)[:, None, None]
     source = jnp.arange(seg)[None, :, None]
-    between = (source < jnp.arange(seg)[None, None, :]) & (jnp.arange(seg)[None, None, :] < after)
-    spans = jnp.prod(jnp.where(between[None], decays[:, None, None, :], 1.0), axis=3)
-    weights_to = jnp.where((source[..., 0] < after[..., 0])[None], spans, 0.0)
-    head_first = jnp.prod(
-        jnp.where(jnp.arange(seg)[None, :] < jnp.arange(seg)[:, None], decays[:, None, :], 1.0), axis=2
-    )
+    middle = jnp.arange(seg)[None, None, :]
+    spans = jnp.prod(jnp.where((source < middle) & (middle < after), decays[None, None, :], 1.0), axis=2)
+    weights_to = jnp.where(source[..., 0] < after[..., 0], spans, 0.0)
     exact = lax.Precision.HIGHEST
-    total_row = jnp.einsum("gj,gjf->gf", weights_to[:, seg], pieces, precision=exact)
-    carry = shifted(total_row, "row", 1)
-    folds = jnp.einsum("gij,gjf->gif", weights_to[:, :seg], pieces, precision=exact)
-    entering = head_first[:, :, None] * carry[:, None, :] + folds
-    entering = jnp.transpose(entering, (1, 0, 2)).reshape(seg, per_owner, head_size, states)
-    entered = lax.all_to_all(entering.astype(jnp.bfloat16), "seg", 0, 0, tiled=True).reshape(
-        heads_dev, head_size, states
+    carry = shifted(jnp.dot(weights_to[seg], pieces, precision=exact), "row", 1)
+    head_first = jnp.prod(jnp.where(middle[0] < after[:seg, :, 0], decays[None, :], 1.0), axis=1)
+    entering = head_first[:, None] * carry[None, :] + jnp.dot(weights_to[:seg], pieces, precision=exact)
+    entered = lax.all_to_all(
+        entering.astype(jnp.bfloat16).reshape(seg, head_size, states), "seg", 0, 0, tiled=True
     )
 
     carried = (

time: 81.8 us -> 86.2 us (1.054)
  other arithmetic: 6.45 us -> 11 us
  local copies, waits for them, and re-layouts: 7.96 us -> 10.7 us
  matrix products: 5.83 us -> 3.8 us
  waiting for transfers between devices: 36.9 us -> 35.5 us
  starting transfers between devices: 13.7 us -> 14.7 us
    slice x8 -> x10, local copies, waits for them, and re-layouts: 1.26 us -> 4.2 us  [the longest x2 1.73 us: conv(): total = total + taps_w[k][None, :] * moved * keeps[k][:, None]]
    convert_element_type x1, other arithmetic: 0.11 us -> 3.02 us  [body(): xconv.astype(jnp.float32) * step_size[:, :, None]]
    ppermute x2, waiting for transfers between devices: 12.3 us -> 9.88 us  [shifted(): return lax.ppermute(block, axis, route)]
    dot_general x1, matrix products: 2.32 us -> 1.27 us  [body(): jnp.einsum('hts,shp->thp', weights, xdt, preferred_element_type=jnp.float32)]
    all_to_all x2, waiting for transfers between devices: 24.6 us -> 25.6 us  [the longest x1 15.9 us: body(): got = lax.all_to_all(payload, 'seg', 0, 0, tiled=True)]
    all_to_all x2, starting transfers between devices: 9.23 us -> 10.2 us  [the longest x1 5.95 us: body(): got = lax.all_to_all(payload, 'seg', 0, 0, tiled=True)]
    unnamed x22 -> x15, local copies, waits for them, and re-layouts: 3.24 us -> 2.35 us
  transfers between devices with their start and end apart: 4 -> 4, of which waited for: 4 -> 4; matrix products, arithmetic and copies ran while one was open for 5% -> 7% of each run, Pallas kernels for 0% -> 0%
where the time goes in v5:
time: 86.2 us; the launch traced here: 85.4 us
  waiting for transfers between devices  35.5 us (41%)
  starting transfers between devices  14.7 us (17%)
  other arithmetic  11 us (13%)
  local copies, waits for them, and re-layouts  10.7 us (12%)
  blocking collectives  9.4 us (11%)
  matrix products  3.8 us (4%)
    all_to_all x1, waiting for transfers between devices, body(): got = lax.all_to_all(payload, 'seg', 0, 0, tiled=True)  15.9 us
    ppermute x2, waiting for transfers between devices, shifted(): return lax.ppermute(block, axis, route)  9.88 us
    all_to_all x1, waiting for transfers between devices, body(): lax.all_to_all(entering.astype(jnp.bfloat16).reshape(seg, head_size, stat...  9.67 us
    all_to_all x1, blocking collectives, body(): lax.all_to_all(jnp.broadcast_to(own[None], (ways, own.shape[0])), 'head',...  9.4 us
    all_to_all x1, starting transfers between devices, body(): got = lax.all_to_all(payload, 'seg', 0, 0, tiled=True)  5.95 us
    ppermute x2, starting transfers between devices, shifted(): return lax.ppermute(block, axis, route)  4.51 us
    all_to_all x1, starting transfers between devices, body(): lax.all_to_all(entering.astype(jnp.bfloat16).reshape(seg, head_size, stat...  4.26 us
    convert_element_type x1, other arithmetic, body(): xconv.astype(jnp.float32) * step_size[:, :, None]  3.02 us
  transfers between devices with their start and end apart: 4, of which 4 were waited for; matrix products, arithmetic and copies ran while one was open for 7% of the time, Pallas kernels for 0%

profile of v5, /device:TPU:32, one launch (start us, length us, event | category | flops | bytes accessed | tf_op | source)
XLA Modules:
  0.0 85.4 jit_solution(7667262054247362043)
XLA Ops:
  0.0 0.0 copy-start
  0.0 0.7 convert.4
  0.7 0.1 slice_bitcast_fusion.1
  0.8 0.1 copy.47
  0.9 0.7 slice.130
  1.6 0.7 slice.129
  2.3 1.9 %collective-permute-start = (bf16[3,1281]{1,0:T(4,128)(2,1)S(1)}, bf16[3,1281]{1,0:T(4,128)(2,1)S(1)}, u32[]{:S(2)}, u32[]{:S(2)}) collective-permute-start(bf16[3,1281]{1,0:T(4,128)(2,1)S(1)} %pad_maximum_fusion.3), channel_id=1, source_target_pairs={{0,4},{4,8},{8,12},{12,16},{16,20},{20,24},{24,28},{28,32},{32,36}... | collective-permute-start | bytes 23066 | tf_op jit(solution)/shard_map/ppermute | solution.py:18
  4.2 0.8 fusion.44
  5.1 0.0 copy-done
  5.1 0.6 reduce-window.6
  5.7 0.2 slice_reduce_fusion
  5.9 0.9 %fusion.43 = (f32[1,1024]{1,0:T(1,128)S(1)}, f32[1,1024]{1,0:T(1,128)S(1)}, f32[1,1024]{1,0:T(1,128)S(1)}, f32[1,1024]{1,0:T(1,128)S(1)}) fusion(f32[4,1024]{1,0:T(4,128)} %param.16), kind=kLoop, calls=%fused_computation.90 | loop fusion | bytes 32768 | tf_op jit(solution)/shard_map/slice | solution.py:43
  6.8 0.1 fusion.42
  6.9 0.2 slice_reduce_fusion.3
  7.0 1.3 %slice.155 = s32[1]{0:T(128)} slice(s32[256]{0:T(256)} %param.15), slice={[255:256]} | slice | bytes 8 | tf_op jit(solution)/shard_map/slice | solution.py:64
  8.3 5.6 %collective-permute-done = bf16[3,1281]{1,0:T(4,128)(2,1)S(1)} collective-permute-done((bf16[3,1281]{1,0:T(4,128)(2,1)S(1)}, bf16[3,1281]{1,0:T(4,128)(2,1)S(1)}, u32[]{:S(2)}, u32[]{:S(2)}) %collective-permute-start) | collective-permute-done | bytes 7718 | tf_op jit(solution)/shard_map/ppermute | solution.py:18
  13.9 0.1 fusion.40
  14.1 0.8 pad_add_fusion
  14.8 0.6 slice.157
  15.4 2.1 %compare_convert_fusion.3 = (f32[256]{0:T(256)S(1)}, f32[256]{0:T(256)S(1)}, f32[256]{0:T(256)S(1)}, pred[256]{0:T(512)(128)(4,1)S(1)}, f32[256]{0:T(256)S(1)}) fusion(s32[256]{0:T(256)} %param.15, s32[259]{0:T(512)S(1)} %pad_add_fusion, s32[]{:T(128)} %bitcast.14, s32[]{:T(128)} %bitcast.17), kind=kLoop, calls=%fused_computation.75 | loop fusion | flops 2304 | bytes 8456 | tf_op jit(solution)/shard_map/convert_element_type | solution.py:36
  17.5 0.6 slice.158
  18.1 0.6 exponential_multiply_fusion.1
  18.7 0.7 exponential_multiply_fusion
  19.4 3.0 %fusion.17 = f32[256,1024]{1,0:T(8,128)S(1)} fusion(f32[256]{0:T(256)S(1)} %get-tuple-element.18, bf16[256,1024]{1,0:T(8,128)(2,1)} %param.10, bf16[3,1024]{1,0:T(4,128)(2,1)S(1)} %slice.167, f32[1024]{0:T(1024)S(1)} %bitcast.75, f32[256]{0:T(256)S(1)} %get-tuple-element.19, f32[1024]{0:T(1024)S(1)} %bitcast.76, f32[256]{0:T(256)S(1)} %get-tuple-element.17, ...), kind=kLoop, calls=%fused_computation.33 | loop fusion | flops 7602176 | bytes 1598464 | tf_op jit(solution)/shard_map/convert_element_type | solution.py:51
  22.5 0.0 copy-start.2
  22.5 0.0 copy-start.3
  22.5 0.3 copy.48
  22.8 0.5 copy-done.2
  23.4 0.2 multiply_convert_fusion.9
  23.6 0.0 copy-done.3
  23.6 0.3 fusion.15
  23.9 0.3 copy.68
  24.2 0.1 broadcast_in_dim.66
  24.3 0.0 copy-start.4
  24.4 1.2 %all_to_all.15 = f32[16,1,8320]{2,1,0:T(1,128)} reshape(f32[16,8320]{1,0:T(8,128)S(1)} %pad_maximum_fusion) | data formatting | bytes 1064960 | tf_op jit(solution)/shard_map/all_to_all | solution.py:73
  25.5 6.0 %all-to-all-start = ((f32[16,1,8320]{2,1,0:T(1,128)}), f32[16,1,8320]{2,1,0:T(1,128)S(1)}, u32[]{:S(2)}, u32[]{:S(2)}) async-start(f32[16,1,8320]{2,1,0:T(1,128)} %all_to_all.15), calls=%async_computation | async-start | bytes 1064960 | tf_op jit(solution)/shard_map/all_to_all | solution.py:73
  31.5 0.0 copy-done.4
  31.5 0.1 fusion.23
  31.6 15.9 %all-to-all-done = f32[16,1,8320]{2,1,0:T(1,128)S(1)} async-done(((f32[16,1,8320]{2,1,0:T(1,128)}), f32[16,1,8320]{2,1,0:T(1,128)S(1)}, u32[]{:S(2)}, u32[]{:S(2)}) %all-to-all-start) | async-done | bytes 532512 | tf_op jit(solution)/shard_map/all_to_all | solution.py:73
  47.6 0.1 slice_reduce_fusion.2
  47.7 0.1 select_reduce_fusion
  47.9 0.2 slice_reduce_fusion.1
  48.1 0.4 fusion.20
  48.5 2.6 %collective-permute-start.1 = (f32[8192]{0:T(1024)S(1)}, f32[8192]{0:T(1024)S(1)}, u32[]{:S(2)}, u32[]{:S(2)}) collective-permute-start(f32[8192]{0:T(1024)S(1)} %bitcast.72), channel_id=1, source_target_pairs={{0,64},{64,128},{128,192},{192,256},{256,320},{320,384},{384,448},... | collective-permute-start | bytes 98312 | tf_op jit(solution)/shard_map/ppermute | solution.py:18
  51.0 0.2 select_reduce_fusion.1
  51.2 4.2 %collective-permute-done.1 = f32[8192]{0:T(1024)S(1)} collective-permute-done((f32[8192]{0:T(1024)S(1)}, f32[8192]{0:T(1024)S(1)}, u32[]{:S(2)}, u32[]{:S(2)}) %collective-permute-start.1) | collective-permute-done | bytes 32800 | tf_op jit(solution)/shard_map/ppermute | solution.py:18
  55.5 0.6 fusion.22
  56.1 0.8 copy.56
  56.9 4.3 %all-to-all-start.1 = ((bf16[16,64,128]{2,1,0:T(8,128)(2,1)}), bf16[16,64,128]{2,1,0:T(8,128)(2,1)S(1)}, u32[]{:S(2)}, u32[]{:S(2)}) async-start(bf16[16,64,128]{2,1,0:T(8,128)(2,1)} %bitcast.31), calls=%async_computation.1 | async-start | bytes 524288 | tf_op jit(solution)/shard_map/all_to_all | solution.py:85
  61.1 0.2 fusion.29
  61.3 1.3 %fusion.6 = f32[256,16,64]{0,2,1:T(8,128)S(1)} fusion(f32[256,256]{1,0:T(8,128)S(1)} %fusion.29, f32[16,256]{1,0:T(8,128)S(1)} %get-tuple-element.8, pred[256,256]{1,0:T(8,128)(4,1)S(1)} %fusion.23, f32[256,16,64]{0,2,1:T(8,128)S(1)} %bitcast.64, f32[256,16]{0,1:T(8,128)S(1)} %copy-done.3), kind=kOutput, calls=%fused_computation.7 | convolution fusion | flops 139984896 | bytes 2457600 | tf_op jit(solution)/shard_map/hts,shp->thp/dot_general | solution.py:61
  62.6 9.7 %all-to-all-done.1 = bf16[16,64,128]{2,1,0:T(8,128)(2,1)S(1)} async-done(((bf16[16,64,128]{2,1,0:T(8,128)(2,1)}), bf16[16,64,128]{2,1,0:T(8,128)(2,1)S(1)}, u32[]{:S(2)}, u32[]{:S(2)}) %all-to-all-start.1) | async-done | bytes 262176 | tf_op jit(solution)/shard_map/all_to_all | solution.py:85
  72.3 1.0 %fusion.8 = f32[256,16,64]{0,2,1:T(8,128)S(1)} fusion(f32[256,16,64]{0,2,1:T(8,128)S(1)} %fusion.6, bf16[16,64,128]{2,1,0:T(8,128)(2,1)S(1)} %all-to-all-done.1, f32[256,16,64]{0,2,1:T(8,128)S(1)} %bitcast.65, f32[16]{0:T(128)} %param.18, f32[256,16]{0,1:T(8,128)} %get-tuple-element.5, bf16[256,256]{1,0:T(8,128)(2,1)S(1)} %multiply_convert_fusion.9), kind=kOutput, calls=%fused_computation.10 | convolution fusion | flops 68157440 | bytes 3489856 | tf_op jit(solution)/shard_map/tn,hpn->thp/dot_general | solution.py:90
  73.3 0.0 copy-start.1
  73.3 0.3 copy.51
  73.7 0.7 copy-done.1
  74.4 0.0 copy-start.5
  74.4 0.4 multiply_reduce_fusion
  74.8 9.4 %all_to_all.23 = f32[4,1,256]{2,1,0:T(1,128)S(1)} all-to-all(f32[4,1,256]{2,1,0:T(1,128)S(1)} %broadcast_in_dim.109), channel_id=1, replica_groups=mesh['row'=8,'seg'=16,'head'=4] {'head'}, dimensions={0} | all-to-all | bytes 8192 | tf_op jit(solution)/shard_map/all_to_all | solution.py:97
  84.2 0.0 copy-done.5
  84.2 1.2 %multiply_convert_fusion.4 = bf16[256,1024]{1,0:T(8,128)(2,1)} fusion(f32[1024]{0:T(1024)S(1)} %copy-done.5, f32[256]{0:T(256)S(1)} %bitcast.77, f32[256,1024]{1,0:T(8,128)S(1)} %copy.51, bf16[256,1024]{1,0:T(8,128)(2,1)S(1)} %copy-done.1), kind=kLoop, calls=%fused_computation.17 | loop fusion | flops 2359296 | bytes 2102272 | tf_op jit(solution)/shard_map/convert_element_type | solution.py:102
  (16 shorter events, 0.2 us)
Async XLA Ops:
  0.0 5.1 %copy-start = (f32[256,16]{0,1:T(8,128)S(1)}, f32[256,16]{0,1:T(8,128)}, u32[]{:S(2)}) copy-start(f32[256,16]{0,1:T(8,128)} %param.14) | copy-start | bytes 49156
  2.3 11.6 %collective-permute-start = (bf16[3,1281]{1,0:T(4,128)(2,1)S(1)}, bf16[3,1281]{1,0:T(4,128)(2,1)S(1)}, u32[]{:S(2)}, u32[]{:S(2)}) collective-permute-start(bf16[3,1281]{1,0:T(4,128)(2,1)S(1)} %pad_maximum_fusion.3), channel_id=1, source_target_pairs={{0,4},{4,8},{8,12},{12,16},{16,20},{20,24},{24,28},{28,32},{32,36}... | collective-permute-start | bytes 23066 | tf_op jit(solution)/shard_map/ppermute | solution.py:18
  22.5 0.9 %copy-start.2 = (bf16[256,256]{1,0:T(8,128)(2,1)S(1)}, bf16[256,256]{1,0:T(8,128)(2,1)}, u32[]{:S(2)}) copy-start(bf16[256,256]{1,0:T(8,128)(2,1)} %param.11) | copy-start | bytes 393220
  22.5 1.1 %copy-start.3 = (f32[256,16]{0,1:T(8,128)S(1)}, f32[256,16]{0,1:T(8,128)}, u32[]{:S(2)}) copy-start(f32[256,16]{0,1:T(8,128)} %param.13) | copy-start | bytes 49156
  24.3 7.2 %copy-start.4 = (s32[256]{0:T(256)S(1)}, s32[256]{0:T(256)}, u32[]{:S(2)}) copy-start(s32[256]{0:T(256)} %param.15) | copy-start | bytes 3076
  25.5 22.1 %all-to-all-start = ((f32[16,1,8320]{2,1,0:T(1,128)}), f32[16,1,8320]{2,1,0:T(1,128)S(1)}, u32[]{:S(2)}, u32[]{:S(2)}) async-start(f32[16,1,8320]{2,1,0:T(1,128)} %all_to_all.15), calls=%async_computation | async-start | bytes 1064960 | tf_op jit(solution)/shard_map/all_to_all | solution.py:73
  48.5 7.0 %collective-permute-start.1 = (f32[8192]{0:T(1024)S(1)}, f32[8192]{0:T(1024)S(1)}, u32[]{:S(2)}, u32[]{:S(2)}) collective-permute-start(f32[8192]{0:T(1024)S(1)} %bitcast.72), channel_id=1, source_target_pairs={{0,64},{64,128},{128,192},{192,256},{256,320},{320,384},{384,448},... | collective-permute-start | bytes 98312 | tf_op jit(solution)/shard_map/ppermute | solution.py:18
  56.9 15.4 %all-to-all-start.1 = ((bf16[16,64,128]{2,1,0:T(8,128)(2,1)}), bf16[16,64,128]{2,1,0:T(8,128)(2,1)S(1)}, u32[]{:S(2)}, u32[]{:S(2)}) async-start(bf16[16,64,128]{2,1,0:T(8,128)(2,1)} %bitcast.31), calls=%async_computation.1 | async-start | bytes 524288 | tf_op jit(solution)/shard_map/all_to_all | solution.py:85
  73.3 1.0 %copy-start.1 = (bf16[256,1024]{1,0:T(8,128)(2,1)S(1)}, bf16[256,1024]{1,0:T(8,128)(2,1)}, u32[]{:S(2)}) copy-start(bf16[256,1024]{1,0:T(8,128)(2,1)} %param.12) | copy-start | bytes 1572868
  74.4 9.8 %copy-start.5 = (f32[1024]{0:T(1024)S(1)}, f32[1024]{0:T(1024)}, u32[]{:S(2)}) copy-start(f32[1024]{0:T(1024)} %param.19) | copy-start | bytes 12292

commit v6 on v4

--- a/solution.py
+++ b/solution.py
@@ -93,8 +93,11 @@
         jnp.einsum("tn,hpn->thp", cconv, entered, preferred_element_type=jnp.float32)
         * entries[:, :, None]
     )
-    scanned = inners + carried + skip[None, :, None] * xconv.astype(jnp.float32)
-    gated_rows = scanned.reshape(GROUP, head_cols) * jax.nn.silu(gate_z.astype(jnp.float32))
+    skipped, gate = lax.optimization_barrier(
+        (skip[None, :, None] * xconv.astype(jnp.float32), jax.nn.silu(gate_z.astype(jnp.float32)))
+    )
+    scanned = inners + carried + skipped
+    gated_rows = scanned.reshape(GROUP, head_cols) * gate
     own = jnp.sum(gated_rows * gated_rows, axis=1)
     ways = lax.axis_size("head")
     each = lax.all_to_all(jnp.broadcast_to(own[None], (ways, own.shape[0])), "head", 0, 0, tiled=True)

time: 81.8 us -> 82.7 us (1.011)
  waiting for transfers between devices: 36.9 us -> 35.3 us
  local copies, waits for them, and re-layouts: 7.96 us -> 9.27 us
  matrix products: 5.83 us -> 6.75 us
    slice x1, local copies, waits for them, and re-layouts: 0.05 us -> 1.08 us  [body(): pieces = jnp.transpose(got[:, :, :flat], (1, 0, 2))]
    all_to_all x1, waiting for transfers between devices: 8.62 us -> 7.74 us  [body(): lax.all_to_all(entering.astype(jnp.bfloat16), 'seg', 0, 0, tiled=True)]
    dot_general x1, matrix products: 0.18 us -> 1.06 us  [body(): gram = jnp.dot(cconv, bconv.T, preferred_element_type=jnp.float32)]
    unnamed x22 -> x24, local copies, waits for them, and re-layouts: 3.24 us -> 2.81 us
  transfers between devices with their start and end apart: 4 -> 4, of which waited for: 4 -> 4; matrix products, arithmetic and copies ran while one was open for 5% -> 7% of each run, Pallas kernels for 0% -> 0%
where the time goes in v6:
time: 82.7 us; the launch traced here: 82 us
  waiting for transfers between devices  35.3 us (43%)
  starting transfers between devices  13.8 us (17%)
  blocking collectives  9.38 us (11%)
  local copies, waits for them, and re-layouts  9.27 us (11%)
  matrix products  6.75 us (8%)
  other arithmetic  6.44 us (8%)
  between operations  1.05 us (1%)
    all_to_all x1, waiting for transfers between devices, body(): lax.all_to_all(payload, 'seg', 0, 0, tiled=True)  15.4 us
    ppermute x2, waiting for transfers between devices, shifted(): return lax.ppermute(block, axis, route)  12.2 us
    all_to_all x1, blocking collectives, body(): lax.all_to_all(jnp.broadcast_to(own[None], (ways, own.shape[0])), 'head',...  9.38 us
    all_to_all x1, waiting for transfers between devices, body(): lax.all_to_all(entering.astype(jnp.bfloat16), 'seg', 0, 0, tiled=True)  7.74 us
    all_to_all x1, starting transfers between devices, body(): lax.all_to_all(payload, 'seg', 0, 0, tiled=True)  5.01 us
    ppermute x2, starting transfers between devices, shifted(): return lax.ppermute(block, axis, route)  4.56 us
    all_to_all x1, starting transfers between devices, body(): lax.all_to_all(entering.astype(jnp.bfloat16), 'seg', 0, 0, tiled=True)  4.26 us
    unnamed x24, local copies, waits for them, and re-layouts  2.81 us
  transfers between devices with their start and end apart: 4, of which 4 were waited for; matrix products, arithmetic and copies ran while one was open for 7% of the time, Pallas kernels for 0%

profile of v6, /device:TPU:32, one launch (start us, length us, event | category | flops | bytes accessed | tf_op | source)
XLA Modules:
  0.0 82.0 jit_solution(7443664888383588375)
XLA Ops:
  0.0 0.0 copy-start
  0.0 0.0 copy-start.6
  0.0 0.0 copy-start.8
  0.0 0.7 broadcast_add_fusion
  0.8 0.1 slice_bitcast_fusion.4
  0.9 0.1 copy.50
  1.0 1.1 %constant_dynamic-update-slice_fusion.3 = bf16[256,1280]{1,0:T(8,128)(2,1)S(1)} fusion(bf16[256,1024]{1,0:T(8,128)(2,1)} %param.10), kind=kLoop, calls=%fused_computation.61 | loop fusion | bytes 1048576
  2.0 0.0 copy-done.3
  2.1 1.9 %collective-permute-start = (bf16[3,1281]{1,0:T(4,128)(2,1)S(1)}, bf16[3,1281]{1,0:T(4,128)(2,1)S(1)}, u32[]{:S(2)}, u32[]{:S(2)}) collective-permute-start(bf16[3,1281]{1,0:T(4,128)(2,1)S(1)} %pad_maximum_fusion.2), channel_id=1, source_target_pairs={{0,4},{4,8},{8,12},{12,16},{16,20},{20,24},{24,28},{28,32},{32,36}... | collective-permute-start | bytes 23066 | tf_op jit(solution)/shard_map/ppermute | solution.py:18
  4.0 0.0 copy-done
  4.1 0.6 reduce-window.6
  4.6 0.2 slice_reduce_fusion
  4.9 0.0 copy-done.6
  4.9 0.1 slice_reduce_fusion.7
  4.9 0.1 fusion.39
  5.0 0.2 slice_reduce_fusion.3
  5.2 0.6 slice.119
  5.8 8.0 %collective-permute-done = bf16[3,1281]{1,0:T(4,128)(2,1)S(1)} collective-permute-done((bf16[3,1281]{1,0:T(4,128)(2,1)S(1)}, bf16[3,1281]{1,0:T(4,128)(2,1)S(1)}, u32[]{:S(2)}, u32[]{:S(2)}) %collective-permute-start) | collective-permute-done | bytes 7718 | tf_op jit(solution)/shard_map/ppermute | solution.py:18
  13.8 0.6 slice.121
  14.3 0.1 fusion.36
  14.5 0.1 pad_add_fusion
  15.2 0.7 compare_convert_fusion.3
  16.0 0.6 slice.122
  16.5 0.6 exponential_multiply_fusion.1
  17.2 0.1 exponential_select_fusion
  17.3 1.2 %multiply_convert_fusion.4 = bf16[256,1280]{1,0:T(8,128)(2,1)S(1)} fusion(bf16[256,1280]{1,0:T(8,128)(2,1)S(1)} %constant_dynamic-update-slice_fusion.2, bf16[3,1280]{1,0:T(4,128)(2,1)S(1)} %slice.134, f32[256]{0:T(256)S(1)} %get-tuple-element.20, f32[1280]{0:T(1024)S(1)} %get-tuple-element.10, f32[256]{0:T(256)S(1)} %get-tuple-element.21, ...), kind=kLoop, calls=%fused_computation.13 | loop fusion | flops 9175040 | bytes 1341952 | tf_op jit(solution)/shard_map/convert_element_type | solution.py:45
  18.6 0.1 slice_convert_fusion
  18.7 0.0 copy-start.4
  18.7 0.3 copy.51
  19.0 0.4 copy-done.1
  19.4 0.1 copy-done.4
  19.4 0.3 fusion.14
  19.7 0.3 copy.80
  20.1 0.1 broadcast_in_dim.68
  20.2 0.0 copy-start.2
  20.2 1.2 %all_to_all.13 = f32[16,1,8320]{2,1,0:T(1,128)} reshape(f32[16,8320]{1,0:T(8,128)S(1)} %pad_maximum_fusion.1) | data formatting | bytes 1064960 | tf_op jit(solution)/shard_map/all_to_all | solution.py:71
  21.4 5.0 %all-to-all-start = ((f32[16,1,8320]{2,1,0:T(1,128)}), f32[16,1,8320]{2,1,0:T(1,128)}, u32[]{:S(2)}, u32[]{:S(2)}) async-start(f32[16,1,8320]{2,1,0:T(1,128)} %all_to_all.13), calls=%async_computation | async-start | bytes 1064960 | tf_op jit(solution)/shard_map/all_to_all | solution.py:71
  26.4 0.0 copy-start.9
  26.4 0.1 fusion.24
  26.5 0.3 convert_multiply_fusion
  26.8 0.2 copy-done.9
  27.0 0.1 broadcast_multiply_fusion
  27.2 15.4 %all-to-all-done = f32[16,1,8320]{2,1,0:T(1,128)} async-done(((f32[16,1,8320]{2,1,0:T(1,128)}), f32[16,1,8320]{2,1,0:T(1,128)}, u32[]{:S(2)}, u32[]{:S(2)}) %all-to-all-start) | async-done | bytes 532512 | tf_op jit(solution)/shard_map/all_to_all | solution.py:71
  42.5 0.9 %slice_reduce_fusion.2 = f32[16]{0:T(128)S(1)} fusion(f32[16,1,8320]{2,1,0:T(1,128)} %all-to-all-done), kind=kLoop, calls=%fused_computation.64 | loop fusion | bytes 128 | tf_op jit(solution)/shard_map/slice | solution.py:73
  43.4 0.1 select_reduce_fusion
  43.6 0.2 slice_reduce_fusion.1
  43.8 1.1 %slice.149 = f32[16,1,8192]{2,1,0:T(1,128)S(1)} slice(f32[16,1,8320]{2,1,0:T(1,128)} %all-to-all-done), slice={[0:16], [0:1], [0:8192]} | slice | bytes 1048576 | tf_op jit(solution)/shard_map/slice | solution.py:72
  44.9 0.6 fusion.17
  45.5 2.6 %collective-permute-start.1 = (f32[1,8192]{1,0:T(1,128)S(1)}, f32[1,8192]{1,0:T(1,128)S(1)}, u32[]{:S(2)}, u32[]{:S(2)}) collective-permute-start(f32[1,8192]{1,0:T(1,128)S(1)} %fusion.17), channel_id=1, source_target_pairs={{0,64},{64,128},{128,192},{192,256},{256,320},{320,384},{384,448},... | collective-permute-start | bytes 98312 | tf_op jit(solution)/shard_map/ppermute | solution.py:18
  48.2 0.1 select_reduce_fusion.1
  48.3 4.3 %collective-permute-done.1 = f32[1,8192]{1,0:T(1,128)S(1)} collective-permute-done((f32[1,8192]{1,0:T(1,128)S(1)}, f32[1,8192]{1,0:T(1,128)S(1)}, u32[]{:S(2)}, u32[]{:S(2)}) %collective-permute-start.1) | collective-permute-done | bytes 32800 | tf_op jit(solution)/shard_map/ppermute | solution.py:18
  52.5 0.8 %fusion.22 = bf16[2,8,64,128]{3,1,2,0:T(8,128)(2,1)S(1)} fusion(f32[8192]{0:T(1024)S(1)} %bitcast.77, f32[16]{0:T(128)S(1)} %select_reduce_fusion.1, f32[16,1,8192]{2,1,0:T(1,128)S(1)} %slice.149, f32[1,17,16]{1,2,0:T(8,128)S(1)} %bitcast_select_fusion), kind=kOutput, calls=%fused_computation.39 | convolution fusion | flops 25559040 | bytes 820352 | tf_op jit(solution)/shard_map/gij,gjf->gif/dot_general | solution.py:85
  53.4 0.8 copy.60
  54.1 4.3 %all-to-all-start.1 = ((bf16[16,1,64,128]{3,2,1,0:T(8,128)(2,1)}), bf16[16,1,64,128]{3,2,1,0:T(8,128)(2,1)S(1)}, u32[]{:S(2)}, u32[]{:S(2)}) async-start(bf16[16,1,64,128]{3,2,1,0:T(8,128)(2,1)} %bitcast.14), calls=%async_computation.1 | async-start | bytes 524288 | tf_op jit(solution)/shard_map/all_to_all | solution.py:88
  58.4 1.1 %fusion.28 = f32[256,256]{1,0:T(8,128)S(1)} fusion(bf16[256,1280]{1,0:T(8,128)(2,1)} %copy-done.1), kind=kOutput, calls=%fused_computation.47 | convolution fusion | flops 16777216 | bytes 393216 | tf_op jit(solution)/shard_map/dot_general | solution.py:53
  59.5 2.3 %fusion.6 = f32[256,16,64]{0,2,1:T(8,128)} fusion(f32[256,256]{1,0:T(8,128)S(1)} %fusion.28, f32[16,256]{1,0:T(8,128)S(1)} %get-tuple-element.18, pred[256,256]{1,0:T(8,128)(4,1)S(1)} %fusion.24, f32[256,16,64]{0,2,1:T(8,128)S(1)} %bitcast.73, f32[256,16]{0,1:T(8,128)S(1)} %copy-done.4), kind=kOutput, calls=%fused_computation.7 | convolution fusion | flops 139984896 | bytes 2457600 | tf_op jit(solution)/shard_map/hts,shp->thp/dot_general | solution.py:59
  61.8 7.7 %all-to-all-done.1 = bf16[16,1,64,128]{3,2,1,0:T(8,128)(2,1)S(1)} async-done(((bf16[16,1,64,128]{3,2,1,0:T(8,128)(2,1)}), bf16[16,1,64,128]{3,2,1,0:T(8,128)(2,1)S(1)}, u32[]{:S(2)}, u32[]{:S(2)}) %all-to-all-start.1) | async-done | bytes 262176 | tf_op jit(solution)/shard_map/all_to_all | solution.py:88
  69.6 1.6 %fusion.8 = f32[256,16,64]{0,2,1:T(8,128)S(1)} fusion(f32[256,16,64]{0,2,1:T(8,128)S(1)} %broadcast_multiply_fusion, f32[256,16,64]{0,2,1:T(8,128)} %fusion.6, f32[256,16]{0,1:T(8,128)S(1)} %get-tuple-element.16, bf16[16,1,64,128]{3,2,1,0:T(8,128)(2,1)S(1)} %all-to-all-done.1, bf16[256,1280]{1,0:T(8,128)(2,1)} %copy-done.1), kind=kOutput, calls=%fused_computation.10 | convolution fusion | flops 67895296 | bytes 3489792 | tf_op jit(solution)/shard_map/tn,hpn->thp/dot_general | solution.py:93
  71.1 0.3 copy.55
  71.5 0.0 copy-start.7
  71.5 0.2 multiply_reduce_fusion
  71.7 9.4 %all_to_all.20 = f32[4,1,256]{2,1,0:T(1,128)S(1)} all-to-all(f32[4,1,256]{2,1,0:T(1,128)S(1)} %broadcast_in_dim.113), channel_id=1, replica_groups=mesh['row'=8,'seg'=16,'head'=4] {'head'}, dimensions={0} | all-to-all | bytes 8192 | tf_op jit(solution)/shard_map/all_to_all | solution.py:103
  81.1 0.0 copy-done.7
  81.1 0.9 %multiply_convert_fusion.5 = bf16[256,1024]{1,0:T(8,128)(2,1)} fusion(f32[256,1024]{1,0:T(8,128)S(1)} %get-tuple-element.14, f32[1024]{0:T(1024)S(1)} %copy-done.7, f32[256]{0:T(256)S(1)} %bitcast.78), kind=kLoop, calls=%fused_computation.17 | loop fusion | flops 786432 | bytes 1577984 | tf_op jit(solution)/shard_map/convert_element_type | solution.py:108
  (22 shorter events, 0.2 us)
Async XLA Ops:
  0.0 4.0 %copy-start = (f32[256,16]{0,1:T(8,128)S(1)}, f32[256,16]{0,1:T(8,128)}, u32[]{:S(2)}) copy-start(f32[256,16]{0,1:T(8,128)} %param.14) | copy-start | bytes 49156
  0.0 5.2 %copy-start.5 = (s32[256]{0:T(256)S(1)}, s32[256]{0:T(256)}, u32[]{:S(2)}) copy-start(s32[256]{0:T(256)} %param.15) | copy-start | bytes 3076
  0.0 2.0 %copy-start.3 = (bf16[256,256]{1,0:T(8,128)(2,1)S(1)}, bf16[256,256]{1,0:T(8,128)(2,1)}, u32[]{:S(2)}) copy-start(bf16[256,256]{1,0:T(8,128)(2,1)} %param.11) | copy-start | bytes 393220
  0.0 4.8 %copy-start.6 = (f32[4,1024]{1,0:T(4,128)S(1)}, f32[4,1024]{1,0:T(4,128)}, u32[]{:S(2)}) copy-start(f32[4,1024]{1,0:T(4,128)} %param.16) | copy-start | bytes 49156
  0.0 4.8 %copy-start.8 = (f32[4,256]{1,0:T(4,128)S(1)}, f32[4,256]{1,0:T(4,128)}, u32[]{:S(2)}) copy-start(f32[4,256]{1,0:T(4,128)} %param.17) | copy-start | bytes 12292
  2.1 11.6 %collective-permute-start = (bf16[3,1281]{1,0:T(4,128)(2,1)S(1)}, bf16[3,1281]{1,0:T(4,128)(2,1)S(1)}, u32[]{:S(2)}, u32[]{:S(2)}) collective-permute-start(bf16[3,1281]{1,0:T(4,128)(2,1)S(1)} %pad_maximum_fusion.2), channel_id=1, source_target_pairs={{0,4},{4,8},{8,12},{12,16},{16,20},{20,24},{24,28},{28,32},{32,36}... | collective-permute-start | bytes 23066 | tf_op jit(solution)/shard_map/ppermute | solution.py:18
  18.5 0.8 %copy-start.1 = (bf16[256,1280]{1,0:T(8,128)(2,1)}, bf16[256,1280]{1,0:T(8,128)(2,1)S(1)}, u32[]{:S(2)}) copy-start(bf16[256,1280]{1,0:T(8,128)(2,1)S(1)} %multiply_convert_fusion.4) | copy-start | bytes 1966084
  18.7 0.8 copy-start.4
  20.2 6.4 %copy-start.2 = (bf16[256,1024]{1,0:T(8,128)(2,1)S(1)}, bf16[256,1024]{1,0:T(8,128)(2,1)}, u32[]{:S(2)}) copy-start(bf16[256,1024]{1,0:T(8,128)(2,1)} %param.12) | copy-start | bytes 1572868
  21.4 21.2 %all-to-all-start = ((f32[16,1,8320]{2,1,0:T(1,128)}), f32[16,1,8320]{2,1,0:T(1,128)}, u32[]{:S(2)}, u32[]{:S(2)}) async-start(f32[16,1,8320]{2,1,0:T(1,128)} %all_to_all.13), calls=%async_computation | async-start | bytes 1064960 | tf_op jit(solution)/shard_map/all_to_all | solution.py:71
  26.4 0.7 copy-start.9
  45.5 7.0 %collective-permute-start.1 = (f32[1,8192]{1,0:T(1,128)S(1)}, f32[1,8192]{1,0:T(1,128)S(1)}, u32[]{:S(2)}, u32[]{:S(2)}) collective-permute-start(f32[1,8192]{1,0:T(1,128)S(1)} %fusion.17), channel_id=1, source_target_pairs={{0,64},{64,128},{128,192},{192,256},{256,320},{320,384},{384,448},... | collective-permute-start | bytes 98312 | tf_op jit(solution)/shard_map/ppermute | solution.py:18
  54.1 15.4 %all-to-all-start.1 = ((bf16[16,1,64,128]{3,2,1,0:T(8,128)(2,1)}), bf16[16,1,64,128]{3,2,1,0:T(8,128)(2,1)S(1)}, u32[]{:S(2)}, u32[]{:S(2)}) async-start(bf16[16,1,64,128]{3,2,1,0:T(8,128)(2,1)} %bitcast.14), calls=%async_computation.1 | async-start | bytes 524288 | tf_op jit(solution)/shard_map/all_to_all | solution.py:88
  71.5 9.6 %copy-start.7 = (f32[1024]{0:T(1024)S(1)}, f32[1024]{0:T(1024)}, u32[]{:S(2)}) copy-start(f32[1024]{0:T(1024)} %param.19) | copy-start | bytes 12292

commit v7 on v4

--- a/solution.py
+++ b/solution.py
@@ -1,6 +1,8 @@
 import jax
 import jax.numpy as jnp
 from jax import lax
+from jax.experimental import pallas as pl
+from jax.experimental.pallas import tpu as pltpu
 from jax.sharding import Mesh
 from jax.sharding import PartitionSpec as P
 
@@ -18,6 +20,57 @@
     return lax.ppermute(block, axis, route)
 
 
+def front_kernel(x_ref, bc_ref, edge_ref, keep_ref, cx_ref, cb_ref, step_ref, ends_ref,
+                 actx_ref, actbc_ref, xdt_ref, local_ref, extx, extb):
+    rows, head_cols = x_ref.shape
+    both = bc_ref.shape[1]
+    pad = edge_ref.shape[0]
+    extx[0:pad, :] = edge_ref[:, 0:head_cols].astype(jnp.float32)
+    extx[pad : pad + rows, :] = x_ref[...].astype(jnp.float32)
+    extb[0:pad, :] = edge_ref[:, head_cols : head_cols + both].astype(jnp.float32)
+    extb[pad : pad + rows, :] = bc_ref[...].astype(jnp.float32)
+
+    def conv(ext, w_ref):
+        total = jnp.zeros((rows, ext.shape[1]), jnp.float32)
+        for k in range(w_ref.shape[0]):
+            moved = ext[pl.ds(pad - k, rows), :]
+            total = total + w_ref[k : k + 1, :] * moved * keep_ref[:, k : k + 1]
+        return jax.nn.silu(total).astype(jnp.bfloat16)
+
+    ax = conv(extx, cx_ref)
+    ab = conv(extb, cb_ref)
+    actx_ref[...] = ax
+    actbc_ref[...] = ab
+    xdt = (ax.astype(jnp.float32) * step_ref[...]).astype(jnp.bfloat16)
+    xdt_ref[...] = xdt
+    written = (xdt.astype(jnp.float32) * ends_ref[...]).astype(jnp.bfloat16)
+    states = local_ref.shape[1]
+    local_ref[...] = lax.dot_general(
+        written, ab[:, 0:states], (((0,), (0,)), ((), ())), preferred_element_type=jnp.float32
+    )
+
+
+def front(x_raw, bc_raw, edge, keeps, conv_x, conv_bc, step_e, ends_e):
+    rows, head_cols = x_raw.shape
+    both = bc_raw.shape[1]
+    vmem = pl.BlockSpec(memory_space=pltpu.VMEM)
+    return pl.pallas_call(
+        front_kernel,
+        out_shape=(
+            jax.ShapeDtypeStruct((rows, head_cols), jnp.bfloat16),
+            jax.ShapeDtypeStruct((rows, both), jnp.bfloat16),
+            jax.ShapeDtypeStruct((rows, head_cols), jnp.bfloat16),
+            jax.ShapeDtypeStruct((head_cols, both // 2), jnp.float32),
+        ),
+        in_specs=[vmem] * 8,
+        out_specs=(vmem, vmem, vmem, vmem),
+        scratch_shapes=[
+            pltpu.VMEM((rows + edge.shape[0], head_cols), jnp.float32),
+            pltpu.VMEM((rows + edge.shape[0], both), jnp.float32),
+        ],
+    )(x_raw, bc_raw, edge, keeps, conv_x, conv_bc, step_e, ends_e)
+
+
 def body(x_raw, bc_raw, gate_z, step_size, log_decay, doc_ids, conv_x, conv_bc, skip, norm_gain):
     rows_dev, head_cols = x_raw.shape
     heads_dev = step_size.shape[1]
@@ -26,30 +79,36 @@
     taps = conv_x.shape[0]
     seg = lax.axis_size("seg")
     per_owner = heads_dev // seg
-    raw_all = jnp.concatenate([x_raw, bc_raw], axis=1)
+    pad = 8
     labels = doc_ids + 1
     edge = jnp.concatenate(
-        [raw_all[rows_dev - (taps - 1) :], labels[rows_dev - (taps - 1) :, None].astype(jnp.bfloat16)], axis=1
+        [x_raw[rows_dev - pad :], bc_raw[rows_dev - pad :], labels[rows_dev - pad :, None].astype(jnp.bfloat16)],
+        axis=1,
     )
     edge = shifted(edge, SEQ, 1)
-    edge_rows = edge[:, : raw_all.shape[1]]
-    edge_docs = edge[:, raw_all.shape[1]].astype(jnp.int32)
-    extended = jnp.concatenate([edge_rows, raw_all], axis=0)
+    edge_docs = edge[:, head_cols + 2 * states].astype(jnp.int32)
     ext_docs = jnp.concatenate([edge_docs, labels], axis=0)
-    kernel = jnp.concatenate([conv_x, conv_bc], axis=1)
-    total = jnp.zeros(raw_all.shape, jnp.float32)
-    for k in range(taps):
-        moved = extended[taps - 1 - k : taps - 1 - k + rows_dev].astype(jnp.float32)
-        keep = (ext_docs[taps - 1 - k : taps - 1 - k + rows_dev] == labels).astype(jnp.float32)
-        total = total + kernel[k][None, :] * moved * keep[:, None]
-    activated = jax.nn.silu(total).astype(jnp.bfloat16)
-    xconv = activated[:, :head_cols].reshape(rows_dev, heads_dev, head_size)
-    bconv = activated[:, head_cols : head_cols + states]
-    cconv = activated[:, head_cols + states :]
-    xdt = (xconv.astype(jnp.float32) * step_size[:, :, None]).astype(jnp.bfloat16)
+    keeps = jnp.stack(
+        [(ext_docs[pad - k : pad - k + rows_dev] == labels).astype(jnp.float32) for k in range(taps)], axis=1
+    )
+    previous = edge_docs[pad - 1] - 1
+    cum = jnp.cumsum(log_decay, axis=0)
+    ends = jnp.where((doc_ids == doc_ids[-1])[:, None], jnp.exp(cum[-1][None, :] - cum), 0.0)
+    xflat, bcconv, xdt_flat, local_flat = front(
+        x_raw,
+        bc_raw,
+        edge,
+        keeps,
+        conv_x,
+        conv_bc,
+        jnp.repeat(step_size, head_size, axis=1),
+        jnp.repeat(ends, head_size, axis=1),
+    )
+    xconv = xflat.reshape(rows_dev, heads_dev, head_size)
+    bconv = bcconv[:, :states]
+    cconv = bcconv[:, states:]
+    xdt = xdt_flat.reshape(rows_dev, heads_dev, head_size)
     lower = jnp.arange(GROUP)[:, None] >= jnp.arange(GROUP)[None, :]
-    previous = edge_docs[taps - 2] - 1
-    cum = jnp.cumsum(log_decay, axis=0)
     gram = jnp.dot(cconv, bconv.T, preferred_element_type=jnp.float32)
     mask = ((doc_ids[:, None] == doc_ids[None, :]) & lower)[None]
     diff = cum.T[:, :, None] - cum.T[:, None, :]
@@ -59,9 +118,7 @@
     inners = jnp.einsum("hts,shp->thp", weights, xdt, preferred_element_type=jnp.float32)
     cont = (doc_ids == previous).astype(jnp.float32)
     entries = jnp.exp(cum) * cont[:, None]
-    ends = jnp.where((doc_ids == doc_ids[-1])[:, None], jnp.exp(cum[-1][None, :] - cum), 0.0)
-    written = (xdt.astype(jnp.float32) * ends[:, :, None]).astype(jnp.bfloat16)
-    local = jnp.einsum("shp,sn->hpn", written, bconv, preferred_element_type=jnp.float32)
+    local = local_flat.reshape(heads_dev, head_size, states)
     through = jnp.exp(cum[-1]) * cont[-1]
 
     flat = head_size * states

time: 81.8 us -> 89.3 us (1.092)
  local copies, waits for them, and re-layouts: 7.96 us -> 14.3 us
  Pallas kernels: 0 us -> 4.49 us
  matrix products: 5.83 us -> 3.3 us
  starting transfers between devices: 13.7 us -> 15.3 us
  other arithmetic: 6.45 us -> 5.16 us
  waiting for transfers between devices: 36.9 us -> 35.7 us
    pallas_call x0 -> x1, Pallas kernels: none -> 4.49 us  [front(): pl.pallas_call(front_kernel, out_shape=(jax.ShapeDtypeStruct((rows, head_...]
    reshape x1 -> x3, local copies, waits for them, and re-layouts: 0.01 us -> 2.7 us  [the longest x1 1.37 us: body(): jnp.repeat(ends, head_size, axis=1)]
    ppermute x2, waiting for transfers between devices: 12.3 us -> 9.65 us  [shifted(): return lax.ppermute(block, axis, route)]
    convert_element_type x5 -> x2, other arithmetic: 2.19 us -> 0.12 us  [body(): edge_docs = edge[:, head_cols + 2 * states].astype(jnp.int32)]
    another operation x1 -> x4, local copies, waits for them, and re-layouts: 0.01 us -> 1.94 us  [the longest x1 1.14 us: body(): local.reshape(heads_dev, flat)]
    slice x5 -> x4, local copies, waits for them, and re-layouts: 0.83 us -> 2.16 us  [the longest x1 0.72 us: body(): x_raw[rows_dev - pad:]]
    all_to_all x1, waiting for transfers between devices: 8.62 us -> 9.94 us  [body(): lax.all_to_all(entering.astype(jnp.bfloat16), 'seg', 0, 0, tiled=True)]
    unnamed x22 -> x19, local copies, waits for them, and re-layouts: 3.24 us -> 1.93 us
  transfers between devices with their start and end apart: 4 -> 4, of which waited for: 4 -> 4; matrix products, arithmetic and copies ran while one was open for 5% -> 6% of each run, Pallas kernels for 0% -> 0%
where the time goes in v7:
time: 89.3 us; the launch traced here: 88.6 us
  waiting for transfers between devices  35.7 us (40%)
  starting transfers between devices  15.3 us (17%)
  local copies, waits for them, and re-layouts  14.3 us (16%)
  blocking collectives  9.4 us (11%)
  other arithmetic  5.16 us (6%)
  Pallas kernels  4.49 us (5%)
  matrix products  3.3 us (4%)
  between operations  0.98 us (1%)
    all_to_all x1, waiting for transfers between devices, body(): lax.all_to_all(payload, 'seg', 0, 0, tiled=True)  16.1 us
    all_to_all x1, waiting for transfers between devices, body(): lax.all_to_all(entering.astype(jnp.bfloat16), 'seg', 0, 0, tiled=True)  9.94 us
    ppermute x2, waiting for transfers between devices, shifted(): return lax.ppermute(block, axis, route)  9.65 us
    all_to_all x1, blocking collectives, body(): lax.all_to_all(jnp.broadcast_to(own[None], (ways, own.shape[0])), 'head',...  9.4 us
    all_to_all x1, starting transfers between devices, body(): lax.all_to_all(payload, 'seg', 0, 0, tiled=True)  6.26 us
    ppermute x2, starting transfers between devices, shifted(): return lax.ppermute(block, axis, route)  4.62 us
    pallas_call x1, Pallas kernels, front(): pl.pallas_call(front_kernel, out_shape=(jax.ShapeDtypeStruct((rows, head_...  4.49 us
    all_to_all x1, starting transfers between devices, body(): lax.all_to_all(entering.astype(jnp.bfloat16), 'seg', 0, 0, tiled=True)  4.39 us
  transfers between devices with their start and end apart: 4, of which 4 were waited for; matrix products, arithmetic and copies ran while one was open for 6% of the time, Pallas kernels for 0%

profile of v7, /device:TPU:32, one launch (start us, length us, event | category | flops | bytes accessed | tf_op | source)
XLA Modules:
  0.0 88.6 jit_solution(10745171471465089382)
XLA Ops:
  0.0 0.0 copy-start
  0.0 0.7 broadcast_add_fusion
  0.7 0.1 slice_bitcast_fusion.4
  0.8 0.1 copy.75
  0.9 0.7 slice.76
  1.6 0.7 slice.77
  2.3 1.9 %collective-permute-start = (bf16[8,1281]{1,0:T(8,128)(2,1)S(1)}, bf16[8,1281]{1,0:T(8,128)(2,1)S(1)}, u32[]{:S(2)}, u32[]{:S(2)}) collective-permute-start(bf16[8,1281]{1,0:T(8,128)(2,1)S(1)} %pad_maximum_fusion.1), channel_id=1, source_target_pairs={{0,4},{4,8},{8,12},{12,16},{16,20},{20,24},{24,28},{28,32},{32,36}... | collective-permute-start | bytes 61496 | tf_op jit(solution)/shard_map/ppermute | solution.py:20
  4.2 0.6 reduce-window.6
  4.8 0.2 slice_reduce_fusion
  5.0 0.1 copy_bitcast_fusion
  5.1 0.2 slice_reduce_fusion.3
  5.3 1.3 %slice.83 = s32[1]{0:T(128)} slice(s32[256]{0:T(256)} %param.15), slice={[255:256]} | slice | bytes 8 | tf_op jit(solution)/shard_map/slice | solution.py:96
  6.5 0.8 broadcast_in_dim.68
  7.3 0.0 copy-start.6
  7.4 1.3 %copy.79.step_ref = f32[256,1024]{1,0:T(8,128)} copy(f32[256,1024]{0,1:T(8,128)S(1)} %bitcast.77) | data formatting | bytes 2097152 | tf_op jit(solution)/shard_map/reshape | solution.py:104
  8.7 5.3 %collective-permute-done.edge_ref = bf16[8,1281]{1,0:T(8,128)(2,1)S(1)} collective-permute-done((bf16[8,1281]{1,0:T(8,128)(2,1)S(1)}, bf16[8,1281]{1,0:T(8,128)(2,1)S(1)}, u32[]{:S(2)}, u32[]{:S(2)}) %collective-permute-start) | collective-permute-done | bytes 20528 | tf_op jit(solution)/shard_map/ppermute | solution.py:20
  14.0 0.6 slice.89
  14.6 0.1 fusion.30
  14.8 0.1 pad_add_fusion
  15.5 0.0 copy-done.6
  15.5 0.7 compare_convert_fusion.3
  16.3 0.7 slice.90
  16.9 0.1 exponential_select_fusion
  17.0 0.1 broadcast_in_dim.106
  17.1 1.4 %copy.80.ends_ref = f32[256,1024]{1,0:T(8,128)} copy(f32[256,1024]{0,1:T(8,128)S(1)} %bitcast.76) | data formatting | bytes 2097152 | tf_op jit(solution)/shard_map/reshape | solution.py:105
  18.5 0.0 copy-done.5
  18.5 0.1 pad_maximum_fusion.2
  18.5 0.8 copy.78.keep_ref
  19.3 4.5 %shard_map.100 = (bf16[256,1024]{1,0:T(8,128)(2,1)}, bf16[256,256]{1,0:T(8,128)(2,1)}, bf16[256,1024]{1,0:T(8,128)(2,1)}, f32[1024,128]{1,0:T(8,128)}) custom-call(bf16[256,1024]{1,0:T(8,128)(2,1)} %x_ref.1, bf16[256,256]{1,0:T(8,128)(2,1)} %bc_ref.1, bf16[8,1281]{1,0:T(8,128)(2,1)} %copy-done.5, f32[256,4]{1,0:T(8,128)} %copy.78.keep_ref, ...), custom_call_target="tpu_custom_call" | custom-call | tf_op jit(solution)/shard_map/pallas_call | solution.py:57
  23.8 1.1 %reshape_reshape.3 = f32[16,8192]{1,0:T(8,128)S(1)} reshape(f32[1024,128]{1,0:T(8,128)} %get-tuple-element.11) | data formatting | bytes 1048576 | tf_op jit(solution)/shard_map/reshape;reshape | solution.py:126
  25.0 0.7 exponential_multiply_fusion.1
  25.7 0.1 broadcast_in_dim.109
  25.8 1.2 %all_to_all.13 = f32[16,1,8320]{2,1,0:T(1,128)} reshape(f32[16,8320]{1,0:T(8,128)S(1)} %pad_maximum_fusion) | data formatting | bytes 1064960 | tf_op jit(solution)/shard_map/all_to_all | solution.py:128
  27.0 6.3 %all-to-all-start = ((f32[16,1,8320]{2,1,0:T(1,128)}), f32[16,1,8320]{2,1,0:T(1,128)S(1)}, u32[]{:S(2)}, u32[]{:S(2)}) async-start(f32[16,1,8320]{2,1,0:T(1,128)} %all_to_all.13), calls=%async_computation | async-start | bytes 1064960 | tf_op jit(solution)/shard_map/all_to_all | solution.py:128
  33.2 16.1 %all-to-all-done = f32[16,1,8320]{2,1,0:T(1,128)S(1)} async-done(((f32[16,1,8320]{2,1,0:T(1,128)}), f32[16,1,8320]{2,1,0:T(1,128)S(1)}, u32[]{:S(2)}, u32[]{:S(2)}) %all-to-all-start) | async-done | bytes 532512 | tf_op jit(solution)/shard_map/all_to_all | solution.py:128
  49.3 0.2 slice_reduce_fusion.2
  49.5 0.1 select_reduce_fusion
  49.7 0.2 slice_reduce_fusion.1
  49.9 0.7 fusion.15
  50.6 0.0 copy-start.2
  50.6 2.7 %collective-permute-start.1 = (f32[1,8192]{1,0:T(1,128)S(1)}, f32[1,8192]{1,0:T(1,128)S(1)}, u32[]{:S(2)}, u32[]{:S(2)}) collective-permute-start(f32[1,8192]{1,0:T(1,128)S(1)} %fusion.15), channel_id=1, source_target_pairs={{0,64},{64,128},{128,192},{192,256},{256,320},{320,384},{384,448},... | collective-permute-start | bytes 98312 | tf_op jit(solution)/shard_map/ppermute | solution.py:20
  53.3 0.1 select_reduce_fusion.1
  53.4 4.3 %collective-permute-done.1 = f32[1,8192]{1,0:T(1,128)S(1)} collective-permute-done((f32[1,8192]{1,0:T(1,128)S(1)}, f32[1,8192]{1,0:T(1,128)S(1)}, u32[]{:S(2)}, u32[]{:S(2)}) %collective-permute-start.1) | collective-permute-done | bytes 32800 | tf_op jit(solution)/shard_map/ppermute | solution.py:20
  57.7 0.8 fusion.19
  58.6 0.7 copy.88
  59.3 4.4 %all-to-all-start.1 = ((bf16[16,1,64,128]{3,2,1,0:T(8,128)(2,1)}), bf16[16,1,64,128]{3,2,1,0:T(8,128)(2,1)S(1)}, u32[]{:S(2)}, u32[]{:S(2)}) async-start(bf16[16,1,64,128]{3,2,1,0:T(8,128)(2,1)} %bitcast.18), calls=%async_computation.1 | async-start | bytes 524288 | tf_op jit(solution)/shard_map/all_to_all | solution.py:145
  63.7 0.1 fusion.21
  63.8 0.0 copy-done.2
  63.8 0.0 copy-start.4
  63.9 0.2 copy.83
  64.1 0.2 copy.81
  64.3 0.0 copy-start.8
  64.3 0.5 copy-done.4
  64.8 0.2 fusion.23
  64.9 9.9 %all-to-all-done.1 = bf16[16,1,64,128]{3,2,1,0:T(8,128)(2,1)S(1)} async-done(((bf16[16,1,64,128]{3,2,1,0:T(8,128)(2,1)}), bf16[16,1,64,128]{3,2,1,0:T(8,128)(2,1)S(1)}, u32[]{:S(2)}, u32[]{:S(2)}) %all-to-all-start.1) | async-done | bytes 262176 | tf_op jit(solution)/shard_map/all_to_all | solution.py:145
  74.9 0.3 convolution_multiply_fusion
  75.2 0.0 copy-done.8
  75.2 1.3 %fusion.8 = f32[256,16,64]{0,2,1:T(8,128)S(1)} fusion(f32[256,16,64]{0,2,1:T(8,128)S(1)} %convolution_multiply_fusion, bf16[256,16,64]{0,2,1:T(8,128)(2,1)S(1)} %bitcast.80, f32[256,256]{1,0:T(8,128)S(1)} %fusion.23, f32[16,256]{1,0:T(8,128)S(1)} %get-tuple-element.13, pred[256,256]{1,0:T(8,128)(4,1)S(1)} %fusion.21, f32[256,16,64]{0,2,1:T(8,128)S(1)} %bitcast.78, ...), kind=kOutput, calls=%fused_computation.10 | convolution fusion | flops 140247040 | bytes 4014144 | tf_op jit(solution)/shard_map/hts,shp->thp/dot_general | solution.py:118
  76.5 0.0 copy-start.1
  76.5 0.3 copy.84
  76.9 0.7 copy-done.1
  77.6 0.4 multiply_reduce_fusion
  78.0 9.4 %all_to_all.20 = f32[4,1,256]{2,1,0:T(1,128)S(1)} all-to-all(f32[4,1,256]{2,1,0:T(1,128)S(1)} %broadcast_in_dim.116), channel_id=1, replica_groups=mesh['row'=8,'seg'=16,'head'=4] {'head'}, dimensions={0} | all-to-all | bytes 8192 | tf_op jit(solution)/shard_map/all_to_all | solution.py:157
  87.4 1.2 %multiply_convert_fusion.8 = bf16[256,1024]{1,0:T(8,128)(2,1)} fusion(f32[1024]{0:T(1024)S(1)} %copy-done.7, f32[256]{0:T(256)S(1)} %bitcast.82, f32[256,1024]{1,0:T(8,128)S(1)} %copy.84, bf16[256,1024]{1,0:T(8,128)(2,1)S(1)} %copy-done.1), kind=kLoop, calls=%fused_computation.17 | loop fusion | flops 2359296 | bytes 2102272 | tf_op jit(solution)/shard_map/convert_element_type | solution.py:162
  (19 shorter events, 0.2 us)
Async XLA Ops:
  0.0 4.2 %copy-start = (f32[256,16]{0,1:T(8,128)S(1)}, f32[256,16]{0,1:T(8,128)}, u32[]{:S(2)}) copy-start(f32[256,16]{0,1:T(8,128)} %param.14) | copy-start | bytes 49156
  2.3 11.7 %collective-permute-start = (bf16[8,1281]{1,0:T(8,128)(2,1)S(1)}, bf16[8,1281]{1,0:T(8,128)(2,1)S(1)}, u32[]{:S(2)}, u32[]{:S(2)}) collective-permute-start(bf16[8,1281]{1,0:T(8,128)(2,1)S(1)} %pad_maximum_fusion.1), channel_id=1, source_target_pairs={{0,4},{4,8},{8,12},{12,16},{16,20},{20,24},{24,28},{28,32},{32,36}... | collective-permute-start | bytes 61496 | tf_op jit(solution)/shard_map/ppermute | solution.py:20
  7.3 8.2 %copy-start.6 = (s32[256]{0:T(256)S(1)}, s32[256]{0:T(256)}, u32[]{:S(2)}) copy-start(s32[256]{0:T(256)} %param.15) | copy-start | bytes 3076
  14.0 4.4 %copy-start.5 = (bf16[8,1281]{1,0:T(8,128)(2,1)}, bf16[8,1281]{1,0:T(8,128)(2,1)S(1)}, u32[]{:S(2)}) copy-start(bf16[8,1281]{1,0:T(8,128)(2,1)S(1)} %collective-permute-done.edge_ref) | copy-start | bytes 61492
  27.0 22.4 %all-to-all-start = ((f32[16,1,8320]{2,1,0:T(1,128)}), f32[16,1,8320]{2,1,0:T(1,128)S(1)}, u32[]{:S(2)}, u32[]{:S(2)}) async-start(f32[16,1,8320]{2,1,0:T(1,128)} %all_to_all.13), calls=%async_computation | async-start | bytes 1064960 | tf_op jit(solution)/shard_map/all_to_all | solution.py:128
  50.6 13.3 %copy-start.2 = (bf16[256,1024]{1,0:T(8,128)(2,1)S(1)}, bf16[256,1024]{1,0:T(8,128)(2,1)}, u32[]{:S(2)}) copy-start(bf16[256,1024]{1,0:T(8,128)(2,1)} %get-tuple-element.12) | copy-start | bytes 1572868
  50.6 7.2 %collective-permute-start.1 = (f32[1,8192]{1,0:T(1,128)S(1)}, f32[1,8192]{1,0:T(1,128)S(1)}, u32[]{:S(2)}, u32[]{:S(2)}) collective-permute-start(f32[1,8192]{1,0:T(1,128)S(1)} %fusion.15), channel_id=1, source_target_pairs={{0,64},{64,128},{128,192},{192,256},{256,320},{320,384},{384,448},... | collective-permute-start | bytes 98312 | tf_op jit(solution)/shard_map/ppermute | solution.py:20
  59.3 4.7 %copy-start.3 = (bf16[256,1024]{1,0:T(8,128)(2,1)S(1)}, bf16[256,1024]{1,0:T(8,128)(2,1)}, u32[]{:S(2)}) copy-start(bf16[256,1024]{1,0:T(8,128)(2,1)} %get-tuple-element.9) | copy-start | bytes 1572868
  59.3 15.5 %all-to-all-start.1 = ((bf16[16,1,64,128]{3,2,1,0:T(8,128)(2,1)}), bf16[16,1,64,128]{3,2,1,0:T(8,128)(2,1)S(1)}, u32[]{:S(2)}, u32[]{:S(2)}) async-start(bf16[16,1,64,128]{3,2,1,0:T(8,128)(2,1)} %bitcast.18), calls=%async_computation.1 | async-start | bytes 524288 | tf_op jit(solution)/shard_map/all_to_all | solution.py:145
  63.8 0.9 %copy-start.4 = (bf16[256,256]{1,0:T(8,128)(2,1)S(1)}, bf16[256,256]{1,0:T(8,128)(2,1)}, u32[]{:S(2)}) copy-start(bf16[256,256]{1,0:T(8,128)(2,1)} %get-tuple-element.10) | copy-start | bytes 393220
  64.3 10.9 %copy-start.8 = (f32[16]{0:T(128)S(1)}, f32[16]{0:T(128)}, u32[]{:S(2)}) copy-start(f32[16]{0:T(128)} %param.18) | copy-start | bytes 196
  76.5 1.0 %copy-start.1 = (bf16[256,1024]{1,0:T(8,128)(2,1)S(1)}, bf16[256,1024]{1,0:T(8,128)(2,1)}, u32[]{:S(2)}) copy-start(bf16[256,1024]{1,0:T(8,128)(2,1)} %param.12) | copy-start | bytes 1572868
  77.6 9.8 %copy-start.7 = (f32[1024]{0:T(1024)S(1)}, f32[1024]{0:T(1024)}, u32[]{:S(2)}) copy-start(f32[1024]{0:T(1024)} %param.19) | copy-start | bytes 12292

commit v8 on v4

--- a/solution.py
+++ b/solution.py
@@ -25,7 +25,6 @@
     states = bc_raw.shape[1] // 2
     taps = conv_x.shape[0]
     seg = lax.axis_size("seg")
-    per_owner = heads_dev // seg
     raw_all = jnp.concatenate([x_raw, bc_raw], axis=1)
     labels = doc_ids + 1
     edge = jnp.concatenate(
@@ -64,30 +63,24 @@
     local = jnp.einsum("shp,sn->hpn", written, bconv, preferred_element_type=jnp.float32)
     through = jnp.exp(cum[-1]) * cont[-1]
 
-    flat = head_size * states
+    pad_rows = 8
     payload = jnp.concatenate(
-        [local.reshape(heads_dev, flat), jnp.broadcast_to(through[:, None], (heads_dev, 128))], axis=1
+        [local, jnp.broadcast_to(through[:, None, None], (heads_dev, pad_rows, states))], axis=1
     )
-    got = lax.all_to_all(payload, "seg", 0, 0, tiled=True).reshape(seg, per_owner, flat + 128)
-    pieces = jnp.transpose(got[:, :, :flat], (1, 0, 2))
-    decays = got[:, :, flat].T
+    got = lax.all_to_all(payload, "seg", 0, 0, tiled=True)
+    pieces = got[:, :head_size, :]
+    decays = got[:, head_size, 0]
     after = jnp.arange(seg + 1)[:, None, None]
     source = jnp.arange(seg)[None, :, None]
-    between = (source < jnp.arange(seg)[None, None, :]) & (jnp.arange(seg)[None, None, :] < after)
-    spans = jnp.prod(jnp.where(between[None], decays[:, None, None, :], 1.0), axis=3)
-    weights_to = jnp.where((source[..., 0] < after[..., 0])[None], spans, 0.0)
-    head_first = jnp.prod(
-        jnp.where(jnp.arange(seg)[None, :] < jnp.arange(seg)[:, None], decays[:, None, :], 1.0), axis=2
-    )
+    middle = jnp.arange(seg)[None, None, :]
+    spans = jnp.prod(jnp.where((source < middle) & (middle < after), decays[None, None, :], 1.0), axis=2)
+    weights_to = jnp.where(source[..., 0] < after[..., 0], spans, 0.0)
     exact = lax.Precision.HIGHEST
-    total_row = jnp.einsum("gj,gjf->gf", weights_to[:, seg], pieces, precision=exact)
-    carry = shifted(total_row, "row", 1)
-    folds = jnp.einsum("gij,gjf->gif", weights_to[:, :seg], pieces, precision=exact)
-    entering = head_first[:, :, None] * carry[:, None, :] + folds
-    entering = jnp.transpose(entering, (1, 0, 2)).reshape(seg, per_owner, head_size, states)
-    entered = lax.all_to_all(entering.astype(jnp.bfloat16), "seg", 0, 0, tiled=True).reshape(
-        heads_dev, head_size, states
-    )
+    carry = shifted(jnp.einsum("j,jpn->pn", weights_to[seg], pieces, precision=exact), "row", 1)
+    head_first = jnp.prod(jnp.where(middle[0] < after[:seg, :, 0], decays[None, :], 1.0), axis=1)
+    folds = jnp.einsum("ij,jpn->ipn", weights_to[:seg], pieces, precision=exact)
+    entering = head_first[:, None, None] * carry[None] + folds
+    entered = lax.all_to_all(entering.astype(jnp.bfloat16), "seg", 0, 0, tiled=True)
 
     carried = (
         jnp.einsum("tn,hpn->thp", cconv, entered, preferred_element_type=jnp.float32)

time: 81.8 us -> 82.3 us (level)
  local copies, waits for them, and re-layouts: 7.96 us -> 6.52 us
  other arithmetic: 6.45 us -> 7.35 us
    all_to_all x1 -> x0, local copies, waits for them, and re-layouts: 1.16 us -> none  [body(): lax.all_to_all(payload, 'seg', 0, 0, tiled=True)]
    unnamed x22 -> x20, local copies, waits for them, and re-layouts: 3.24 us -> 2.18 us
    all_to_all x1, waiting for transfers between devices: 16 us -> 16.9 us  [body(): got = lax.all_to_all(payload, 'seg', 0, 0, tiled=True)]
    concatenate x1, other arithmetic: 0.04 us -> 0.86 us  [body(): jnp.concatenate([local, jnp.broadcast_to(through[:, None, None], (heads_d...]
  transfers between devices with their start and end apart: 4 -> 4, of which waited for: 4 -> 4; matrix products, arithmetic and copies ran while one was open for 5% -> 6% of each run, Pallas kernels for 0% -> 0%
where the time goes in v8:
time: 82.3 us; the launch traced here: 81.7 us
  waiting for transfers between devices  37.7 us (46%)
  starting transfers between devices  13.9 us (17%)
  blocking collectives  9.39 us (11%)
  other arithmetic  7.35 us (9%)
  local copies, waits for them, and re-layouts  6.52 us (8%)
  matrix products  5.81 us (7%)
  between operations  1 us (1%)
    all_to_all x1, waiting for transfers between devices, body(): got = lax.all_to_all(payload, 'seg', 0, 0, tiled=True)  16.9 us
    ppermute x2, waiting for transfers between devices, shifted(): return lax.ppermute(block, axis, route)  12.2 us
    all_to_all x1, blocking collectives, body(): lax.all_to_all(jnp.broadcast_to(own[None], (ways, own.shape[0])), 'head',...  9.39 us
    all_to_all x1, waiting for transfers between devices, body(): lax.all_to_all(entering.astype(jnp.bfloat16), 'seg', 0, 0, tiled=True)  8.62 us
    all_to_all x1, starting transfers between devices, body(): got = lax.all_to_all(payload, 'seg', 0, 0, tiled=True)  4.97 us
    ppermute x2, starting transfers between devices, shifted(): return lax.ppermute(block, axis, route)  4.51 us
    all_to_all x1, starting transfers between devices, body(): lax.all_to_all(entering.astype(jnp.bfloat16), 'seg', 0, 0, tiled=True)  4.47 us
    dot_general x1, matrix products, body(): jnp.einsum('hts,shp->thp', weights, xdt, preferred_element_type=jnp.float32)  2.32 us
  transfers between devices with their start and end apart: 4, of which 4 were waited for; matrix products, arithmetic and copies ran while one was open for 6% of the time, Pallas kernels for 0%

profile of v8, /device:TPU:32, one launch (start us, length us, event | category | flops | bytes accessed | tf_op | source)
XLA Modules:
  0.0 81.7 jit_solution(12244782162749314667)
XLA Ops:
  0.0 0.0 copy-start
  0.0 0.0 copy-start.4
  0.0 0.0 copy-start.2
  0.0 0.0 copy-start.5
  0.0 0.0 copy-start.7
  0.0 0.7 broadcast_add_fusion
  0.8 0.1 slice_bitcast_fusion.7
  0.9 0.1 copy.38
  1.0 1.1 %constant_dynamic-update-slice_fusion.3 = bf16[256,1280]{1,0:T(8,128)(2,1)S(1)} fusion(bf16[256,1024]{1,0:T(8,128)(2,1)} %param.10), kind=kLoop, calls=%fused_computation.57 | loop fusion | bytes 1048576
  2.0 0.0 copy-done.2
  2.1 1.9 %collective-permute-start = (bf16[3,1281]{1,0:T(4,128)(2,1)S(1)}, bf16[3,1281]{1,0:T(4,128)(2,1)S(1)}, u32[]{:S(2)}, u32[]{:S(2)}) collective-permute-start(bf16[3,1281]{1,0:T(4,128)(2,1)S(1)} %pad_maximum_fusion.2), channel_id=1, source_target_pairs={{0,4},{4,8},{8,12},{12,16},{16,20},{20,24},{24,28},{28,32},{32,36}... | collective-permute-start | bytes 23066 | tf_op jit(solution)/shard_map/ppermute | solution.py:18
  4.0 0.0 copy-done
  4.1 0.6 reduce-window.6
  4.6 0.2 slice_reduce_fusion
  4.9 0.0 copy-done.5
  4.9 0.0 copy-done.7
  4.9 0.1 slice_reduce_fusion.6
  4.9 0.1 fusion.35
  5.0 0.2 slice_reduce_fusion.2
  5.2 0.0 copy-done.4
  5.2 0.6 slice.123
  5.8 8.0 %collective-permute-done = bf16[3,1281]{1,0:T(4,128)(2,1)S(1)} collective-permute-done((bf16[3,1281]{1,0:T(4,128)(2,1)S(1)}, bf16[3,1281]{1,0:T(4,128)(2,1)S(1)}, u32[]{:S(2)}, u32[]{:S(2)}) %collective-permute-start) | collective-permute-done | bytes 7718 | tf_op jit(solution)/shard_map/ppermute | solution.py:18
  13.8 0.6 slice.125
  14.3 0.1 fusion.32
  14.5 0.1 pad_add_fusion
  15.2 0.7 compare_convert_fusion.3
  16.0 0.6 slice.126
  16.5 0.6 exponential_multiply_fusion.1
  17.2 0.1 exponential_multiply_fusion
  17.3 1.2 %multiply_convert_fusion.4 = bf16[256,1280]{1,0:T(8,128)(2,1)S(1)} fusion(bf16[256,1280]{1,0:T(8,128)(2,1)S(1)} %constant_dynamic-update-slice_fusion.2, bf16[3,1280]{1,0:T(4,128)(2,1)S(1)} %slice.138, f32[256]{0:T(256)S(1)} %get-tuple-element.14, f32[1280]{0:T(1024)S(1)} %get-tuple-element.6, f32[256]{0:T(256)S(1)} %get-tuple-element.15, ...), kind=kLoop, calls=%fused_computation.13 | loop fusion | flops 9175040 | bytes 1341952 | tf_op jit(solution)/shard_map/convert_element_type | solution.py:44
  18.5 0.1 slice_convert_fusion
  18.7 0.0 copy-start.3
  18.7 0.3 copy.39
  19.0 0.4 copy-done.3
  19.4 0.3 fusion.15
  19.7 0.1 broadcast_in_dim.66
  19.8 0.9 %pad_maximum_fusion.1 = f32[16,72,128]{2,1,0:T(8,128)} fusion(f32[16,8,128]{2,1,0:T(8,128)S(1)} %broadcast_in_dim.66, f32[16,64,128]{2,1,0:T(8,128)S(1)} %fusion.15), kind=kLoop, calls=%fused_computation.27 | loop fusion | flops 147456 | bytes 1179648 | tf_op jit(solution)/shard_map/concatenate | solution.py:67
  20.6 5.0 %all-to-all-start = ((f32[16,72,128]{2,1,0:T(8,128)}), f32[16,72,128]{2,1,0:T(8,128)S(1)}, u32[]{:S(2)}, u32[]{:S(2)}) async-start(f32[16,72,128]{2,1,0:T(8,128)} %pad_maximum_fusion.1), calls=%async_computation | async-start | bytes 1179648 | tf_op jit(solution)/shard_map/all_to_all | solution.py:70
  25.6 0.1 copy.42
  25.7 0.1 fusion.21
  25.8 16.9 %all-to-all-done = f32[16,72,128]{2,1,0:T(8,128)S(1)} async-done(((f32[16,72,128]{2,1,0:T(8,128)}), f32[16,72,128]{2,1,0:T(8,128)S(1)}, u32[]{:S(2)}, u32[]{:S(2)}) %all-to-all-start) | async-done | bytes 589856 | tf_op jit(solution)/shard_map/all_to_all | solution.py:70
  42.7 0.2 slice_reduce_fusion.1
  42.9 0.1 select_reduce_fusion
  43.1 0.1 copy.43
  43.2 0.7 fusion.17
  43.9 2.6 %collective-permute-start.1 = (f32[64,128]{1,0:T(8,128)S(1)}, f32[64,128]{1,0:T(8,128)S(1)}, u32[]{:S(2)}, u32[]{:S(2)}) collective-permute-start(f32[64,128]{1,0:T(8,128)S(1)} %bitcast.57), channel_id=1, source_target_pairs={{0,64},{64,128},{128,192},{192,256},{256,320},{320,384},{384,448},... | collective-permute-start | bytes 98312 | tf_op jit(solution)/shard_map/ppermute | solution.py:18
  46.5 0.2 select_reduce_fusion.1
  46.7 4.2 %collective-permute-done.1 = f32[64,128]{1,0:T(8,128)S(1)} collective-permute-done((f32[64,128]{1,0:T(8,128)S(1)}, f32[64,128]{1,0:T(8,128)S(1)}, u32[]{:S(2)}, u32[]{:S(2)}) %collective-permute-start.1) | collective-permute-done | bytes 32800 | tf_op jit(solution)/shard_map/ppermute | solution.py:18
  50.9 0.8 %add_convert_fusion = bf16[16,64,128]{2,0,1:T(8,128)(2,1)S(1)} fusion(f32[64,128]{1,0:T(8,128)S(1)} %collective-permute-done.1, f32[16]{0:T(128)S(1)} %select_reduce_fusion.1, f32[16,64,128]{2,1,0:T(8,128)S(1)} %slice.153, f32[17,16]{1,0:T(8,128)S(1)} %broadcast_select_fusion), kind=kOutput, calls=%fused_computation.30 | convolution fusion | flops 25559040 | bytes 827904 | tf_op jit(solution)/shard_map/ij,jpn->ipn/dot_general | solution.py:81
  51.7 0.8 copy.45
  52.5 4.5 %all-to-all-start.1 = ((bf16[16,64,128]{2,1,0:T(8,128)(2,1)}), bf16[16,64,128]{2,1,0:T(8,128)(2,1)S(1)}, u32[]{:S(2)}, u32[]{:S(2)}) async-start(bf16[16,64,128]{2,1,0:T(8,128)(2,1)} %copy.45), calls=%async_computation.1 | async-start | bytes 524288 | tf_op jit(solution)/shard_map/all_to_all | solution.py:83
  57.0 0.2 fusion.25
  57.2 0.0 copy-start.8
  57.2 2.3 %fusion.6 = f32[256,16,64]{0,2,1:T(8,128)} fusion(f32[256,256]{1,0:T(8,128)S(1)} %fusion.25, f32[16,256]{1,0:T(8,128)S(1)} %get-tuple-element.12, pred[256,256]{1,0:T(8,128)(4,1)S(1)} %fusion.21, f32[256,16,64]{0,2,1:T(8,128)S(1)} %bitcast.54, f32[256,16]{0,1:T(8,128)S(1)} %copy-done.3), kind=kOutput, calls=%fused_computation.7 | convolution fusion | flops 139984896 | bytes 2457600 | tf_op jit(solution)/shard_map/hts,shp->thp/dot_general | solution.py:58
  59.5 8.6 %all-to-all-done.1 = bf16[16,64,128]{2,1,0:T(8,128)(2,1)S(1)} async-done(((bf16[16,64,128]{2,1,0:T(8,128)(2,1)}), bf16[16,64,128]{2,1,0:T(8,128)(2,1)S(1)}, u32[]{:S(2)}, u32[]{:S(2)}) %all-to-all-start.1) | async-done | bytes 262176 | tf_op jit(solution)/shard_map/all_to_all | solution.py:83
  68.1 0.0 copy-done.8
  68.1 1.5 %fusion.8 = f32[256,16,64]{0,2,1:T(8,128)S(1)} fusion(f32[256,16,64]{0,2,1:T(8,128)} %fusion.6, bf16[16,64,128]{2,1,0:T(8,128)(2,1)S(1)} %all-to-all-done.1, f32[256,16,64]{0,2,1:T(8,128)S(1)} %bitcast.55, f32[16]{0:T(128)S(1)} %copy-done.8, f32[256,16]{0,1:T(8,128)S(1)} %get-tuple-element.9, bf16[256,1280]{1,0:T(8,128)(2,1)S(1)} %multiply_convert_fusion.4), kind=kOutput, calls=%fused_computation.10 | convolution fusion | flops 68157440 | bytes 3490304 | tf_op jit(solution)/shard_map/tn,hpn->thp/dot_general | solution.py:86
  69.7 0.0 copy-start.1
  69.7 0.3 copy.46
  70.0 0.7 copy-done.1
  70.7 0.4 multiply_reduce_fusion
  71.1 9.4 %all_to_all.16 = f32[4,1,256]{2,1,0:T(1,128)S(1)} all-to-all(f32[4,1,256]{2,1,0:T(1,128)S(1)} %broadcast_in_dim.106), channel_id=1, replica_groups=mesh['row'=8,'seg'=16,'head'=4] {'head'}, dimensions={0} | all-to-all | bytes 8192 | tf_op jit(solution)/shard_map/all_to_all | solution.py:93
  80.5 0.0 copy-done.6
  80.6 1.2 %multiply_convert_fusion.5 = bf16[256,1024]{1,0:T(8,128)(2,1)} fusion(f32[1024]{0:T(1024)S(1)} %copy-done.6, f32[256]{0:T(256)S(1)} %bitcast.58, f32[256,1024]{1,0:T(8,128)S(1)} %copy.46, bf16[256,1024]{1,0:T(8,128)(2,1)S(1)} %copy-done.1), kind=kLoop, calls=%fused_computation.18 | loop fusion | flops 2359296 | bytes 2102272 | tf_op jit(solution)/shard_map/convert_element_type | solution.py:98
  (19 shorter events, 0.2 us)
Async XLA Ops:
  0.0 4.0 %copy-start = (f32[256,16]{0,1:T(8,128)S(1)}, f32[256,16]{0,1:T(8,128)}, u32[]{:S(2)}) copy-start(f32[256,16]{0,1:T(8,128)} %param.14) | copy-start | bytes 49156
  0.0 5.2 %copy-start.4 = (s32[256]{0:T(256)S(1)}, s32[256]{0:T(256)}, u32[]{:S(2)}) copy-start(s32[256]{0:T(256)} %param.15) | copy-start | bytes 3076
  0.0 2.0 %copy-start.2 = (bf16[256,256]{1,0:T(8,128)(2,1)S(1)}, bf16[256,256]{1,0:T(8,128)(2,1)}, u32[]{:S(2)}) copy-start(bf16[256,256]{1,0:T(8,128)(2,1)} %param.11) | copy-start | bytes 393220
  0.0 4.8 %copy-start.5 = (f32[4,1024]{1,0:T(4,128)S(1)}, f32[4,1024]{1,0:T(4,128)}, u32[]{:S(2)}) copy-start(f32[4,1024]{1,0:T(4,128)} %param.16) | copy-start | bytes 49156
  0.0 4.8 %copy-start.7 = (f32[4,256]{1,0:T(4,128)S(1)}, f32[4,256]{1,0:T(4,128)}, u32[]{:S(2)}) copy-start(f32[4,256]{1,0:T(4,128)} %param.17) | copy-start | bytes 12292
  2.1 11.6 %collective-permute-start = (bf16[3,1281]{1,0:T(4,128)(2,1)S(1)}, bf16[3,1281]{1,0:T(4,128)(2,1)S(1)}, u32[]{:S(2)}, u32[]{:S(2)}) collective-permute-start(bf16[3,1281]{1,0:T(4,128)(2,1)S(1)} %pad_maximum_fusion.2), channel_id=1, source_target_pairs={{0,4},{4,8},{8,12},{12,16},{16,20},{20,24},{24,28},{28,32},{32,36}... | collective-permute-start | bytes 23066 | tf_op jit(solution)/shard_map/ppermute | solution.py:18
  18.7 0.7 copy-start.3
  20.6 22.1 %all-to-all-start = ((f32[16,72,128]{2,1,0:T(8,128)}), f32[16,72,128]{2,1,0:T(8,128)S(1)}, u32[]{:S(2)}, u32[]{:S(2)}) async-start(f32[16,72,128]{2,1,0:T(8,128)} %pad_maximum_fusion.1), calls=%async_computation | async-start | bytes 1179648 | tf_op jit(solution)/shard_map/all_to_all | solution.py:70
  43.9 7.0 %collective-permute-start.1 = (f32[64,128]{1,0:T(8,128)S(1)}, f32[64,128]{1,0:T(8,128)S(1)}, u32[]{:S(2)}, u32[]{:S(2)}) collective-permute-start(f32[64,128]{1,0:T(8,128)S(1)} %bitcast.57), channel_id=1, source_target_pairs={{0,64},{64,128},{128,192},{192,256},{256,320},{320,384},{384,448},... | collective-permute-start | bytes 98312 | tf_op jit(solution)/shard_map/ppermute | solution.py:18
  52.5 15.6 %all-to-all-start.1 = ((bf16[16,64,128]{2,1,0:T(8,128)(2,1)}), bf16[16,64,128]{2,1,0:T(8,128)(2,1)S(1)}, u32[]{:S(2)}, u32[]{:S(2)}) async-start(bf16[16,64,128]{2,1,0:T(8,128)(2,1)} %copy.45), calls=%async_computation.1 | async-start | bytes 524288 | tf_op jit(solution)/shard_map/all_to_all | solution.py:83
  57.2 11.0 %copy-start.8 = (f32[16]{0:T(128)S(1)}, f32[16]{0:T(128)}, u32[]{:S(2)}) copy-start(f32[16]{0:T(128)} %param.18) | copy-start | bytes 196
  69.7 1.0 %copy-start.1 = (bf16[256,1024]{1,0:T(8,128)(2,1)S(1)}, bf16[256,1024]{1,0:T(8,128)(2,1)}, u32[]{:S(2)}) copy-start(bf16[256,1024]{1,0:T(8,128)(2,1)} %param.12) | copy-start | bytes 1572868
  70.7 9.8 %copy-start.6 = (f32[1024]{0:T(1024)S(1)}, f32[1024]{0:T(1024)}, u32[]{:S(2)}) copy-start(f32[1024]{0:T(1024)} %param.19) | copy-start | bytes 12292

commit v9 on v4

--- a/solution.py
+++ b/solution.py
@@ -57,6 +57,7 @@
         jnp.bfloat16
     )
     inners = jnp.einsum("hts,shp->thp", weights, xdt, preferred_element_type=jnp.float32)
+    inners, gate = lax.optimization_barrier((inners, jax.nn.silu(gate_z.astype(jnp.float32))))
     cont = (doc_ids == previous).astype(jnp.float32)
     entries = jnp.exp(cum) * cont[:, None]
     ends = jnp.where((doc_ids == doc_ids[-1])[:, None], jnp.exp(cum[-1][None, :] - cum), 0.0)
@@ -94,7 +95,7 @@
         * entries[:, :, None]
     )
     scanned = inners + carried + skip[None, :, None] * xconv.astype(jnp.float32)
-    gated_rows = scanned.reshape(GROUP, head_cols) * jax.nn.silu(gate_z.astype(jnp.float32))
+    gated_rows = scanned.reshape(GROUP, head_cols) * gate
     own = jnp.sum(gated_rows * gated_rows, axis=1)
     ways = lax.axis_size("head")
     each = lax.all_to_all(jnp.broadcast_to(own[None], (ways, own.shape[0])), "head", 0, 0, tiled=True)

time: 81.8 us -> 80.8 us (0.988)
  waiting for transfers between devices: 36.9 us -> 35.5 us
  other arithmetic: 6.45 us -> 7.36 us
    all_to_all x1, waiting for transfers between devices: 16 us -> 14.6 us  [body(): lax.all_to_all(payload, 'seg', 0, 0, tiled=True)]
    mul x0 -> x1, other arithmetic: none -> 1.32 us  [body(): jax.nn.silu(gate_z.astype(jnp.float32))]
  transfers between devices with their start and end apart: 4 -> 4, of which waited for: 4 -> 4; matrix products, arithmetic and copies ran while one was open for 5% -> 7% of each run, Pallas kernels for 0% -> 0%
where the time goes in v9:
time: 80.8 us; the launch traced here: 80.2 us
  waiting for transfers between devices  35.5 us (44%)
  starting transfers between devices  13.7 us (17%)
  blocking collectives  9.39 us (12%)
  other arithmetic  7.36 us (9%)
  local copies, waits for them, and re-layouts  7.31 us (9%)
  matrix products  5.88 us (7%)
  between operations  1.03 us (1%)
    all_to_all x1, waiting for transfers between devices, body(): lax.all_to_all(payload, 'seg', 0, 0, tiled=True)  14.6 us
    ppermute x2, waiting for transfers between devices, shifted(): return lax.ppermute(block, axis, route)  12.3 us
    all_to_all x1, blocking collectives, body(): lax.all_to_all(jnp.broadcast_to(own[None], (ways, own.shape[0])), 'head',...  9.39 us
    all_to_all x1, waiting for transfers between devices, body(): lax.all_to_all(entering.astype(jnp.bfloat16), 'seg', 0, 0, tiled=True)  8.61 us
    all_to_all x1, starting transfers between devices, body(): lax.all_to_all(payload, 'seg', 0, 0, tiled=True)  4.97 us
    ppermute x2, starting transfers between devices, shifted(): return lax.ppermute(block, axis, route)  4.51 us
    all_to_all x1, starting transfers between devices, body(): lax.all_to_all(entering.astype(jnp.bfloat16), 'seg', 0, 0, tiled=True)  4.25 us
    unnamed x22, local copies, waits for them, and re-layouts  2.6 us
  transfers between devices with their start and end apart: 4, of which 4 were waited for; matrix products, arithmetic and copies ran while one was open for 7% of the time, Pallas kernels for 0%

profile of v9, /device:TPU:32, one launch (start us, length us, event | category | flops | bytes accessed | tf_op | source)
XLA Modules:
  0.0 80.2 jit_solution(16161574632054264326)
XLA Ops:
  0.0 0.0 copy-start
  0.0 0.0 copy-start.5
  0.0 0.0 copy-start.7
  0.0 0.7 broadcast_add_fusion
  0.8 0.1 slice_bitcast_fusion.4
  0.9 0.1 copy.50
  1.0 1.1 %constant_dynamic-update-slice_fusion.3 = bf16[256,1280]{1,0:T(8,128)(2,1)S(1)} fusion(bf16[256,1024]{1,0:T(8,128)(2,1)} %param.10), kind=kLoop, calls=%fused_computation.60 | loop fusion | bytes 1048576
  2.0 0.0 copy-done.2
  2.1 1.9 %collective-permute-start = (bf16[3,1281]{1,0:T(4,128)(2,1)S(1)}, bf16[3,1281]{1,0:T(4,128)(2,1)S(1)}, u32[]{:S(2)}, u32[]{:S(2)}) collective-permute-start(bf16[3,1281]{1,0:T(4,128)(2,1)S(1)} %pad_maximum_fusion.2), channel_id=1, source_target_pairs={{0,4},{4,8},{8,12},{12,16},{16,20},{20,24},{24,28},{28,32},{32,36}... | collective-permute-start | bytes 23066 | tf_op jit(solution)/shard_map/ppermute | solution.py:18
  4.0 0.0 copy-done
  4.1 0.6 reduce-window.6
  4.6 0.2 slice_reduce_fusion
  4.9 0.0 copy-done.5
  4.9 0.0 copy-done.7
  4.9 0.1 slice_reduce_fusion.7
  4.9 0.1 fusion.39
  5.0 0.2 slice_reduce_fusion.3
  5.2 0.0 copy-done.4
  5.2 0.6 slice.119
  5.8 8.0 %collective-permute-done = bf16[3,1281]{1,0:T(4,128)(2,1)S(1)} collective-permute-done((bf16[3,1281]{1,0:T(4,128)(2,1)S(1)}, bf16[3,1281]{1,0:T(4,128)(2,1)S(1)}, u32[]{:S(2)}, u32[]{:S(2)}) %collective-permute-start) | collective-permute-done | bytes 7718 | tf_op jit(solution)/shard_map/ppermute | solution.py:18
  13.8 0.6 slice.121
  14.3 0.1 fusion.36
  14.5 0.1 pad_add_fusion
  15.2 0.7 compare_convert_fusion.3
  16.0 0.6 slice.122
  16.5 0.6 exponential_multiply_fusion.1
  17.2 0.1 exponential_select_fusion
  17.3 1.2 %multiply_convert_fusion.4 = bf16[256,1280]{1,0:T(8,128)(2,1)S(1)} fusion(bf16[256,1280]{1,0:T(8,128)(2,1)S(1)} %constant_dynamic-update-slice_fusion.2, bf16[3,1280]{1,0:T(4,128)(2,1)S(1)} %slice.134, f32[256]{0:T(256)S(1)} %get-tuple-element.20, f32[1280]{0:T(1024)S(1)} %get-tuple-element.10, f32[256]{0:T(256)S(1)} %get-tuple-element.21, ...), kind=kLoop, calls=%fused_computation.13 | loop fusion | flops 9175040 | bytes 1341952 | tf_op jit(solution)/shard_map/convert_element_type | solution.py:45
  18.5 0.0 copy-start.1
  18.6 0.1 slice_convert_fusion
  18.7 0.0 copy-start.3
  18.7 0.3 copy.51
  19.0 0.4 copy-done.3
  19.4 0.3 fusion.14
  19.7 0.3 copy.80
  20.1 0.1 broadcast_in_dim.68
  20.2 1.2 %all_to_all.13 = f32[16,1,8320]{2,1,0:T(1,128)} reshape(f32[16,8320]{1,0:T(8,128)S(1)} %pad_maximum_fusion.1) | data formatting | bytes 1064960 | tf_op jit(solution)/shard_map/all_to_all | solution.py:72
  21.3 5.0 %all-to-all-start = ((f32[16,1,8320]{2,1,0:T(1,128)}), f32[16,1,8320]{2,1,0:T(1,128)S(1)}, u32[]{:S(2)}, u32[]{:S(2)}) async-start(f32[16,1,8320]{2,1,0:T(1,128)} %all_to_all.13), calls=%async_computation | async-start | bytes 1064960 | tf_op jit(solution)/shard_map/all_to_all | solution.py:72
  26.3 0.1 fusion.24
  26.4 1.3 %convert_multiply_fusion = f32[256,1024]{1,0:T(8,128)S(1)} fusion(bf16[256,1024]{1,0:T(8,128)(2,1)} %param.12), kind=kLoop, calls=%fused_computation.11 | loop fusion | flops 1310720 | bytes 1572864 | tf_op jit(solution)/shard_map/jit(silu)/mul | solution.py:60
  27.8 14.6 %all-to-all-done = f32[16,1,8320]{2,1,0:T(1,128)S(1)} async-done(((f32[16,1,8320]{2,1,0:T(1,128)}), f32[16,1,8320]{2,1,0:T(1,128)S(1)}, u32[]{:S(2)}, u32[]{:S(2)}) %all-to-all-start) | async-done | bytes 532512 | tf_op jit(solution)/shard_map/all_to_all | solution.py:72
  42.4 0.2 slice_reduce_fusion.2
  42.6 0.1 select_reduce_fusion
  42.8 0.2 slice_reduce_fusion.1
  42.9 0.1 slice.149
  43.0 0.7 fusion.17
  43.7 2.6 %collective-permute-start.1 = (f32[1,8192]{1,0:T(1,128)S(1)}, f32[1,8192]{1,0:T(1,128)S(1)}, u32[]{:S(2)}, u32[]{:S(2)}) collective-permute-start(f32[1,8192]{1,0:T(1,128)S(1)} %fusion.17), channel_id=1, source_target_pairs={{0,64},{64,128},{128,192},{192,256},{256,320},{320,384},{384,448},... | collective-permute-start | bytes 98312 | tf_op jit(solution)/shard_map/ppermute | solution.py:18
  46.3 0.1 select_reduce_fusion.1
  46.4 4.3 %collective-permute-done.1 = f32[1,8192]{1,0:T(1,128)S(1)} collective-permute-done((f32[1,8192]{1,0:T(1,128)S(1)}, f32[1,8192]{1,0:T(1,128)S(1)}, u32[]{:S(2)}, u32[]{:S(2)}) %collective-permute-start.1) | collective-permute-done | bytes 32800 | tf_op jit(solution)/shard_map/ppermute | solution.py:18
  50.7 0.9 %fusion.22 = bf16[2,8,64,128]{3,1,2,0:T(8,128)(2,1)S(1)} fusion(f32[8192]{0:T(1024)S(1)} %bitcast.77, f32[16]{0:T(128)S(1)} %select_reduce_fusion.1, f32[16,1,8192]{2,1,0:T(1,128)S(1)} %slice.149, f32[1,17,16]{1,2,0:T(8,128)S(1)} %bitcast_select_fusion), kind=kOutput, calls=%fused_computation.38 | convolution fusion | flops 25559040 | bytes 820352 | tf_op jit(solution)/shard_map/gij,gjf->gif/dot_general | solution.py:86
  51.5 0.8 copy.60
  52.3 4.3 %all-to-all-start.1 = ((bf16[16,1,64,128]{3,2,1,0:T(8,128)(2,1)}), bf16[16,1,64,128]{3,2,1,0:T(8,128)(2,1)S(1)}, u32[]{:S(2)}, u32[]{:S(2)}) async-start(bf16[16,1,64,128]{3,2,1,0:T(8,128)(2,1)} %bitcast.14), calls=%async_computation.1 | async-start | bytes 524288 | tf_op jit(solution)/shard_map/all_to_all | solution.py:89
  56.6 0.0 copy-done.1
  56.6 0.2 fusion.28
  56.8 0.0 copy-start.8
  56.8 2.3 %fusion.6 = f32[256,16,64]{0,2,1:T(8,128)} fusion(f32[256,256]{1,0:T(8,128)S(1)} %fusion.28, f32[16,256]{1,0:T(8,128)S(1)} %get-tuple-element.18, pred[256,256]{1,0:T(8,128)(4,1)S(1)} %fusion.24, f32[256,16,64]{0,2,1:T(8,128)S(1)} %bitcast.72, f32[256,16]{0,1:T(8,128)S(1)} %copy-done.3), kind=kOutput, calls=%fused_computation.7 | convolution fusion | flops 139984896 | bytes 2457600 | tf_op jit(solution)/shard_map/hts,shp->thp/dot_general | solution.py:59
  59.1 8.6 %all-to-all-done.1 = bf16[16,1,64,128]{3,2,1,0:T(8,128)(2,1)S(1)} async-done(((bf16[16,1,64,128]{3,2,1,0:T(8,128)(2,1)}), bf16[16,1,64,128]{3,2,1,0:T(8,128)(2,1)S(1)}, u32[]{:S(2)}, u32[]{:S(2)}) %all-to-all-start.1) | async-done | bytes 262176 | tf_op jit(solution)/shard_map/all_to_all | solution.py:89
  67.7 0.0 copy-done.8
  67.7 1.6 %fusion.8 = f32[256,16,64]{0,2,1:T(8,128)S(1)} fusion(f32[256,16,64]{0,2,1:T(8,128)} %fusion.6, f32[256,16,64]{0,2,1:T(8,128)S(1)} %bitcast.73, f32[16]{0:T(128)S(1)} %copy-done.8, f32[256,16]{0,1:T(8,128)S(1)} %get-tuple-element.16, bf16[16,1,64,128]{3,2,1,0:T(8,128)(2,1)S(1)} %all-to-all-done.1, bf16[256,1280]{1,0:T(8,128)(2,1)} %copy-done.1), kind=kOutput, calls=%fused_computation.10 | convolution fusion | flops 68157440 | bytes 3489856 | tf_op jit(solution)/shard_map/tn,hpn->thp/dot_general | solution.py:94
  69.3 0.3 copy.55
  69.6 0.0 copy-start.6
  69.6 0.2 multiply_reduce_fusion
  69.9 9.4 %all_to_all.20 = f32[4,1,256]{2,1,0:T(1,128)S(1)} all-to-all(f32[4,1,256]{2,1,0:T(1,128)S(1)} %broadcast_in_dim.113), channel_id=1, replica_groups=mesh['row'=8,'seg'=16,'head'=4] {'head'}, dimensions={0} | all-to-all | bytes 8192 | tf_op jit(solution)/shard_map/all_to_all | solution.py:101
  79.3 0.9 %multiply_convert_fusion.5 = bf16[256,1024]{1,0:T(8,128)(2,1)} fusion(f32[256,1024]{1,0:T(8,128)S(1)} %get-tuple-element.14, f32[1024]{0:T(1024)S(1)} %copy-done.6, f32[256]{0:T(256)S(1)} %bitcast.78), kind=kLoop, calls=%fused_computation.17 | loop fusion | flops 786432 | bytes 1577984 | tf_op jit(solution)/shard_map/convert_element_type | solution.py:106
  (19 shorter events, 0.2 us)
Async XLA Ops:
  0.0 4.0 %copy-start = (f32[256,16]{0,1:T(8,128)S(1)}, f32[256,16]{0,1:T(8,128)}, u32[]{:S(2)}) copy-start(f32[256,16]{0,1:T(8,128)} %param.14) | copy-start | bytes 49156
  0.0 5.2 %copy-start.4 = (s32[256]{0:T(256)S(1)}, s32[256]{0:T(256)}, u32[]{:S(2)}) copy-start(s32[256]{0:T(256)} %param.15) | copy-start | bytes 3076
  0.0 2.0 %copy-start.2 = (bf16[256,256]{1,0:T(8,128)(2,1)S(1)}, bf16[256,256]{1,0:T(8,128)(2,1)}, u32[]{:S(2)}) copy-start(bf16[256,256]{1,0:T(8,128)(2,1)} %param.11) | copy-start | bytes 393220
  0.0 4.8 %copy-start.5 = (f32[4,1024]{1,0:T(4,128)S(1)}, f32[4,1024]{1,0:T(4,128)}, u32[]{:S(2)}) copy-start(f32[4,1024]{1,0:T(4,128)} %param.16) | copy-start | bytes 49156
  0.0 4.8 %copy-start.7 = (f32[4,256]{1,0:T(4,128)S(1)}, f32[4,256]{1,0:T(4,128)}, u32[]{:S(2)}) copy-start(f32[4,256]{1,0:T(4,128)} %param.17) | copy-start | bytes 12292
  2.1 11.6 %collective-permute-start = (bf16[3,1281]{1,0:T(4,128)(2,1)S(1)}, bf16[3,1281]{1,0:T(4,128)(2,1)S(1)}, u32[]{:S(2)}, u32[]{:S(2)}) collective-permute-start(bf16[3,1281]{1,0:T(4,128)(2,1)S(1)} %pad_maximum_fusion.2), channel_id=1, source_target_pairs={{0,4},{4,8},{8,12},{12,16},{16,20},{20,24},{24,28},{28,32},{32,36}... | collective-permute-start | bytes 23066 | tf_op jit(solution)/shard_map/ppermute | solution.py:18
  18.5 38.0 %copy-start.1 = (bf16[256,1280]{1,0:T(8,128)(2,1)}, bf16[256,1280]{1,0:T(8,128)(2,1)S(1)}, u32[]{:S(2)}) copy-start(bf16[256,1280]{1,0:T(8,128)(2,1)S(1)} %multiply_convert_fusion.4) | copy-start | bytes 1966084
  18.7 0.8 copy-start.3
  21.3 21.1 %all-to-all-start = ((f32[16,1,8320]{2,1,0:T(1,128)}), f32[16,1,8320]{2,1,0:T(1,128)S(1)}, u32[]{:S(2)}, u32[]{:S(2)}) async-start(f32[16,1,8320]{2,1,0:T(1,128)} %all_to_all.13), calls=%async_computation | async-start | bytes 1064960 | tf_op jit(solution)/shard_map/all_to_all | solution.py:72
  43.7 7.0 %collective-permute-start.1 = (f32[1,8192]{1,0:T(1,128)S(1)}, f32[1,8192]{1,0:T(1,128)S(1)}, u32[]{:S(2)}, u32[]{:S(2)}) collective-permute-start(f32[1,8192]{1,0:T(1,128)S(1)} %fusion.17), channel_id=1, source_target_pairs={{0,64},{64,128},{128,192},{192,256},{256,320},{320,384},{384,448},... | collective-permute-start | bytes 98312 | tf_op jit(solution)/shard_map/ppermute | solution.py:18
  52.3 15.4 %all-to-all-start.1 = ((bf16[16,1,64,128]{3,2,1,0:T(8,128)(2,1)}), bf16[16,1,64,128]{3,2,1,0:T(8,128)(2,1)S(1)}, u32[]{:S(2)}, u32[]{:S(2)}) async-start(bf16[16,1,64,128]{3,2,1,0:T(8,128)(2,1)} %bitcast.14), calls=%async_computation.1 | async-start | bytes 524288 | tf_op jit(solution)/shard_map/all_to_all | solution.py:89
  56.8 10.9 %copy-start.8 = (f32[16]{0:T(128)S(1)}, f32[16]{0:T(128)}, u32[]{:S(2)}) copy-start(f32[16]{0:T(128)} %param.18) | copy-start | bytes 196
  69.6 9.6 %copy-start.6 = (f32[1024]{0:T(1024)S(1)}, f32[1024]{0:T(1024)}, u32[]{:S(2)}) copy-start(f32[1024]{0:T(1024)} %param.19) | copy-start | bytes 12292

commit v10 on v9

--- a/solution.py
+++ b/solution.py
@@ -63,7 +63,7 @@
     ends = jnp.where((doc_ids == doc_ids[-1])[:, None], jnp.exp(cum[-1][None, :] - cum), 0.0)
     written = (xdt.astype(jnp.float32) * ends[:, :, None]).astype(jnp.bfloat16)
     local = jnp.einsum("shp,sn->hpn", written, bconv, preferred_element_type=jnp.float32)
-    through = jnp.exp(cum[-1]) * cont[-1]
+    through = jnp.where(doc_ids[-1] == previous, jnp.exp(cum[-1]), 0.0)
 
     flat = head_size * states
     payload = jnp.concatenate(

time: 80.8 us -> 80.1 us (level)
  no operation moved by 1% of the time
where the time goes in v10:
time: 80.1 us; the launch traced here: 79.5 us
  waiting for transfers between devices  35.5 us (44%)
  starting transfers between devices  13.7 us (17%)
  blocking collectives  9.39 us (12%)
  other arithmetic  6.72 us (8%)
  local copies, waits for them, and re-layouts  6.62 us (8%)
  matrix products  5.88 us (7%)
  between operations  1.68 us (2%)
    all_to_all x1, waiting for transfers between devices, body(): lax.all_to_all(payload, 'seg', 0, 0, tiled=True)  14.6 us
    ppermute x2, waiting for transfers between devices, shifted(): return lax.ppermute(block, axis, route)  12.3 us
    all_to_all x1, blocking collectives, body(): lax.all_to_all(jnp.broadcast_to(own[None], (ways, own.shape[0])), 'head',...  9.39 us
    all_to_all x1, waiting for transfers between devices, body(): lax.all_to_all(entering.astype(jnp.bfloat16), 'seg', 0, 0, tiled=True)  8.61 us
    all_to_all x1, starting transfers between devices, body(): lax.all_to_all(payload, 'seg', 0, 0, tiled=True)  4.97 us
    ppermute x2, starting transfers between devices, shifted(): return lax.ppermute(block, axis, route)  4.51 us
    all_to_all x1, starting transfers between devices, body(): lax.all_to_all(entering.astype(jnp.bfloat16), 'seg', 0, 0, tiled=True)  4.25 us
    unnamed x22, local copies, waits for them, and re-layouts  2.49 us
  transfers between devices with their start and end apart: 4, of which 4 were waited for; matrix products, arithmetic and copies ran while one was open for 7% of the time, Pallas kernels for 0%

profile of v10, /device:TPU:32, one launch (start us, length us, event | category | flops | bytes accessed | tf_op | source)
XLA Modules:
  0.0 79.5 jit_solution(783447604144106297)
XLA Ops:
  0.0 0.0 copy-start
  0.0 0.0 copy-start.4
  0.0 0.0 copy-start.5
  0.0 0.0 copy-start.7
  0.0 0.7 broadcast_add_fusion
  0.8 0.1 slice_bitcast_fusion.4
  0.9 0.1 copy.50
  1.0 1.1 %constant_dynamic-update-slice_fusion.3 = bf16[256,1280]{1,0:T(8,128)(2,1)S(1)} fusion(bf16[256,1024]{1,0:T(8,128)(2,1)} %param.10), kind=kLoop, calls=%fused_computation.60 | loop fusion | bytes 1048576
  2.0 0.0 copy-done.2
  2.1 1.9 %collective-permute-start = (bf16[3,1281]{1,0:T(4,128)(2,1)S(1)}, bf16[3,1281]{1,0:T(4,128)(2,1)S(1)}, u32[]{:S(2)}, u32[]{:S(2)}) collective-permute-start(bf16[3,1281]{1,0:T(4,128)(2,1)S(1)} %pad_maximum_fusion.2), channel_id=1, source_target_pairs={{0,4},{4,8},{8,12},{12,16},{16,20},{20,24},{24,28},{28,32},{32,36}... | collective-permute-start | bytes 23066 | tf_op jit(solution)/shard_map/ppermute | solution.py:18
  4.0 0.0 copy-done
  4.1 0.6 reduce-window.6
  4.6 0.2 slice_reduce_fusion
  4.9 0.0 copy-done.5
  4.9 0.0 copy-done.7
  4.9 0.1 slice_reduce_fusion.7
  4.9 0.1 fusion.39
  5.0 0.2 slice_reduce_fusion.3
  5.2 0.0 copy-done.4
  5.2 0.6 slice.117
  5.8 8.0 %collective-permute-done = bf16[3,1281]{1,0:T(4,128)(2,1)S(1)} collective-permute-done((bf16[3,1281]{1,0:T(4,128)(2,1)S(1)}, bf16[3,1281]{1,0:T(4,128)(2,1)S(1)}, u32[]{:S(2)}, u32[]{:S(2)}) %collective-permute-start) | collective-permute-done | bytes 7718 | tf_op jit(solution)/shard_map/ppermute | solution.py:18
  13.8 0.6 slice.119
  14.3 0.1 fusion.36
  14.5 0.1 pad_add_fusion
  15.9 0.7 compare_convert_fusion.3
  16.6 1.2 %multiply_convert_fusion.4 = bf16[256,1280]{1,0:T(8,128)(2,1)S(1)} fusion(bf16[256,1280]{1,0:T(8,128)(2,1)S(1)} %constant_dynamic-update-slice_fusion.2, bf16[3,1280]{1,0:T(4,128)(2,1)S(1)} %slice.131, f32[256]{0:T(256)S(1)} %get-tuple-element.20, f32[1280]{0:T(1024)S(1)} %get-tuple-element.10, f32[256]{0:T(256)S(1)} %get-tuple-element.21, ...), kind=kLoop, calls=%fused_computation.13 | loop fusion | flops 9175040 | bytes 1341952 | tf_op jit(solution)/shard_map/convert_element_type | solution.py:45
  17.9 0.0 copy-start.1
  17.9 0.1 slice_convert_fusion
  18.0 0.0 copy-start.3
  18.0 0.3 copy.51
  18.4 0.1 exponential_select_fusion
  18.5 0.3 copy-done.3
  18.8 0.3 fusion.14
  19.1 0.3 copy.80
  19.4 0.1 broadcast_in_dim.73
  19.5 1.2 %all_to_all.13 = f32[16,1,8320]{2,1,0:T(1,128)} reshape(f32[16,8320]{1,0:T(8,128)S(1)} %pad_maximum_fusion.1) | data formatting | bytes 1064960 | tf_op jit(solution)/shard_map/all_to_all | solution.py:72
  20.6 5.0 %all-to-all-start = ((f32[16,1,8320]{2,1,0:T(1,128)}), f32[16,1,8320]{2,1,0:T(1,128)S(1)}, u32[]{:S(2)}, u32[]{:S(2)}) async-start(f32[16,1,8320]{2,1,0:T(1,128)} %all_to_all.13), calls=%async_computation | async-start | bytes 1064960 | tf_op jit(solution)/shard_map/all_to_all | solution.py:72
  25.6 0.1 fusion.24
  25.8 1.3 %convert_multiply_fusion = f32[256,1024]{1,0:T(8,128)S(1)} fusion(bf16[256,1024]{1,0:T(8,128)(2,1)} %param.12), kind=kLoop, calls=%fused_computation.11 | loop fusion | flops 1310720 | bytes 1572864 | tf_op jit(solution)/shard_map/jit(silu)/mul | solution.py:60
  27.1 14.6 %all-to-all-done = f32[16,1,8320]{2,1,0:T(1,128)S(1)} async-done(((f32[16,1,8320]{2,1,0:T(1,128)}), f32[16,1,8320]{2,1,0:T(1,128)S(1)}, u32[]{:S(2)}, u32[]{:S(2)}) %all-to-all-start) | async-done | bytes 532512 | tf_op jit(solution)/shard_map/all_to_all | solution.py:72
  41.7 0.2 slice_reduce_fusion.2
  41.9 0.1 select_reduce_fusion
  42.1 0.2 slice_reduce_fusion.1
  42.3 0.1 slice.146
  42.3 0.7 fusion.17
  43.0 2.6 %collective-permute-start.1 = (f32[1,8192]{1,0:T(1,128)S(1)}, f32[1,8192]{1,0:T(1,128)S(1)}, u32[]{:S(2)}, u32[]{:S(2)}) collective-permute-start(f32[1,8192]{1,0:T(1,128)S(1)} %fusion.17), channel_id=1, source_target_pairs={{0,64},{64,128},{128,192},{192,256},{256,320},{320,384},{384,448},... | collective-permute-start | bytes 98312 | tf_op jit(solution)/shard_map/ppermute | solution.py:18
  45.6 0.1 select_reduce_fusion.1
  45.7 4.3 %collective-permute-done.1 = f32[1,8192]{1,0:T(1,128)S(1)} collective-permute-done((f32[1,8192]{1,0:T(1,128)S(1)}, f32[1,8192]{1,0:T(1,128)S(1)}, u32[]{:S(2)}, u32[]{:S(2)}) %collective-permute-start.1) | collective-permute-done | bytes 32800 | tf_op jit(solution)/shard_map/ppermute | solution.py:18
  50.0 0.9 %fusion.22 = bf16[2,8,64,128]{3,1,2,0:T(8,128)(2,1)S(1)} fusion(f32[8192]{0:T(1024)S(1)} %bitcast.76, f32[16]{0:T(128)S(1)} %select_reduce_fusion.1, f32[16,1,8192]{2,1,0:T(1,128)S(1)} %slice.146, f32[1,17,16]{1,2,0:T(8,128)S(1)} %bitcast_select_fusion), kind=kOutput, calls=%fused_computation.38 | convolution fusion | flops 25559040 | bytes 820352 | tf_op jit(solution)/shard_map/gij,gjf->gif/dot_general | solution.py:86
  50.9 0.8 copy.60
  51.6 4.3 %all-to-all-start.1 = ((bf16[16,1,64,128]{3,2,1,0:T(8,128)(2,1)}), bf16[16,1,64,128]{3,2,1,0:T(8,128)(2,1)S(1)}, u32[]{:S(2)}, u32[]{:S(2)}) async-start(bf16[16,1,64,128]{3,2,1,0:T(8,128)(2,1)} %bitcast.13), calls=%async_computation.1 | async-start | bytes 524288 | tf_op jit(solution)/shard_map/all_to_all | solution.py:89
  55.9 0.0 copy-done.1
  55.9 0.2 fusion.28
  56.1 0.0 copy-start.8
  56.1 2.3 %fusion.6 = f32[256,16,64]{0,2,1:T(8,128)} fusion(f32[256,256]{1,0:T(8,128)S(1)} %fusion.28, f32[16,256]{1,0:T(8,128)S(1)} %get-tuple-element.18, pred[256,256]{1,0:T(8,128)(4,1)S(1)} %fusion.24, f32[256,16,64]{0,2,1:T(8,128)S(1)} %bitcast.71, f32[256,16]{0,1:T(8,128)S(1)} %copy-done.3), kind=kOutput, calls=%fused_computation.7 | convolution fusion | flops 139984896 | bytes 2457600 | tf_op jit(solution)/shard_map/hts,shp->thp/dot_general | solution.py:59
  58.4 8.6 %all-to-all-done.1 = bf16[16,1,64,128]{3,2,1,0:T(8,128)(2,1)S(1)} async-done(((bf16[16,1,64,128]{3,2,1,0:T(8,128)(2,1)}), bf16[16,1,64,128]{3,2,1,0:T(8,128)(2,1)S(1)}, u32[]{:S(2)}, u32[]{:S(2)}) %all-to-all-start.1) | async-done | bytes 262176 | tf_op jit(solution)/shard_map/all_to_all | solution.py:89
  67.0 0.0 copy-done.8
  67.0 1.6 %fusion.8 = f32[256,16,64]{0,2,1:T(8,128)S(1)} fusion(f32[256,16,64]{0,2,1:T(8,128)} %fusion.6, f32[256,16,64]{0,2,1:T(8,128)S(1)} %bitcast.72, f32[16]{0:T(128)S(1)} %copy-done.8, f32[256,16]{0,1:T(8,128)S(1)} %get-tuple-element.16, bf16[16,1,64,128]{3,2,1,0:T(8,128)(2,1)S(1)} %all-to-all-done.1, bf16[256,1280]{1,0:T(8,128)(2,1)} %copy-done.1), kind=kOutput, calls=%fused_computation.10 | convolution fusion | flops 68157440 | bytes 3489856 | tf_op jit(solution)/shard_map/tn,hpn->thp/dot_general | solution.py:94
  68.6 0.3 copy.55
  69.0 0.0 copy-start.6
  69.0 0.2 multiply_reduce_fusion
  69.2 9.4 %all_to_all.20 = f32[4,1,256]{2,1,0:T(1,128)S(1)} all-to-all(f32[4,1,256]{2,1,0:T(1,128)S(1)} %broadcast_in_dim.118), channel_id=1, replica_groups=mesh['row'=8,'seg'=16,'head'=4] {'head'}, dimensions={0} | all-to-all | bytes 8192 | tf_op jit(solution)/shard_map/all_to_all | solution.py:101
  78.6 0.0 copy-done.6
  78.6 0.9 %multiply_convert_fusion.5 = bf16[256,1024]{1,0:T(8,128)(2,1)} fusion(f32[256,1024]{1,0:T(8,128)S(1)} %get-tuple-element.14, f32[1024]{0:T(1024)S(1)} %copy-done.6, f32[256]{0:T(256)S(1)} %bitcast.77), kind=kLoop, calls=%fused_computation.17 | loop fusion | flops 786432 | bytes 1577984 | tf_op jit(solution)/shard_map/convert_element_type | solution.py:106
  (18 shorter events, 0.2 us)
Async XLA Ops:
  0.0 4.0 %copy-start = (f32[256,16]{0,1:T(8,128)S(1)}, f32[256,16]{0,1:T(8,128)}, u32[]{:S(2)}) copy-start(f32[256,16]{0,1:T(8,128)} %param.14) | copy-start | bytes 49156
  0.0 5.2 %copy-start.4 = (s32[256]{0:T(256)S(1)}, s32[256]{0:T(256)}, u32[]{:S(2)}) copy-start(s32[256]{0:T(256)} %param.15) | copy-start | bytes 3076
  0.0 2.0 %copy-start.2 = (bf16[256,256]{1,0:T(8,128)(2,1)S(1)}, bf16[256,256]{1,0:T(8,128)(2,1)}, u32[]{:S(2)}) copy-start(bf16[256,256]{1,0:T(8,128)(2,1)} %param.11) | copy-start | bytes 393220
  0.0 4.8 %copy-start.5 = (f32[4,1024]{1,0:T(4,128)S(1)}, f32[4,1024]{1,0:T(4,128)}, u32[]{:S(2)}) copy-start(f32[4,1024]{1,0:T(4,128)} %param.16) | copy-start | bytes 49156
  0.0 4.8 %copy-start.7 = (f32[4,256]{1,0:T(4,128)S(1)}, f32[4,256]{1,0:T(4,128)}, u32[]{:S(2)}) copy-start(f32[4,256]{1,0:T(4,128)} %param.17) | copy-start | bytes 12292
  2.1 11.6 %collective-permute-start = (bf16[3,1281]{1,0:T(4,128)(2,1)S(1)}, bf16[3,1281]{1,0:T(4,128)(2,1)S(1)}, u32[]{:S(2)}, u32[]{:S(2)}) collective-permute-start(bf16[3,1281]{1,0:T(4,128)(2,1)S(1)} %pad_maximum_fusion.2), channel_id=1, source_target_pairs={{0,4},{4,8},{8,12},{12,16},{16,20},{20,24},{24,28},{28,32},{32,36}... | collective-permute-start | bytes 23066 | tf_op jit(solution)/shard_map/ppermute | solution.py:18
  17.9 38.0 %copy-start.1 = (bf16[256,1280]{1,0:T(8,128)(2,1)}, bf16[256,1280]{1,0:T(8,128)(2,1)S(1)}, u32[]{:S(2)}) copy-start(bf16[256,1280]{1,0:T(8,128)(2,1)S(1)} %multiply_convert_fusion.4) | copy-start | bytes 1966084
  18.0 0.8 copy-start.3
  20.6 21.1 %all-to-all-start = ((f32[16,1,8320]{2,1,0:T(1,128)}), f32[16,1,8320]{2,1,0:T(1,128)S(1)}, u32[]{:S(2)}, u32[]{:S(2)}) async-start(f32[16,1,8320]{2,1,0:T(1,128)} %all_to_all.13), calls=%async_computation | async-start | bytes 1064960 | tf_op jit(solution)/shard_map/all_to_all | solution.py:72
  43.0 7.0 %collective-permute-start.1 = (f32[1,8192]{1,0:T(1,128)S(1)}, f32[1,8192]{1,0:T(1,128)S(1)}, u32[]{:S(2)}, u32[]{:S(2)}) collective-permute-start(f32[1,8192]{1,0:T(1,128)S(1)} %fusion.17), channel_id=1, source_target_pairs={{0,64},{64,128},{128,192},{192,256},{256,320},{320,384},{384,448},... | collective-permute-start | bytes 98312 | tf_op jit(solution)/shard_map/ppermute | solution.py:18
  51.6 15.4 %all-to-all-start.1 = ((bf16[16,1,64,128]{3,2,1,0:T(8,128)(2,1)}), bf16[16,1,64,128]{3,2,1,0:T(8,128)(2,1)S(1)}, u32[]{:S(2)}, u32[]{:S(2)}) async-start(bf16[16,1,64,128]{3,2,1,0:T(8,128)(2,1)} %bitcast.13), calls=%async_computation.1 | async-start | bytes 524288 | tf_op jit(solution)/shard_map/all_to_all | solution.py:89
  56.1 10.9 %copy-start.8 = (f32[16]{0:T(128)S(1)}, f32[16]{0:T(128)}, u32[]{:S(2)}) copy-start(f32[16]{0:T(128)} %param.18) | copy-start | bytes 196
  69.0 9.6 %copy-start.6 = (f32[1024]{0:T(1024)S(1)}, f32[1024]{0:T(1024)}, u32[]{:S(2)}) copy-start(f32[1024]{0:T(1024)} %param.19) | copy-start | bytes 12292

commit v11 on v10

--- a/solution.py
+++ b/solution.py
@@ -60,10 +60,11 @@
     inners, gate = lax.optimization_barrier((inners, jax.nn.silu(gate_z.astype(jnp.float32))))
     cont = (doc_ids == previous).astype(jnp.float32)
     entries = jnp.exp(cum) * cont[:, None]
-    ends = jnp.where((doc_ids == doc_ids[-1])[:, None], jnp.exp(cum[-1][None, :] - cum), 0.0)
+    last_doc = jnp.max(doc_ids)
+    ends = jnp.where((doc_ids == last_doc)[:, None], jnp.exp(cum[-1][None, :] - cum), 0.0)
     written = (xdt.astype(jnp.float32) * ends[:, :, None]).astype(jnp.bfloat16)
     local = jnp.einsum("shp,sn->hpn", written, bconv, preferred_element_type=jnp.float32)
-    through = jnp.where(doc_ids[-1] == previous, jnp.exp(cum[-1]), 0.0)
+    through = jnp.where(last_doc == previous, jnp.exp(cum[-1]), 0.0)
 
     flat = head_size * states
     payload = jnp.concatenate(

time: 80.1 us -> 80.8 us (level)
    reduce_max x0 -> x1, other arithmetic: none -> 1.39 us  [body(): last_doc = jnp.max(doc_ids)]
  transfers between devices with their start and end apart: 4 -> 4, of which waited for: 4 -> 4; matrix products, arithmetic and copies ran while one was open for 7% -> 6% of each run, Pallas kernels for 0% -> 0%
where the time goes in v11:
time: 80.8 us; the launch traced here: 80.2 us
  waiting for transfers between devices  36.1 us (45%)
  starting transfers between devices  13.7 us (17%)
  blocking collectives  9.37 us (12%)
  other arithmetic  7.36 us (9%)
  local copies, waits for them, and re-layouts  6.04 us (7%)
  matrix products  5.87 us (7%)
  between operations  1.68 us (2%)
    all_to_all x1, waiting for transfers between devices, body(): lax.all_to_all(payload, 'seg', 0, 0, tiled=True)  14.6 us
    ppermute x2, waiting for transfers between devices, shifted(): return lax.ppermute(block, axis, route)  12.9 us
    all_to_all x1, blocking collectives, body(): lax.all_to_all(jnp.broadcast_to(own[None], (ways, own.shape[0])), 'head',...  9.37 us
    all_to_all x1, waiting for transfers between devices, body(): lax.all_to_all(entering.astype(jnp.bfloat16), 'seg', 0, 0, tiled=True)  8.61 us
    all_to_all x1, starting transfers between devices, body(): lax.all_to_all(payload, 'seg', 0, 0, tiled=True)  4.97 us
    ppermute x2, starting transfers between devices, shifted(): return lax.ppermute(block, axis, route)  4.51 us
    all_to_all x1, starting transfers between devices, body(): lax.all_to_all(entering.astype(jnp.bfloat16), 'seg', 0, 0, tiled=True)  4.26 us
    unnamed x22, local copies, waits for them, and re-layouts  2.49 us
  transfers between devices with their start and end apart: 4, of which 4 were waited for; matrix products, arithmetic and copies ran while one was open for 6% of the time, Pallas kernels for 0%

profile of v11, /device:TPU:32, one launch (start us, length us, event | category | flops | bytes accessed | tf_op | source)
XLA Modules:
  0.0 80.2 jit_solution(9200445613071463293)
XLA Ops:
  0.0 0.0 copy-start
  0.0 0.0 copy-start.4
  0.0 0.0 copy-start.2
  0.0 0.0 copy-start.5
  0.0 0.0 copy-start.7
  0.0 1.4 %fusion.40 = (s32[]{:T(128)}, bf16[256]{0:T(256)(128)(2,1)S(1)}, s32[256]{0:T(256)S(1)}) fusion(s32[256]{0:T(256)} %param.15), kind=kLoop, calls=%fused_computation.95 | loop fusion | flops 767 | bytes 2564 | tf_op jit(solution)/shard_map/reduce_max | solution.py:63
  1.4 0.1 slice_bitcast_fusion.4
  1.5 0.1 copy.50
  1.6 1.1 %constant_dynamic-update-slice_fusion.3 = bf16[256,1280]{1,0:T(8,128)(2,1)S(1)} fusion(bf16[256,1024]{1,0:T(8,128)(2,1)} %param.10), kind=kLoop, calls=%fused_computation.60 | loop fusion | bytes 1048576
  2.7 0.0 copy-done.2
  2.7 1.9 %collective-permute-start = (bf16[3,1281]{1,0:T(4,128)(2,1)S(1)}, bf16[3,1281]{1,0:T(4,128)(2,1)S(1)}, u32[]{:S(2)}, u32[]{:S(2)}) collective-permute-start(bf16[3,1281]{1,0:T(4,128)(2,1)S(1)} %pad_maximum_fusion.2), channel_id=1, source_target_pairs={{0,4},{4,8},{8,12},{12,16},{16,20},{20,24},{24,28},{28,32},{32,36}... | collective-permute-start | bytes 23066 | tf_op jit(solution)/shard_map/ppermute | solution.py:18
  4.7 0.0 copy-done
  4.7 0.6 reduce-window.6
  5.3 0.2 slice_reduce_fusion
  5.5 0.0 copy-done.5
  5.5 0.0 copy-done.7
  5.5 0.1 slice_reduce_fusion.7
  5.6 0.1 fusion.39
  5.7 0.2 slice_reduce_fusion.3
  5.8 8.5 %collective-permute-done = bf16[3,1281]{1,0:T(4,128)(2,1)S(1)} collective-permute-done((bf16[3,1281]{1,0:T(4,128)(2,1)S(1)}, bf16[3,1281]{1,0:T(4,128)(2,1)S(1)}, u32[]{:S(2)}, u32[]{:S(2)}) %collective-permute-start) | collective-permute-done | bytes 7718 | tf_op jit(solution)/shard_map/ppermute | solution.py:18
  14.4 0.6 slice.114
  15.0 0.1 fusion.36
  15.1 0.1 pad_add_fusion
  16.5 0.0 copy-done.4
  16.5 0.7 compare_convert_fusion.3
  17.3 1.2 %multiply_convert_fusion.4 = bf16[256,1280]{1,0:T(8,128)(2,1)S(1)} fusion(bf16[256,1280]{1,0:T(8,128)(2,1)S(1)} %constant_dynamic-update-slice_fusion.2, bf16[3,1280]{1,0:T(4,128)(2,1)S(1)} %slice.126, f32[256]{0:T(256)S(1)} %get-tuple-element.20, f32[1280]{0:T(1024)S(1)} %get-tuple-element.10, f32[256]{0:T(256)S(1)} %get-tuple-element.21, ...), kind=kLoop, calls=%fused_computation.13 | loop fusion | flops 9175040 | bytes 1341952 | tf_op jit(solution)/shard_map/convert_element_type | solution.py:45
  18.5 0.0 copy-start.1
  18.5 0.1 slice_convert_fusion
  18.6 0.0 copy-start.3
  18.7 0.3 copy.51
  19.0 0.1 exponential_select_fusion
  19.1 0.3 copy-done.3
  19.4 0.3 fusion.14
  19.7 0.3 copy.80
  20.0 0.1 broadcast_in_dim.73
  20.1 1.2 %all_to_all.13 = f32[16,1,8320]{2,1,0:T(1,128)} reshape(f32[16,8320]{1,0:T(8,128)S(1)} %pad_maximum_fusion.1) | data formatting | bytes 1064960 | tf_op jit(solution)/shard_map/all_to_all | solution.py:73
  21.3 5.0 %all-to-all-start = ((f32[16,1,8320]{2,1,0:T(1,128)}), f32[16,1,8320]{2,1,0:T(1,128)S(1)}, u32[]{:S(2)}, u32[]{:S(2)}) async-start(f32[16,1,8320]{2,1,0:T(1,128)} %all_to_all.13), calls=%async_computation | async-start | bytes 1064960 | tf_op jit(solution)/shard_map/all_to_all | solution.py:73
  26.3 0.1 fusion.24
  26.4 1.3 %convert_multiply_fusion = f32[256,1024]{1,0:T(8,128)S(1)} fusion(bf16[256,1024]{1,0:T(8,128)(2,1)} %param.12), kind=kLoop, calls=%fused_computation.11 | loop fusion | flops 1310720 | bytes 1572864 | tf_op jit(solution)/shard_map/jit(silu)/mul | solution.py:60
  27.7 14.6 %all-to-all-done = f32[16,1,8320]{2,1,0:T(1,128)S(1)} async-done(((f32[16,1,8320]{2,1,0:T(1,128)}), f32[16,1,8320]{2,1,0:T(1,128)S(1)}, u32[]{:S(2)}, u32[]{:S(2)}) %all-to-all-start) | async-done | bytes 532512 | tf_op jit(solution)/shard_map/all_to_all | solution.py:73
  42.4 0.2 slice_reduce_fusion.2
  42.6 0.1 select_reduce_fusion
  42.7 0.2 slice_reduce_fusion.1
  42.9 0.1 slice.141
  43.0 0.7 fusion.17
  43.6 2.6 %collective-permute-start.1 = (f32[1,8192]{1,0:T(1,128)S(1)}, f32[1,8192]{1,0:T(1,128)S(1)}, u32[]{:S(2)}, u32[]{:S(2)}) collective-permute-start(f32[1,8192]{1,0:T(1,128)S(1)} %fusion.17), channel_id=1, source_target_pairs={{0,64},{64,128},{128,192},{192,256},{256,320},{320,384},{384,448},... | collective-permute-start | bytes 98312 | tf_op jit(solution)/shard_map/ppermute | solution.py:18
  46.2 0.1 select_reduce_fusion.1
  46.3 4.3 %collective-permute-done.1 = f32[1,8192]{1,0:T(1,128)S(1)} collective-permute-done((f32[1,8192]{1,0:T(1,128)S(1)}, f32[1,8192]{1,0:T(1,128)S(1)}, u32[]{:S(2)}, u32[]{:S(2)}) %collective-permute-start.1) | collective-permute-done | bytes 32800 | tf_op jit(solution)/shard_map/ppermute | solution.py:18
  50.6 0.9 %fusion.22 = bf16[2,8,64,128]{3,1,2,0:T(8,128)(2,1)S(1)} fusion(f32[8192]{0:T(1024)S(1)} %bitcast.75, f32[16]{0:T(128)S(1)} %select_reduce_fusion.1, f32[16,1,8192]{2,1,0:T(1,128)S(1)} %slice.141, f32[1,17,16]{1,2,0:T(8,128)S(1)} %bitcast_select_fusion), kind=kOutput, calls=%fused_computation.38 | convolution fusion | flops 25559040 | bytes 820352 | tf_op jit(solution)/shard_map/gij,gjf->gif/dot_general | solution.py:87
  51.5 0.8 copy.60
  52.3 4.3 %all-to-all-start.1 = ((bf16[16,1,64,128]{3,2,1,0:T(8,128)(2,1)}), bf16[16,1,64,128]{3,2,1,0:T(8,128)(2,1)S(1)}, u32[]{:S(2)}, u32[]{:S(2)}) async-start(bf16[16,1,64,128]{3,2,1,0:T(8,128)(2,1)} %bitcast.12), calls=%async_computation.1 | async-start | bytes 524288 | tf_op jit(solution)/shard_map/all_to_all | solution.py:90
  56.5 0.0 copy-done.1
  56.5 0.2 fusion.28
  56.7 0.0 copy-start.8
  56.7 2.3 %fusion.6 = f32[256,16,64]{0,2,1:T(8,128)} fusion(f32[256,256]{1,0:T(8,128)S(1)} %fusion.28, f32[16,256]{1,0:T(8,128)S(1)} %get-tuple-element.18, pred[256,256]{1,0:T(8,128)(4,1)S(1)} %fusion.24, f32[256,16,64]{0,2,1:T(8,128)S(1)} %bitcast.70, f32[256,16]{0,1:T(8,128)S(1)} %copy-done.3), kind=kOutput, calls=%fused_computation.7 | convolution fusion | flops 139984896 | bytes 2457600 | tf_op jit(solution)/shard_map/hts,shp->thp/dot_general | solution.py:59
  59.1 8.6 %all-to-all-done.1 = bf16[16,1,64,128]{3,2,1,0:T(8,128)(2,1)S(1)} async-done(((bf16[16,1,64,128]{3,2,1,0:T(8,128)(2,1)}), bf16[16,1,64,128]{3,2,1,0:T(8,128)(2,1)S(1)}, u32[]{:S(2)}, u32[]{:S(2)}) %all-to-all-start.1) | async-done | bytes 262176 | tf_op jit(solution)/shard_map/all_to_all | solution.py:90
  67.7 0.0 copy-done.8
  67.7 1.6 %fusion.8 = f32[256,16,64]{0,2,1:T(8,128)S(1)} fusion(f32[256,16,64]{0,2,1:T(8,128)} %fusion.6, f32[256,16,64]{0,2,1:T(8,128)S(1)} %bitcast.71, f32[16]{0:T(128)S(1)} %copy-done.8, f32[256,16]{0,1:T(8,128)S(1)} %get-tuple-element.16, bf16[16,1,64,128]{3,2,1,0:T(8,128)(2,1)S(1)} %all-to-all-done.1, bf16[256,1280]{1,0:T(8,128)(2,1)} %copy-done.1), kind=kOutput, calls=%fused_computation.10 | convolution fusion | flops 68157440 | bytes 3489856 | tf_op jit(solution)/shard_map/tn,hpn->thp/dot_general | solution.py:95
  69.3 0.3 copy.55
  69.6 0.0 copy-start.6
  69.6 0.2 multiply_reduce_fusion
  69.8 9.4 %all_to_all.20 = f32[4,1,256]{2,1,0:T(1,128)S(1)} all-to-all(f32[4,1,256]{2,1,0:T(1,128)S(1)} %broadcast_in_dim.118), channel_id=1, replica_groups=mesh['row'=8,'seg'=16,'head'=4] {'head'}, dimensions={0} | all-to-all | bytes 8192 | tf_op jit(solution)/shard_map/all_to_all | solution.py:102
  79.2 0.0 copy-done.6
  79.2 0.9 %multiply_convert_fusion.5 = bf16[256,1024]{1,0:T(8,128)(2,1)} fusion(f32[256,1024]{1,0:T(8,128)S(1)} %get-tuple-element.14, f32[1024]{0:T(1024)S(1)} %copy-done.6, f32[256]{0:T(256)S(1)} %bitcast.76), kind=kLoop, calls=%fused_computation.17 | loop fusion | flops 786432 | bytes 1577984 | tf_op jit(solution)/shard_map/convert_element_type | solution.py:107
  (17 shorter events, 0.2 us)
Async XLA Ops:
  0.0 4.7 %copy-start = (f32[256,16]{0,1:T(8,128)S(1)}, f32[256,16]{0,1:T(8,128)}, u32[]{:S(2)}) copy-start(f32[256,16]{0,1:T(8,128)} %param.14) | copy-start | bytes 49156
  0.0 16.5 %copy-start.4 = (s32[256]{0:T(256)S(1)}, s32[256]{0:T(256)}, u32[]{:S(2)}) copy-start(s32[256]{0:T(256)} %param.15) | copy-start | bytes 3076
  0.0 2.7 %copy-start.2 = (bf16[256,256]{1,0:T(8,128)(2,1)S(1)}, bf16[256,256]{1,0:T(8,128)(2,1)}, u32[]{:S(2)}) copy-start(bf16[256,256]{1,0:T(8,128)(2,1)} %param.11) | copy-start | bytes 393220
  0.0 5.5 %copy-start.5 = (f32[4,1024]{1,0:T(4,128)S(1)}, f32[4,1024]{1,0:T(4,128)}, u32[]{:S(2)}) copy-start(f32[4,1024]{1,0:T(4,128)} %param.16) | copy-start | bytes 49156
  0.0 5.5 %copy-start.7 = (f32[4,256]{1,0:T(4,128)S(1)}, f32[4,256]{1,0:T(4,128)}, u32[]{:S(2)}) copy-start(f32[4,256]{1,0:T(4,128)} %param.17) | copy-start | bytes 12292
  2.7 11.6 %collective-permute-start = (bf16[3,1281]{1,0:T(4,128)(2,1)S(1)}, bf16[3,1281]{1,0:T(4,128)(2,1)S(1)}, u32[]{:S(2)}, u32[]{:S(2)}) collective-permute-start(bf16[3,1281]{1,0:T(4,128)(2,1)S(1)} %pad_maximum_fusion.2), channel_id=1, source_target_pairs={{0,4},{4,8},{8,12},{12,16},{16,20},{20,24},{24,28},{28,32},{32,36}... | collective-permute-start | bytes 23066 | tf_op jit(solution)/shard_map/ppermute | solution.py:18
  18.5 38.0 %copy-start.1 = (bf16[256,1280]{1,0:T(8,128)(2,1)}, bf16[256,1280]{1,0:T(8,128)(2,1)S(1)}, u32[]{:S(2)}) copy-start(bf16[256,1280]{1,0:T(8,128)(2,1)S(1)} %multiply_convert_fusion.4) | copy-start | bytes 1966084
  18.6 0.8 copy-start.3
  21.3 21.1 %all-to-all-start = ((f32[16,1,8320]{2,1,0:T(1,128)}), f32[16,1,8320]{2,1,0:T(1,128)S(1)}, u32[]{:S(2)}, u32[]{:S(2)}) async-start(f32[16,1,8320]{2,1,0:T(1,128)} %all_to_all.13), calls=%async_computation | async-start | bytes 1064960 | tf_op jit(solution)/shard_map/all_to_all | solution.py:73
  43.6 7.0 %collective-permute-start.1 = (f32[1,8192]{1,0:T(1,128)S(1)}, f32[1,8192]{1,0:T(1,128)S(1)}, u32[]{:S(2)}, u32[]{:S(2)}) collective-permute-start(f32[1,8192]{1,0:T(1,128)S(1)} %fusion.17), channel_id=1, source_target_pairs={{0,64},{64,128},{128,192},{192,256},{256,320},{320,384},{384,448},... | collective-permute-start | bytes 98312 | tf_op jit(solution)/shard_map/ppermute | solution.py:18
  52.3 15.4 %all-to-all-start.1 = ((bf16[16,1,64,128]{3,2,1,0:T(8,128)(2,1)}), bf16[16,1,64,128]{3,2,1,0:T(8,128)(2,1)S(1)}, u32[]{:S(2)}, u32[]{:S(2)}) async-start(bf16[16,1,64,128]{3,2,1,0:T(8,128)(2,1)} %bitcast.12), calls=%async_computation.1 | async-start | bytes 524288 | tf_op jit(solution)/shard_map/all_to_all | solution.py:90
  56.7 10.9 %copy-start.8 = (f32[16]{0:T(128)S(1)}, f32[16]{0:T(128)}, u32[]{:S(2)}) copy-start(f32[16]{0:T(128)} %param.18) | copy-start | bytes 196
  69.6 9.6 %copy-start.6 = (f32[1024]{0:T(1024)S(1)}, f32[1024]{0:T(1024)}, u32[]{:S(2)}) copy-start(f32[1024]{0:T(1024)} %param.19) | copy-start | bytes 12292

commit v12 on v10

--- a/solution.py
+++ b/solution.py
@@ -48,7 +48,7 @@
     cconv = activated[:, head_cols + states :]
     xdt = (xconv.astype(jnp.float32) * step_size[:, :, None]).astype(jnp.bfloat16)
     lower = jnp.arange(GROUP)[:, None] >= jnp.arange(GROUP)[None, :]
-    previous = edge_docs[taps - 2] - 1
+    previous = jnp.max(edge_docs) - 1
     cum = jnp.cumsum(log_decay, axis=0)
     gram = jnp.dot(cconv, bconv.T, preferred_element_type=jnp.float32)
     mask = ((doc_ids[:, None] == doc_ids[None, :]) & lower)[None]

time: 80.1 us -> 80.1 us (level)
  no operation moved by 1% of the time
where the time goes in v12:
time: 80.1 us; the launch traced here: 79.5 us
  waiting for transfers between devices  35.4 us (44%)
  starting transfers between devices  13.7 us (17%)
  blocking collectives  9.38 us (12%)
  other arithmetic  7.3 us (9%)
  local copies, waits for them, and re-layouts  6.11 us (8%)
  matrix products  5.87 us (7%)
  between operations  1.67 us (2%)
    all_to_all x1, waiting for transfers between devices, body(): lax.all_to_all(payload, 'seg', 0, 0, tiled=True)  14.6 us
    ppermute x2, waiting for transfers between devices, shifted(): return lax.ppermute(block, axis, route)  12.2 us
    all_to_all x1, blocking collectives, body(): lax.all_to_all(jnp.broadcast_to(own[None], (ways, own.shape[0])), 'head',...  9.38 us
    all_to_all x1, waiting for transfers between devices, body(): lax.all_to_all(entering.astype(jnp.bfloat16), 'seg', 0, 0, tiled=True)  8.61 us
    all_to_all x1, starting transfers between devices, body(): lax.all_to_all(payload, 'seg', 0, 0, tiled=True)  4.97 us
    ppermute x2, starting transfers between devices, shifted(): return lax.ppermute(block, axis, route)  4.51 us
    all_to_all x1, starting transfers between devices, body(): lax.all_to_all(entering.astype(jnp.bfloat16), 'seg', 0, 0, tiled=True)  4.26 us
    unnamed x22, local copies, waits for them, and re-layouts  2.49 us
  transfers between devices with their start and end apart: 4, of which 4 were waited for; matrix products, arithmetic and copies ran while one was open for 7% of the time, Pallas kernels for 0%

profile of v12, /device:TPU:32, one launch (start us, length us, event | category | flops | bytes accessed | tf_op | source)
XLA Modules:
  0.0 79.5 jit_solution(6420426999799418979)
XLA Ops:
  0.0 0.0 copy-start
  0.0 0.0 copy-start.4
  0.0 0.0 copy-start.2
  0.0 0.0 copy-start.5
  0.0 0.0 copy-start.7
  0.0 0.7 broadcast_add_fusion
  0.8 0.1 slice_bitcast_fusion.4
  0.9 0.1 copy.50
  1.0 1.1 %constant_dynamic-update-slice_fusion.3 = bf16[256,1280]{1,0:T(8,128)(2,1)S(1)} fusion(bf16[256,1024]{1,0:T(8,128)(2,1)} %param.10), kind=kLoop, calls=%fused_computation.60 | loop fusion | bytes 1048576
  2.0 0.0 copy-done.2
  2.1 1.9 %collective-permute-start = (bf16[3,1281]{1,0:T(4,128)(2,1)S(1)}, bf16[3,1281]{1,0:T(4,128)(2,1)S(1)}, u32[]{:S(2)}, u32[]{:S(2)}) collective-permute-start(bf16[3,1281]{1,0:T(4,128)(2,1)S(1)} %pad_maximum_fusion.2), channel_id=1, source_target_pairs={{0,4},{4,8},{8,12},{12,16},{16,20},{20,24},{24,28},{28,32},{32,36}... | collective-permute-start | bytes 23066 | tf_op jit(solution)/shard_map/ppermute | solution.py:18
  4.0 0.0 copy-done
  4.1 0.6 reduce-window.6
  4.6 0.2 slice_reduce_fusion
  4.9 0.0 copy-done.5
  4.9 0.0 copy-done.7
  4.9 0.1 slice_reduce_fusion.7
  4.9 0.1 fusion.38
  5.0 0.2 slice_reduce_fusion.3
  5.2 0.0 copy-done.4
  5.2 0.7 slice.113
  5.9 7.9 %collective-permute-done = bf16[3,1281]{1,0:T(4,128)(2,1)S(1)} collective-permute-done((bf16[3,1281]{1,0:T(4,128)(2,1)S(1)}, bf16[3,1281]{1,0:T(4,128)(2,1)S(1)}, u32[]{:S(2)}, u32[]{:S(2)}) %collective-permute-start) | collective-permute-done | bytes 7718 | tf_op jit(solution)/shard_map/ppermute | solution.py:18
  13.7 0.7 convert_reduce_fusion
  15.8 0.1 pad_add_fusion
  15.8 0.8 compare_convert_fusion.3
  16.6 1.2 %multiply_convert_fusion.4 = bf16[256,1280]{1,0:T(8,128)(2,1)S(1)} fusion(bf16[256,1280]{1,0:T(8,128)(2,1)S(1)} %constant_dynamic-update-slice_fusion.2, bf16[3,1280]{1,0:T(4,128)(2,1)S(1)} %slice.126, f32[256]{0:T(256)S(1)} %get-tuple-element.22, f32[1280]{0:T(1024)S(1)} %get-tuple-element.10, f32[256]{0:T(256)S(1)} %get-tuple-element.23, ...), kind=kLoop, calls=%fused_computation.13 | loop fusion | flops 9175040 | bytes 1341952 | tf_op jit(solution)/shard_map/convert_element_type | solution.py:45
  17.8 0.0 copy-start.1
  17.9 0.1 slice_convert_fusion
  18.0 0.0 copy-start.3
  18.0 0.3 copy.51
  18.3 0.1 exponential_select_fusion
  18.4 0.3 copy-done.3
  18.7 0.3 fusion.14
  19.0 0.3 copy.80
  19.4 0.1 broadcast_in_dim.73
  19.5 1.2 %all_to_all.13 = f32[16,1,8320]{2,1,0:T(1,128)} reshape(f32[16,8320]{1,0:T(8,128)S(1)} %pad_maximum_fusion.1) | data formatting | bytes 1064960 | tf_op jit(solution)/shard_map/all_to_all | solution.py:72
  20.6 5.0 %all-to-all-start = ((f32[16,1,8320]{2,1,0:T(1,128)}), f32[16,1,8320]{2,1,0:T(1,128)S(1)}, u32[]{:S(2)}, u32[]{:S(2)}) async-start(f32[16,1,8320]{2,1,0:T(1,128)} %all_to_all.13), calls=%async_computation | async-start | bytes 1064960 | tf_op jit(solution)/shard_map/all_to_all | solution.py:72
  25.6 0.1 fusion.24
  25.7 1.3 %convert_multiply_fusion = f32[256,1024]{1,0:T(8,128)S(1)} fusion(bf16[256,1024]{1,0:T(8,128)(2,1)} %param.12), kind=kLoop, calls=%fused_computation.11 | loop fusion | flops 1310720 | bytes 1572864 | tf_op jit(solution)/shard_map/jit(silu)/mul | solution.py:60
  27.1 14.6 %all-to-all-done = f32[16,1,8320]{2,1,0:T(1,128)S(1)} async-done(((f32[16,1,8320]{2,1,0:T(1,128)}), f32[16,1,8320]{2,1,0:T(1,128)S(1)}, u32[]{:S(2)}, u32[]{:S(2)}) %all-to-all-start) | async-done | bytes 532512 | tf_op jit(solution)/shard_map/all_to_all | solution.py:72
  41.7 0.2 slice_reduce_fusion.2
  41.9 0.1 select_reduce_fusion
  42.1 0.2 slice_reduce_fusion.1
  42.2 0.1 slice.141
  42.3 0.7 fusion.17
  43.0 2.6 %collective-permute-start.1 = (f32[1,8192]{1,0:T(1,128)S(1)}, f32[1,8192]{1,0:T(1,128)S(1)}, u32[]{:S(2)}, u32[]{:S(2)}) collective-permute-start(f32[1,8192]{1,0:T(1,128)S(1)} %fusion.17), channel_id=1, source_target_pairs={{0,64},{64,128},{128,192},{192,256},{256,320},{320,384},{384,448},... | collective-permute-start | bytes 98312 | tf_op jit(solution)/shard_map/ppermute | solution.py:18
  45.6 0.1 select_reduce_fusion.1
  45.7 4.3 %collective-permute-done.1 = f32[1,8192]{1,0:T(1,128)S(1)} collective-permute-done((f32[1,8192]{1,0:T(1,128)S(1)}, f32[1,8192]{1,0:T(1,128)S(1)}, u32[]{:S(2)}, u32[]{:S(2)}) %collective-permute-start.1) | collective-permute-done | bytes 32800 | tf_op jit(solution)/shard_map/ppermute | solution.py:18
  50.0 0.8 %fusion.22 = bf16[2,8,64,128]{3,1,2,0:T(8,128)(2,1)S(1)} fusion(f32[8192]{0:T(1024)S(1)} %bitcast.75, f32[16]{0:T(128)S(1)} %select_reduce_fusion.1, f32[16,1,8192]{2,1,0:T(1,128)S(1)} %slice.141, f32[1,17,16]{1,2,0:T(8,128)S(1)} %bitcast_select_fusion), kind=kOutput, calls=%fused_computation.38 | convolution fusion | flops 25559040 | bytes 820352 | tf_op jit(solution)/shard_map/gij,gjf->gif/dot_general | solution.py:86
  50.8 0.8 copy.60
  51.6 4.3 %all-to-all-start.1 = ((bf16[16,1,64,128]{3,2,1,0:T(8,128)(2,1)}), bf16[16,1,64,128]{3,2,1,0:T(8,128)(2,1)S(1)}, u32[]{:S(2)}, u32[]{:S(2)}) async-start(bf16[16,1,64,128]{3,2,1,0:T(8,128)(2,1)} %bitcast.12), calls=%async_computation.1 | async-start | bytes 524288 | tf_op jit(solution)/shard_map/all_to_all | solution.py:89
  55.9 0.0 copy-done.1
  55.9 0.2 fusion.28
  56.1 0.0 copy-start.8
  56.1 2.3 %fusion.6 = f32[256,16,64]{0,2,1:T(8,128)} fusion(f32[256,256]{1,0:T(8,128)S(1)} %fusion.28, f32[16,256]{1,0:T(8,128)S(1)} %get-tuple-element.20, pred[256,256]{1,0:T(8,128)(4,1)S(1)} %fusion.24, f32[256,16,64]{0,2,1:T(8,128)S(1)} %bitcast.70, f32[256,16]{0,1:T(8,128)S(1)} %copy-done.3), kind=kOutput, calls=%fused_computation.7 | convolution fusion | flops 139984896 | bytes 2457600 | tf_op jit(solution)/shard_map/hts,shp->thp/dot_general | solution.py:59
  58.4 8.6 %all-to-all-done.1 = bf16[16,1,64,128]{3,2,1,0:T(8,128)(2,1)S(1)} async-done(((bf16[16,1,64,128]{3,2,1,0:T(8,128)(2,1)}), bf16[16,1,64,128]{3,2,1,0:T(8,128)(2,1)S(1)}, u32[]{:S(2)}, u32[]{:S(2)}) %all-to-all-start.1) | async-done | bytes 262176 | tf_op jit(solution)/shard_map/all_to_all | solution.py:89
  67.0 0.0 copy-done.8
  67.0 1.6 %fusion.8 = f32[256,16,64]{0,2,1:T(8,128)S(1)} fusion(f32[256,16,64]{0,2,1:T(8,128)} %fusion.6, f32[256,16,64]{0,2,1:T(8,128)S(1)} %bitcast.71, f32[16]{0:T(128)S(1)} %copy-done.8, f32[256,16]{0,1:T(8,128)S(1)} %get-tuple-element.18, bf16[16,1,64,128]{3,2,1,0:T(8,128)(2,1)S(1)} %all-to-all-done.1, bf16[256,1280]{1,0:T(8,128)(2,1)} %copy-done.1), kind=kOutput, calls=%fused_computation.10 | convolution fusion | flops 68157440 | bytes 3489856 | tf_op jit(solution)/shard_map/tn,hpn->thp/dot_general | solution.py:94
  68.6 0.3 copy.55
  68.9 0.0 copy-start.6
  68.9 0.2 multiply_reduce_fusion
  69.1 9.4 %all_to_all.20 = f32[4,1,256]{2,1,0:T(1,128)S(1)} all-to-all(f32[4,1,256]{2,1,0:T(1,128)S(1)} %broadcast_in_dim.118), channel_id=1, replica_groups=mesh['row'=8,'seg'=16,'head'=4] {'head'}, dimensions={0} | all-to-all | bytes 8192 | tf_op jit(solution)/shard_map/all_to_all | solution.py:101
  78.5 0.0 copy-done.6
  78.6 0.9 %multiply_convert_fusion.5 = bf16[256,1024]{1,0:T(8,128)(2,1)} fusion(f32[256,1024]{1,0:T(8,128)S(1)} %get-tuple-element.16, f32[1024]{0:T(1024)S(1)} %copy-done.6, f32[256]{0:T(256)S(1)} %bitcast.76), kind=kLoop, calls=%fused_computation.17 | loop fusion | flops 786432 | bytes 1577984 | tf_op jit(solution)/shard_map/convert_element_type | solution.py:106
  (16 shorter events, 0.2 us)
Async XLA Ops:
  0.0 4.0 %copy-start = (f32[256,16]{0,1:T(8,128)S(1)}, f32[256,16]{0,1:T(8,128)}, u32[]{:S(2)}) copy-start(f32[256,16]{0,1:T(8,128)} %param.14) | copy-start | bytes 49156
  0.0 5.2 %copy-start.4 = (s32[256]{0:T(256)S(1)}, s32[256]{0:T(256)}, u32[]{:S(2)}) copy-start(s32[256]{0:T(256)} %param.15) | copy-start | bytes 3076
  0.0 2.0 %copy-start.2 = (bf16[256,256]{1,0:T(8,128)(2,1)S(1)}, bf16[256,256]{1,0:T(8,128)(2,1)}, u32[]{:S(2)}) copy-start(bf16[256,256]{1,0:T(8,128)(2,1)} %param.11) | copy-start | bytes 393220
  0.0 4.8 %copy-start.5 = (f32[4,1024]{1,0:T(4,128)S(1)}, f32[4,1024]{1,0:T(4,128)}, u32[]{:S(2)}) copy-start(f32[4,1024]{1,0:T(4,128)} %param.16) | copy-start | bytes 49156
  0.0 4.8 %copy-start.7 = (f32[4,256]{1,0:T(4,128)S(1)}, f32[4,256]{1,0:T(4,128)}, u32[]{:S(2)}) copy-start(f32[4,256]{1,0:T(4,128)} %param.17) | copy-start | bytes 12292
  2.1 11.6 %collective-permute-start = (bf16[3,1281]{1,0:T(4,128)(2,1)S(1)}, bf16[3,1281]{1,0:T(4,128)(2,1)S(1)}, u32[]{:S(2)}, u32[]{:S(2)}) collective-permute-start(bf16[3,1281]{1,0:T(4,128)(2,1)S(1)} %pad_maximum_fusion.2), channel_id=1, source_target_pairs={{0,4},{4,8},{8,12},{12,16},{16,20},{20,24},{24,28},{28,32},{32,36}... | collective-permute-start | bytes 23066 | tf_op jit(solution)/shard_map/ppermute | solution.py:18
  17.8 38.0 %copy-start.1 = (bf16[256,1280]{1,0:T(8,128)(2,1)}, bf16[256,1280]{1,0:T(8,128)(2,1)S(1)}, u32[]{:S(2)}) copy-start(bf16[256,1280]{1,0:T(8,128)(2,1)S(1)} %multiply_convert_fusion.4) | copy-start | bytes 1966084
  18.0 0.8 copy-start.3
  20.6 21.1 %all-to-all-start = ((f32[16,1,8320]{2,1,0:T(1,128)}), f32[16,1,8320]{2,1,0:T(1,128)S(1)}, u32[]{:S(2)}, u32[]{:S(2)}) async-start(f32[16,1,8320]{2,1,0:T(1,128)} %all_to_all.13), calls=%async_computation | async-start | bytes 1064960 | tf_op jit(solution)/shard_map/all_to_all | solution.py:72
  43.0 7.0 %collective-permute-start.1 = (f32[1,8192]{1,0:T(1,128)S(1)}, f32[1,8192]{1,0:T(1,128)S(1)}, u32[]{:S(2)}, u32[]{:S(2)}) collective-permute-start(f32[1,8192]{1,0:T(1,128)S(1)} %fusion.17), channel_id=1, source_target_pairs={{0,64},{64,128},{128,192},{192,256},{256,320},{320,384},{384,448},... | collective-permute-start | bytes 98312 | tf_op jit(solution)/shard_map/ppermute | solution.py:18
  51.6 15.4 %all-to-all-start.1 = ((bf16[16,1,64,128]{3,2,1,0:T(8,128)(2,1)}), bf16[16,1,64,128]{3,2,1,0:T(8,128)(2,1)S(1)}, u32[]{:S(2)}, u32[]{:S(2)}) async-start(bf16[16,1,64,128]{3,2,1,0:T(8,128)(2,1)} %bitcast.12), calls=%async_computation.1 | async-start | bytes 524288 | tf_op jit(solution)/shard_map/all_to_all | solution.py:89
  56.1 11.0 %copy-start.8 = (f32[16]{0:T(128)S(1)}, f32[16]{0:T(128)}, u32[]{:S(2)}) copy-start(f32[16]{0:T(128)} %param.18) | copy-start | bytes 196
  68.9 9.6 %copy-start.6 = (f32[1024]{0:T(1024)S(1)}, f32[1024]{0:T(1024)}, u32[]{:S(2)}) copy-start(f32[1024]{0:T(1024)} %param.19) | copy-start | bytes 12292
